TPU v7x, 512 devices: a whole 4x8x8 slice. The times are simulated.
512 devices in a mesh: tm: 32 (over y, z_lo), space: 16 (over x, z_hi, core).
Axes of the slice: x: 4, y: 8, z: 8 (z_hi: 2, z_lo: 4; z = z_hi * 4 + z_lo), core: 2. Of those that a mesh axis runs over, the one named last changes fastest.
Arguments:
- prior_adjoint_iterate: float32 [32, 256, 128, 128], P('tm', 'space'), may hold values from -6 to 6
- material: int32 [256, 128, 128], P('space'), may hold values from 0 to 7
- probe_cell_index: int32 [1024], P('space'), may hold values from 0 to 4194303, as said below
- misfit: float32 [32, 1024], P('tm', 'space'), may hold values from -12 to 12
- ventilation_heat_loss: float32 [32], P('tm'), as said below
- conductance: float32 [8], replicated, may hold values from 0.03 to 0.14
- rock_heat_drain: float32 [8], replicated, as said below
Outputs:
- adjoint_new: float32 [32, 256, 128, 128], P('tm', 'space')
Inputs may be any that keep to these rules, and one draw needn't show every extreme that they name: `probe_cell_index`: sensors 64 p to 64 (p + 1) - 1 lie in the p-th block of 16 planes of the first dimension; a cell may hold several sensors. `ventilation_heat_loss`: Non-negative. `rock_heat_drain`: Positive.
All inputs are finite; a program needn't handle non-finite values.
Results may differ from a plain program's by a relative error of at most 0.00002.
Values sent between devices are 32-bit elements; how exact they have to be, the bound alone decides.
No kernel may reach another device: no remote copies, remote signals or barrier semaphores. Data moves between devices by JAX's collectives and lax.ppermute only.
A program may use at most 64 MiB of HBM per device.

v0:
```python
import jax
import jax.numpy as jnp
from jax import lax
from jax.sharding import PartitionSpec as P

FINE_STEPS = 4


def padded_2(value, sides, width):
    for axis, dim in sides:
        size, length = (lax.axis_size(axis), value.shape[dim])
        up = [(i, (i + 1) % size) for i in range(size - 1)]
        down = [(j, i) for i, j in up]
        last = lax.slice_in_dim(value, length - width, length, axis=dim)
        initial = lax.slice_in_dim(value, 0, width, axis=dim)
        before = lax.ppermute(last, axis, up)
        after = lax.ppermute(initial, axis, down)
        value = jnp.concatenate([before, value, after], axis=dim)
    return value


def shifted(value, axis, steps):
    count = lax.axis_size(axis)
    initial, last = (max(0, -steps), min(count, count - steps))
    return lax.ppermute(value, axis, [(source, source + steps) for source in range(initial, last)])


def coarsen(field):
    split = field.reshape(field.shape[0] // 2, 2, field.shape[1] // 2, 2, field.shape[2])
    return 0.25 * (split[:, 0, :, 0] + split[:, 1, :, 0] + (split[:, 0, :, 1] + split[:, 1, :, 1]))


def refine(coarse):
    return jnp.repeat(jnp.repeat(coarse, 2, axis=0), 2, axis=1)


def neighbours(padded):
    x_sides = padded[2:, 1:-1, 1:-1] + padded[:-2, 1:-1, 1:-1]
    y_sides = padded[1:-1, 2:, 1:-1] + padded[1:-1, :-2, 1:-1]
    z_sides = padded[1:-1, 1:-1, 2:] + padded[1:-1, 1:-1, :-2]
    return x_sides + y_sides + z_sides


def lookup(material, values):
    summed = jnp.zeros(material.shape, jnp.float32)
    for rock_type in range(values.shape[0]):
        summed = summed + jnp.where(material == rock_type, values[rock_type], 0.0)
    return summed


def on_device(
    prior_adjoint_iterate,
    material,
    probe_cell_index,
    misfit,
    ventilation_heat_loss,
    conductance,
    rock_heat_drain,
):
    adjoint = prior_adjoint_iterate[0]
    planes = adjoint.shape[0]
    across = adjoint.shape[1]
    depth = adjoint.shape[2]
    cond_cell = lookup(material, conductance)
    cell_heat_drain = lookup(material, rock_heat_drain)
    drain_amounts = cell_heat_drain + ventilation_heat_loss[0]
    local_cell = probe_cell_index - lax.axis_index("space") * (planes * across * depth)
    source = (
        jnp.zeros((planes * across * depth,), jnp.float32)
        .at[local_cell]
        .add(misfit[0])
        .reshape(planes, across, depth)
    )
    seeded = adjoint + source
    current = seeded
    for sweep_index in range(FINE_STEPS):
        weighted = cond_cell * current
        padded_x = padded_2(weighted, (("space", 0),), 1)
        padded = jnp.pad(padded_x, ((0, 0), (1, 1), (1, 1)))
        current = current + (neighbours(padded) - 6.0 * weighted) - drain_amounts * current
    coarse_baseline = coarsen(cell_heat_drain)
    coarse_decay_rate = jnp.exp(-FINE_STEPS * (coarse_baseline + ventilation_heat_loss[0]))
    coarse_old = coarsen(adjoint)
    correction = current - refine(coarse_decay_rate * coarse_old)
    reduced = coarsen(correction)
    is_last = lax.axis_index("tm") == lax.axis_size("tm") - 1

    def advance(turn_index, chained):
        outgoing = coarse_decay_rate * chained + reduced
        arrived = shifted(outgoing, "tm", -1)
        return jnp.where(is_last, coarse_old, arrived)

    chained = lax.fori_loop(0, lax.axis_size("tm") - 1, advance, coarse_old)
    adjoint_new = refine(coarse_decay_rate * chained) + correction
    return adjoint_new[None]


def solution(mesh):
    in_specs = (
        P("tm", "space", None, None),
        P("space", None, None),
        P("space"),
        P("tm", "space"),
        P("tm"),
        P(),
        P(),
    )
    out_specs = P("tm", "space", None, None)
    return jax.shard_map(
        on_device, mesh=mesh, in_specs=in_specs, out_specs=out_specs, check_vma=False
    )
```

profile of v0, /device:TPU:38, one launch (start us, length us, event | category | flops | bytes accessed | tf_op | source)
XLA Modules:
  0.0 489.4 jit_solution(2795607529333366399)
XLA Ops:
  3.6 8.3 %fusion.30 = (f32[16,128,128]{2,1,0:T(8,128)S(1)}, f32[16,128,128]{2,1,0:T(8,128)S(1)}, pred[16,128,128]{2,1,0:T(8,128)(4,1)S(1)}, pred[16,128,128]{2,1,0:T(8,12...) fusion(f32[16,128,128]{2,1,0:T(8,128)S(1)} %bitcast.74, ...), kind=kLoop, calls=%fused_computation.73 | loop fusion | flops 6553600 | bytes 7340064 | tf_op jit(solution)/shard_map/mul | solution.py:77
  12.0 10.8 %collective-permute-start.1 = (f32[1,128,128]{2,1,0:T(8,128)S(1)}, f32[1,128,128]{2,1,0:T(8,128)S(1)}, u32[]{:S(2)}, u32[]{:S(2)}) collective-permute-start(f32[1,128,128]{2,1,0:T(8,128)S(1)} %get-tuple-element.85), channel_id=1, source_target_pairs={{1,0},{2,1},{3,2},{4,3},{5,4},{6,5},{7,6},{8,7},{9,8},{10,9},{11,1... | collective-permute-start | bytes 196616 | tf_op jit(solution)/shard_map/ppermute | solution.py:17
  26.0 7.7 %collective-permute-done.2 = f32[1,128,128]{2,1,0:T(8,128)S(1)} collective-permute-done((f32[1,128,128]{2,1,0:T(8,128)S(1)}, f32[1,128,128]{2,1,0:T(8,128)S(1)}, u32[]{:S(2)}, u32[]{:S(2)}) %collective-permute-start.2) | collective-permute-done | bytes 65568 | tf_op jit(solution)/shard_map/ppermute | solution.py:16
  34.5 7.9 %fusion.39 = (f32[16,128,128]{2,1,0:T(8,128)S(1)}, f32[16,128,128]{2,1,0:T(8,128)}, f32[16,128,128]{2,1,0:T(8,128)S(1)}) fusion(f32[16,128,128]{2,1,0:T(8,128)S(1)} %get-tuple-element.58, f32[]{:T(128)} %bitcast.67, f32[16,128,128]{2,1,0:T(8,128)S(1)} %get-tuple-element.57, f32[18,130,130]{2,1,0:T(8,128)S(1)} %select_maximum_fusion.6, ...), kind=kLoop, calls=%fused_computation.84 | loop fusion | flops 7864320 | bytes 13762596 | tf_op jit(solution)/shard_map/mul | solution.py:77
  49.2 6.8 %collective-permute-done.4 = f32[1,128,128]{2,1,0:T(8,128)S(1)} collective-permute-done((f32[1,128,128]{2,1,0:T(8,128)}, f32[1,128,128]{2,1,0:T(8,128)S(1)}, u32[]{:S(2)}, u32[]{:S(2)}) %collective-permute-start.4) | collective-permute-done | bytes 65568 | tf_op jit(solution)/shard_map/ppermute | solution.py:16
  63.3 7.5 %collective-permute-done.6 = f32[1,128,128]{2,1,0:T(8,128)S(1)} collective-permute-done((f32[1,128,128]{2,1,0:T(8,128)S(1)}, f32[1,128,128]{2,1,0:T(8,128)S(1)}, u32[]{:S(2)}, u32[]{:S(2)}) %collective-permute-start.6) | collective-permute-done | bytes 65568 | tf_op jit(solution)/shard_map/ppermute | solution.py:16
  77.5 7.5 %collective-permute-done.8 = f32[1,128,128]{2,1,0:T(8,128)S(1)} collective-permute-done((f32[1,128,128]{2,1,0:T(8,128)S(1)}, f32[1,128,128]{2,1,0:T(8,128)S(1)}, u32[]{:S(2)}, u32[]{:S(2)}) %collective-permute-start.8) | collective-permute-done | bytes 65568 | tf_op jit(solution)/shard_map/ppermute | solution.py:16
  88.4 399.5 %while.10 = (s32[]{:T(128)}, f32[8,64,128]{2,1,0:T(8,128)S(1)}, pred[]{:T(512)}, f32[8,64,128]{2,1,0:T(8,128)S(1)}, f32[8,64,128]{2,1,0:T(8,128)S(1)}, /*index=5*/f32[8,64,128]{2,1,0:T(8,128)S(1)}, s32[]{:T(128)}) while((s32[]{:T(128)}, f32[8,64,128]{2,1,0:T(8,128)S(1)}, pred[]{:T(512)}, f32[8,64,128]{2,1,0:T(8,128)S(1)}, ...), condition=%wide.region_2.3_spmd, body=%wide.region_1.2_spmd.sunk | while | flops 196610 | bytes 2883702 | solution.py:93
  92.2 6.9 %collective-permute-done = f32[8,64,128]{2,1,0:T(8,128)S(1)} collective-permute-done((f32[8,64,128]{2,1,0:T(8,128)S(1)}, f32[8,64,128]{2,1,0:T(8,128)S(1)}, u32[]{:S(2)}, u32[]{:S(2)}) %collective-permute-start) | collective-permute-done | bytes 262176 | tf_op jit(solution)/shard_map/while/body/eval_jaxpr/ppermute | solution.py:25
  104.5 5.4 %collective-permute-done = f32[8,64,128]{2,1,0:T(8,128)S(1)} collective-permute-done((f32[8,64,128]{2,1,0:T(8,128)S(1)}, f32[8,64,128]{2,1,0:T(8,128)S(1)}, u32[]{:S(2)}, u32[]{:S(2)}) %collective-permute-start) | collective-permute-done | bytes 262176 | tf_op jit(solution)/shard_map/while/body/eval_jaxpr/ppermute | solution.py:25
  110.0 7.2 %collective-permute-start = (f32[8,64,128]{2,1,0:T(8,128)S(1)}, f32[8,64,128]{2,1,0:T(8,128)S(1)}, u32[]{:S(2)}, u32[]{:S(2)}) collective-permute-start(f32[8,64,128]{2,1,0:T(8,128)S(1)} %multiply_add_fusion.2), channel_id=1, source_target_pairs={{16,0},{32,16},{48,32},{64,48},{80,64},{96,80},{112,96},{128,112},... | collective-permute-start | bytes 786440 | tf_op jit(solution)/shard_map/while/body/eval_jaxpr/ppermute | solution.py:25
  117.2 5.5 %collective-permute-done = f32[8,64,128]{2,1,0:T(8,128)S(1)} collective-permute-done((f32[8,64,128]{2,1,0:T(8,128)S(1)}, f32[8,64,128]{2,1,0:T(8,128)S(1)}, u32[]{:S(2)}, u32[]{:S(2)}) %collective-permute-start) | collective-permute-done | bytes 262176 | tf_op jit(solution)/shard_map/while/body/eval_jaxpr/ppermute | solution.py:25
  122.8 8.3 %collective-permute-start = (f32[8,64,128]{2,1,0:T(8,128)S(1)}, f32[8,64,128]{2,1,0:T(8,128)S(1)}, u32[]{:S(2)}, u32[]{:S(2)}) collective-permute-start(f32[8,64,128]{2,1,0:T(8,128)S(1)} %multiply_add_fusion.2), channel_id=1, source_target_pairs={{16,0},{32,16},{48,32},{64,48},{80,64},{96,80},{112,96},{128,112},... | collective-permute-start | bytes 786440 | tf_op jit(solution)/shard_map/while/body/eval_jaxpr/ppermute | solution.py:25
  131.1 6.6 %collective-permute-done = f32[8,64,128]{2,1,0:T(8,128)S(1)} collective-permute-done((f32[8,64,128]{2,1,0:T(8,128)S(1)}, f32[8,64,128]{2,1,0:T(8,128)S(1)}, u32[]{:S(2)}, u32[]{:S(2)}) %collective-permute-start) | collective-permute-done | bytes 262176 | tf_op jit(solution)/shard_map/while/body/eval_jaxpr/ppermute | solution.py:25
  137.8 8.3 %collective-permute-start = (f32[8,64,128]{2,1,0:T(8,128)S(1)}, f32[8,64,128]{2,1,0:T(8,128)S(1)}, u32[]{:S(2)}, u32[]{:S(2)}) collective-permute-start(f32[8,64,128]{2,1,0:T(8,128)S(1)} %multiply_add_fusion.2), channel_id=1, source_target_pairs={{16,0},{32,16},{48,32},{64,48},{80,64},{96,80},{112,96},{128,112},... | collective-permute-start | bytes 786440 | tf_op jit(solution)/shard_map/while/body/eval_jaxpr/ppermute | solution.py:25
  146.1 5.8 %collective-permute-done = f32[8,64,128]{2,1,0:T(8,128)S(1)} collective-permute-done((f32[8,64,128]{2,1,0:T(8,128)S(1)}, f32[8,64,128]{2,1,0:T(8,128)S(1)}, u32[]{:S(2)}, u32[]{:S(2)}) %collective-permute-start) | collective-permute-done | bytes 262176 | tf_op jit(solution)/shard_map/while/body/eval_jaxpr/ppermute | solution.py:25
  152.1 8.3 %collective-permute-start = (f32[8,64,128]{2,1,0:T(8,128)S(1)}, f32[8,64,128]{2,1,0:T(8,128)S(1)}, u32[]{:S(2)}, u32[]{:S(2)}) collective-permute-start(f32[8,64,128]{2,1,0:T(8,128)S(1)} %multiply_add_fusion.2), channel_id=1, source_target_pairs={{16,0},{32,16},{48,32},{64,48},{80,64},{96,80},{112,96},{128,112},... | collective-permute-start | bytes 786440 | tf_op jit(solution)/shard_map/while/body/eval_jaxpr/ppermute | solution.py:25
  165.4 8.3 %collective-permute-start = (f32[8,64,128]{2,1,0:T(8,128)S(1)}, f32[8,64,128]{2,1,0:T(8,128)S(1)}, u32[]{:S(2)}, u32[]{:S(2)}) collective-permute-start(f32[8,64,128]{2,1,0:T(8,128)S(1)} %multiply_add_fusion.2), channel_id=1, source_target_pairs={{16,0},{32,16},{48,32},{64,48},{80,64},{96,80},{112,96},{128,112},... | collective-permute-start | bytes 786440 | tf_op jit(solution)/shard_map/while/body/eval_jaxpr/ppermute | solution.py:25
  178.0 8.3 %collective-permute-start = (f32[8,64,128]{2,1,0:T(8,128)S(1)}, f32[8,64,128]{2,1,0:T(8,128)S(1)}, u32[]{:S(2)}, u32[]{:S(2)}) collective-permute-start(f32[8,64,128]{2,1,0:T(8,128)S(1)} %multiply_add_fusion.2), channel_id=1, source_target_pairs={{16,0},{32,16},{48,32},{64,48},{80,64},{96,80},{112,96},{128,112},... | collective-permute-start | bytes 786440 | tf_op jit(solution)/shard_map/while/body/eval_jaxpr/ppermute | solution.py:25
  190.2 8.3 %collective-permute-start = (f32[8,64,128]{2,1,0:T(8,128)S(1)}, f32[8,64,128]{2,1,0:T(8,128)S(1)}, u32[]{:S(2)}, u32[]{:S(2)}) collective-permute-start(f32[8,64,128]{2,1,0:T(8,128)S(1)} %multiply_add_fusion.2), channel_id=1, source_target_pairs={{16,0},{32,16},{48,32},{64,48},{80,64},{96,80},{112,96},{128,112},... | collective-permute-start | bytes 786440 | tf_op jit(solution)/shard_map/while/body/eval_jaxpr/ppermute | solution.py:25
  202.5 8.3 %collective-permute-start = (f32[8,64,128]{2,1,0:T(8,128)S(1)}, f32[8,64,128]{2,1,0:T(8,128)S(1)}, u32[]{:S(2)}, u32[]{:S(2)}) collective-permute-start(f32[8,64,128]{2,1,0:T(8,128)S(1)} %multiply_add_fusion.2), channel_id=1, source_target_pairs={{16,0},{32,16},{48,32},{64,48},{80,64},{96,80},{112,96},{128,112},... | collective-permute-start | bytes 786440 | tf_op jit(solution)/shard_map/while/body/eval_jaxpr/ppermute | solution.py:25
  214.8 8.3 %collective-permute-start = (f32[8,64,128]{2,1,0:T(8,128)S(1)}, f32[8,64,128]{2,1,0:T(8,128)S(1)}, u32[]{:S(2)}, u32[]{:S(2)}) collective-permute-start(f32[8,64,128]{2,1,0:T(8,128)S(1)} %multiply_add_fusion.2), channel_id=1, source_target_pairs={{16,0},{32,16},{48,32},{64,48},{80,64},{96,80},{112,96},{128,112},... | collective-permute-start | bytes 786440 | tf_op jit(solution)/shard_map/while/body/eval_jaxpr/ppermute | solution.py:25
  227.0 8.3 %collective-permute-start = (f32[8,64,128]{2,1,0:T(8,128)S(1)}, f32[8,64,128]{2,1,0:T(8,128)S(1)}, u32[]{:S(2)}, u32[]{:S(2)}) collective-permute-start(f32[8,64,128]{2,1,0:T(8,128)S(1)} %multiply_add_fusion.2), channel_id=1, source_target_pairs={{16,0},{32,16},{48,32},{64,48},{80,64},{96,80},{112,96},{128,112},... | collective-permute-start | bytes 786440 | tf_op jit(solution)/shard_map/while/body/eval_jaxpr/ppermute | solution.py:25
  239.3 8.3 %collective-permute-start = (f32[8,64,128]{2,1,0:T(8,128)S(1)}, f32[8,64,128]{2,1,0:T(8,128)S(1)}, u32[]{:S(2)}, u32[]{:S(2)}) collective-permute-start(f32[8,64,128]{2,1,0:T(8,128)S(1)} %multiply_add_fusion.2), channel_id=1, source_target_pairs={{16,0},{32,16},{48,32},{64,48},{80,64},{96,80},{112,96},{128,112},... | collective-permute-start | bytes 786440 | tf_op jit(solution)/shard_map/while/body/eval_jaxpr/ppermute | solution.py:25
  252.4 8.3 %collective-permute-start = (f32[8,64,128]{2,1,0:T(8,128)S(1)}, f32[8,64,128]{2,1,0:T(8,128)S(1)}, u32[]{:S(2)}, u32[]{:S(2)}) collective-permute-start(f32[8,64,128]{2,1,0:T(8,128)S(1)} %multiply_add_fusion.2), channel_id=1, source_target_pairs={{16,0},{32,16},{48,32},{64,48},{80,64},{96,80},{112,96},{128,112},... | collective-permute-start | bytes 786440 | tf_op jit(solution)/shard_map/while/body/eval_jaxpr/ppermute | solution.py:25
  260.7 5.9 %collective-permute-done = f32[8,64,128]{2,1,0:T(8,128)S(1)} collective-permute-done((f32[8,64,128]{2,1,0:T(8,128)S(1)}, f32[8,64,128]{2,1,0:T(8,128)S(1)}, u32[]{:S(2)}, u32[]{:S(2)}) %collective-permute-start) | collective-permute-done | bytes 262176 | tf_op jit(solution)/shard_map/while/body/eval_jaxpr/ppermute | solution.py:25
  266.7 8.3 %collective-permute-start = (f32[8,64,128]{2,1,0:T(8,128)S(1)}, f32[8,64,128]{2,1,0:T(8,128)S(1)}, u32[]{:S(2)}, u32[]{:S(2)}) collective-permute-start(f32[8,64,128]{2,1,0:T(8,128)S(1)} %multiply_add_fusion.2), channel_id=1, source_target_pairs={{16,0},{32,16},{48,32},{64,48},{80,64},{96,80},{112,96},{128,112},... | collective-permute-start | bytes 786440 | tf_op jit(solution)/shard_map/while/body/eval_jaxpr/ppermute | solution.py:25
  275.0 6.3 %collective-permute-done = f32[8,64,128]{2,1,0:T(8,128)S(1)} collective-permute-done((f32[8,64,128]{2,1,0:T(8,128)S(1)}, f32[8,64,128]{2,1,0:T(8,128)S(1)}, u32[]{:S(2)}, u32[]{:S(2)}) %collective-permute-start) | collective-permute-done | bytes 262176 | tf_op jit(solution)/shard_map/while/body/eval_jaxpr/ppermute | solution.py:25
  281.5 8.3 %collective-permute-start = (f32[8,64,128]{2,1,0:T(8,128)S(1)}, f32[8,64,128]{2,1,0:T(8,128)S(1)}, u32[]{:S(2)}, u32[]{:S(2)}) collective-permute-start(f32[8,64,128]{2,1,0:T(8,128)S(1)} %multiply_add_fusion.2), channel_id=1, source_target_pairs={{16,0},{32,16},{48,32},{64,48},{80,64},{96,80},{112,96},{128,112},... | collective-permute-start | bytes 786440 | tf_op jit(solution)/shard_map/while/body/eval_jaxpr/ppermute | solution.py:25
  289.8 5.5 %collective-permute-done = f32[8,64,128]{2,1,0:T(8,128)S(1)} collective-permute-done((f32[8,64,128]{2,1,0:T(8,128)S(1)}, f32[8,64,128]{2,1,0:T(8,128)S(1)}, u32[]{:S(2)}, u32[]{:S(2)}) %collective-permute-start) | collective-permute-done | bytes 262176 | tf_op jit(solution)/shard_map/while/body/eval_jaxpr/ppermute | solution.py:25
  295.3 8.3 %collective-permute-start = (f32[8,64,128]{2,1,0:T(8,128)S(1)}, f32[8,64,128]{2,1,0:T(8,128)S(1)}, u32[]{:S(2)}, u32[]{:S(2)}) collective-permute-start(f32[8,64,128]{2,1,0:T(8,128)S(1)} %multiply_add_fusion.2), channel_id=1, source_target_pairs={{16,0},{32,16},{48,32},{64,48},{80,64},{96,80},{112,96},{128,112},... | collective-permute-start | bytes 786440 | tf_op jit(solution)/shard_map/while/body/eval_jaxpr/ppermute | solution.py:25
  308.4 8.3 %collective-permute-start = (f32[8,64,128]{2,1,0:T(8,128)S(1)}, f32[8,64,128]{2,1,0:T(8,128)S(1)}, u32[]{:S(2)}, u32[]{:S(2)}) collective-permute-start(f32[8,64,128]{2,1,0:T(8,128)S(1)} %multiply_add_fusion.2), channel_id=1, source_target_pairs={{16,0},{32,16},{48,32},{64,48},{80,64},{96,80},{112,96},{128,112},... | collective-permute-start | bytes 786440 | tf_op jit(solution)/shard_map/while/body/eval_jaxpr/ppermute | solution.py:25
  320.6 8.3 %collective-permute-start = (f32[8,64,128]{2,1,0:T(8,128)S(1)}, f32[8,64,128]{2,1,0:T(8,128)S(1)}, u32[]{:S(2)}, u32[]{:S(2)}) collective-permute-start(f32[8,64,128]{2,1,0:T(8,128)S(1)} %multiply_add_fusion.2), channel_id=1, source_target_pairs={{16,0},{32,16},{48,32},{64,48},{80,64},{96,80},{112,96},{128,112},... | collective-permute-start | bytes 786440 | tf_op jit(solution)/shard_map/while/body/eval_jaxpr/ppermute | solution.py:25
  332.9 8.3 %collective-permute-start = (f32[8,64,128]{2,1,0:T(8,128)S(1)}, f32[8,64,128]{2,1,0:T(8,128)S(1)}, u32[]{:S(2)}, u32[]{:S(2)}) collective-permute-start(f32[8,64,128]{2,1,0:T(8,128)S(1)} %multiply_add_fusion.2), channel_id=1, source_target_pairs={{16,0},{32,16},{48,32},{64,48},{80,64},{96,80},{112,96},{128,112},... | collective-permute-start | bytes 786440 | tf_op jit(solution)/shard_map/while/body/eval_jaxpr/ppermute | solution.py:25
  345.2 8.3 %collective-permute-start = (f32[8,64,128]{2,1,0:T(8,128)S(1)}, f32[8,64,128]{2,1,0:T(8,128)S(1)}, u32[]{:S(2)}, u32[]{:S(2)}) collective-permute-start(f32[8,64,128]{2,1,0:T(8,128)S(1)} %multiply_add_fusion.2), channel_id=1, source_target_pairs={{16,0},{32,16},{48,32},{64,48},{80,64},{96,80},{112,96},{128,112},... | collective-permute-start | bytes 786440 | tf_op jit(solution)/shard_map/while/body/eval_jaxpr/ppermute | solution.py:25
  357.5 8.3 %collective-permute-start = (f32[8,64,128]{2,1,0:T(8,128)S(1)}, f32[8,64,128]{2,1,0:T(8,128)S(1)}, u32[]{:S(2)}, u32[]{:S(2)}) collective-permute-start(f32[8,64,128]{2,1,0:T(8,128)S(1)} %multiply_add_fusion.2), channel_id=1, source_target_pairs={{16,0},{32,16},{48,32},{64,48},{80,64},{96,80},{112,96},{128,112},... | collective-permute-start | bytes 786440 | tf_op jit(solution)/shard_map/while/body/eval_jaxpr/ppermute | solution.py:25
  369.7 8.3 %collective-permute-start = (f32[8,64,128]{2,1,0:T(8,128)S(1)}, f32[8,64,128]{2,1,0:T(8,128)S(1)}, u32[]{:S(2)}, u32[]{:S(2)}) collective-permute-start(f32[8,64,128]{2,1,0:T(8,128)S(1)} %multiply_add_fusion.2), channel_id=1, source_target_pairs={{16,0},{32,16},{48,32},{64,48},{80,64},{96,80},{112,96},{128,112},... | collective-permute-start | bytes 786440 | tf_op jit(solution)/shard_map/while/body/eval_jaxpr/ppermute | solution.py:25
  382.3 8.3 %collective-permute-start = (f32[8,64,128]{2,1,0:T(8,128)S(1)}, f32[8,64,128]{2,1,0:T(8,128)S(1)}, u32[]{:S(2)}, u32[]{:S(2)}) collective-permute-start(f32[8,64,128]{2,1,0:T(8,128)S(1)} %multiply_add_fusion.2), channel_id=1, source_target_pairs={{16,0},{32,16},{48,32},{64,48},{80,64},{96,80},{112,96},{128,112},... | collective-permute-start | bytes 786440 | tf_op jit(solution)/shard_map/while/body/eval_jaxpr/ppermute | solution.py:25
  390.6 5.3 %collective-permute-done = f32[8,64,128]{2,1,0:T(8,128)S(1)} collective-permute-done((f32[8,64,128]{2,1,0:T(8,128)S(1)}, f32[8,64,128]{2,1,0:T(8,128)S(1)}, u32[]{:S(2)}, u32[]{:S(2)}) %collective-permute-start) | collective-permute-done | bytes 262176 | tf_op jit(solution)/shard_map/while/body/eval_jaxpr/ppermute | solution.py:25
  396.1 8.3 %collective-permute-start = (f32[8,64,128]{2,1,0:T(8,128)S(1)}, f32[8,64,128]{2,1,0:T(8,128)S(1)}, u32[]{:S(2)}, u32[]{:S(2)}) collective-permute-start(f32[8,64,128]{2,1,0:T(8,128)S(1)} %multiply_add_fusion.2), channel_id=1, source_target_pairs={{16,0},{32,16},{48,32},{64,48},{80,64},{96,80},{112,96},{128,112},... | collective-permute-start | bytes 786440 | tf_op jit(solution)/shard_map/while/body/eval_jaxpr/ppermute | solution.py:25
  404.4 6.5 %collective-permute-done = f32[8,64,128]{2,1,0:T(8,128)S(1)} collective-permute-done((f32[8,64,128]{2,1,0:T(8,128)S(1)}, f32[8,64,128]{2,1,0:T(8,128)S(1)}, u32[]{:S(2)}, u32[]{:S(2)}) %collective-permute-start) | collective-permute-done | bytes 262176 | tf_op jit(solution)/shard_map/while/body/eval_jaxpr/ppermute | solution.py:25
  411.0 8.3 %collective-permute-start = (f32[8,64,128]{2,1,0:T(8,128)S(1)}, f32[8,64,128]{2,1,0:T(8,128)S(1)}, u32[]{:S(2)}, u32[]{:S(2)}) collective-permute-start(f32[8,64,128]{2,1,0:T(8,128)S(1)} %multiply_add_fusion.2), channel_id=1, source_target_pairs={{16,0},{32,16},{48,32},{64,48},{80,64},{96,80},{112,96},{128,112},... | collective-permute-start | bytes 786440 | tf_op jit(solution)/shard_map/while/body/eval_jaxpr/ppermute | solution.py:25
  419.3 5.8 %collective-permute-done = f32[8,64,128]{2,1,0:T(8,128)S(1)} collective-permute-done((f32[8,64,128]{2,1,0:T(8,128)S(1)}, f32[8,64,128]{2,1,0:T(8,128)S(1)}, u32[]{:S(2)}, u32[]{:S(2)}) %collective-permute-start) | collective-permute-done | bytes 262176 | tf_op jit(solution)/shard_map/while/body/eval_jaxpr/ppermute | solution.py:25
  425.2 8.3 %collective-permute-start = (f32[8,64,128]{2,1,0:T(8,128)S(1)}, f32[8,64,128]{2,1,0:T(8,128)S(1)}, u32[]{:S(2)}, u32[]{:S(2)}) collective-permute-start(f32[8,64,128]{2,1,0:T(8,128)S(1)} %multiply_add_fusion.2), channel_id=1, source_target_pairs={{16,0},{32,16},{48,32},{64,48},{80,64},{96,80},{112,96},{128,112},... | collective-permute-start | bytes 786440 | tf_op jit(solution)/shard_map/while/body/eval_jaxpr/ppermute | solution.py:25
  438.6 8.3 %collective-permute-start = (f32[8,64,128]{2,1,0:T(8,128)S(1)}, f32[8,64,128]{2,1,0:T(8,128)S(1)}, u32[]{:S(2)}, u32[]{:S(2)}) collective-permute-start(f32[8,64,128]{2,1,0:T(8,128)S(1)} %multiply_add_fusion.2), channel_id=1, source_target_pairs={{16,0},{32,16},{48,32},{64,48},{80,64},{96,80},{112,96},{128,112},... | collective-permute-start | bytes 786440 | tf_op jit(solution)/shard_map/while/body/eval_jaxpr/ppermute | solution.py:25
  451.1 8.3 %collective-permute-start = (f32[8,64,128]{2,1,0:T(8,128)S(1)}, f32[8,64,128]{2,1,0:T(8,128)S(1)}, u32[]{:S(2)}, u32[]{:S(2)}) collective-permute-start(f32[8,64,128]{2,1,0:T(8,128)S(1)} %multiply_add_fusion.2), channel_id=1, source_target_pairs={{16,0},{32,16},{48,32},{64,48},{80,64},{96,80},{112,96},{128,112},... | collective-permute-start | bytes 786440 | tf_op jit(solution)/shard_map/while/body/eval_jaxpr/ppermute | solution.py:25
  463.4 8.3 %collective-permute-start = (f32[8,64,128]{2,1,0:T(8,128)S(1)}, f32[8,64,128]{2,1,0:T(8,128)S(1)}, u32[]{:S(2)}, u32[]{:S(2)}) collective-permute-start(f32[8,64,128]{2,1,0:T(8,128)S(1)} %multiply_add_fusion.2), channel_id=1, source_target_pairs={{16,0},{32,16},{48,32},{64,48},{80,64},{96,80},{112,96},{128,112},... | collective-permute-start | bytes 786440 | tf_op jit(solution)/shard_map/while/body/eval_jaxpr/ppermute | solution.py:25
  475.7 8.3 %collective-permute-start = (f32[8,64,128]{2,1,0:T(8,128)S(1)}, f32[8,64,128]{2,1,0:T(8,128)S(1)}, u32[]{:S(2)}, u32[]{:S(2)}) collective-permute-start(f32[8,64,128]{2,1,0:T(8,128)S(1)} %multiply_add_fusion.2), channel_id=1, source_target_pairs={{16,0},{32,16},{48,32},{64,48},{80,64},{96,80},{112,96},{128,112},... | collective-permute-start | bytes 786440 | tf_op jit(solution)/shard_map/while/body/eval_jaxpr/ppermute | solution.py:25
  (138 shorter events, 125.7 us)
Async XLA Ops:
  3.6 8.3 %copy-start.1 = (f32[262144]{0:T(1024)}, f32[262144]{0:T(1024)S(1)}, u32[]{:S(2)}) copy-start(f32[262144]{0:T(1024)S(1)} %scatter_custom_fusion) | copy-start | bytes 3145732
  3.6 21.7 %copy-start.7 = (f32[8]{0:T(128)S(1)}, f32[8]{0:T(128)}, u32[]{:S(2)}) copy-start(f32[8]{0:T(128)} %param.15) | copy-start | bytes 100
  11.9 22.5 %copy-start = (f32[1,16,128,128]{3,2,1,0:T(8,128)S(1)}, f32[1,16,128,128]{3,2,1,0:T(8,128)}, u32[]{:S(2)}) copy-start(f32[1,16,128,128]{3,2,1,0:T(8,128)} %param.9) | copy-start | bytes 3145732
  12.0 22.5 %copy-start.2 = (f32[262144]{0:T(1024)S(1)}, f32[262144]{0:T(1024)}, u32[]{:S(2)}) copy-start(f32[262144]{0:T(1024)} %copy-done.1) | copy-start | bytes 3145732
  12.0 14.0 %collective-permute-start.1 = (f32[1,128,128]{2,1,0:T(8,128)S(1)}, f32[1,128,128]{2,1,0:T(8,128)S(1)}, u32[]{:S(2)}, u32[]{:S(2)}) collective-permute-start(f32[1,128,128]{2,1,0:T(8,128)S(1)} %get-tuple-element.85), channel_id=1, source_target_pairs={{1,0},{2,1},{3,2},{4,3},{5,4},{6,5},{7,6},{8,7},{9,8},{10,9},{11,1... | collective-permute-start | bytes 196616 | tf_op jit(solution)/shard_map/ppermute | solution.py:17
  22.7 11.0 %collective-permute-start.2 = (f32[1,128,128]{2,1,0:T(8,128)S(1)}, f32[1,128,128]{2,1,0:T(8,128)S(1)}, u32[]{:S(2)}, u32[]{:S(2)}) collective-permute-start(f32[1,128,128]{2,1,0:T(8,128)S(1)} %get-tuple-element.84), channel_id=1, source_target_pairs={{0,1},{1,2},{2,3},{3,4},{4,5},{5,6},{6,7},{7,8},{8,9},{9,10},{10,1... | collective-permute-start | bytes 196616 | tf_op jit(solution)/shard_map/ppermute | solution.py:16
  43.1 6.1 %collective-permute-start.3 = (f32[1,128,128]{2,1,0:T(8,128)}, f32[1,128,128]{2,1,0:T(8,128)S(1)}, u32[]{:S(2)}, u32[]{:S(2)}) collective-permute-start(f32[1,128,128]{2,1,0:T(8,128)} %get-tuple-element.79), channel_id=1, source_target_pairs={{1,0},{2,1},{3,2},{4,3},{5,4},{6,5},{7,6},{8,7},{9,8},{10,9},{11,1... | collective-permute-start | bytes 196616 | tf_op jit(solution)/shard_map/ppermute | solution.py:17
  45.0 11.0 %collective-permute-start.4 = (f32[1,128,128]{2,1,0:T(8,128)}, f32[1,128,128]{2,1,0:T(8,128)S(1)}, u32[]{:S(2)}, u32[]{:S(2)}) collective-permute-start(f32[1,128,128]{2,1,0:T(8,128)} %get-tuple-element.78), channel_id=1, source_target_pairs={{0,1},{1,2},{2,3},{3,4},{4,5},{5,6},{6,7},{7,8},{8,9},{9,10},{10,1... | collective-permute-start | bytes 196616 | tf_op jit(solution)/shard_map/ppermute | solution.py:16
  49.2 7.5 %copy-start.3 = (f32[16,128,128]{2,1,0:T(8,128)S(1)}, f32[16,128,128]{2,1,0:T(8,128)}, u32[]{:S(2)}) copy-start(f32[16,128,128]{2,1,0:T(8,128)} %get-tuple-element.55) | copy-start | bytes 3145732
  58.0 5.2 %collective-permute-start.5 = (f32[1,128,128]{2,1,0:T(8,128)S(1)}, f32[1,128,128]{2,1,0:T(8,128)S(1)}, u32[]{:S(2)}, u32[]{:S(2)}) collective-permute-start(f32[1,128,128]{2,1,0:T(8,128)S(1)} %get-tuple-element.77), channel_id=1, source_target_pairs={{1,0},{2,1},{3,2},{4,3},{5,4},{6,5},{7,6},{8,7},{9,8},{10,9},{11,1... | collective-permute-start | bytes 196616 | tf_op jit(solution)/shard_map/ppermute | solution.py:17
  59.9 10.8 %collective-permute-start.6 = (f32[1,128,128]{2,1,0:T(8,128)S(1)}, f32[1,128,128]{2,1,0:T(8,128)S(1)}, u32[]{:S(2)}, u32[]{:S(2)}) collective-permute-start(f32[1,128,128]{2,1,0:T(8,128)S(1)} %get-tuple-element.76), channel_id=1, source_target_pairs={{0,1},{1,2},{2,3},{3,4},{4,5},{5,6},{6,7},{7,8},{8,9},{9,10},{10,1... | collective-permute-start | bytes 196616 | tf_op jit(solution)/shard_map/ppermute | solution.py:16
  71.4 5.8 %copy-start.4 = (f32[8,1,64,1,128]{4,3,2,1,0:T(1,128)S(1)}, f32[8,1,64,1,128]{4,3,2,1,0:T(1,128)}, u32[]{:S(2)}) copy-start(f32[8,1,64,1,128]{4,3,2,1,0:T(1,128)} %get-tuple-element.87) | copy-start | bytes 786436
  71.4 5.8 %copy-start.5 = (f32[8,1,64,1,128]{4,3,2,1,0:T(1,128)S(1)}, f32[8,1,64,1,128]{4,3,2,1,0:T(1,128)}, u32[]{:S(2)}) copy-start(f32[8,1,64,1,128]{4,3,2,1,0:T(1,128)} %get-tuple-element.88) | copy-start | bytes 786436
  71.5 5.8 %copy-start.6 = (f32[8,1,64,1,128]{4,3,2,1,0:T(1,128)S(1)}, f32[8,1,64,1,128]{4,3,2,1,0:T(1,128)}, u32[]{:S(2)}) copy-start(f32[8,1,64,1,128]{4,3,2,1,0:T(1,128)} %get-tuple-element.89) | copy-start | bytes 786436
  72.7 4.8 collective-permute-start.7
  74.7 10.4 %collective-permute-start.8 = (f32[1,128,128]{2,1,0:T(8,128)S(1)}, f32[1,128,128]{2,1,0:T(8,128)S(1)}, u32[]{:S(2)}, u32[]{:S(2)}) collective-permute-start(f32[1,128,128]{2,1,0:T(8,128)S(1)} %get-tuple-element.74), channel_id=1, source_target_pairs={{0,1},{1,2},{2,3},{3,4},{4,5},{5,6},{6,7},{7,8},{8,9},{9,10},{10,1... | collective-permute-start | bytes 196616 | tf_op jit(solution)/shard_map/ppermute | solution.py:16
  88.4 10.7 %collective-permute-start = (f32[8,64,128]{2,1,0:T(8,128)S(1)}, f32[8,64,128]{2,1,0:T(8,128)S(1)}, u32[]{:S(2)}, u32[]{:S(2)}) collective-permute-start(f32[8,64,128]{2,1,0:T(8,128)S(1)} %multiply_add_fusion.2), channel_id=1, source_target_pairs={{16,0},{32,16},{48,32},{64,48},{80,64},{96,80},{112,96},{128,112},... | collective-permute-start | bytes 786440 | tf_op jit(solution)/shard_map/while/body/eval_jaxpr/ppermute | solution.py:25
  99.3 10.7 %collective-permute-start = (f32[8,64,128]{2,1,0:T(8,128)S(1)}, f32[8,64,128]{2,1,0:T(8,128)S(1)}, u32[]{:S(2)}, u32[]{:S(2)}) collective-permute-start(f32[8,64,128]{2,1,0:T(8,128)S(1)} %multiply_add_fusion.2), channel_id=1, source_target_pairs={{16,0},{32,16},{48,32},{64,48},{80,64},{96,80},{112,96},{128,112},... | collective-permute-start | bytes 786440 | tf_op jit(solution)/shard_map/while/body/eval_jaxpr/ppermute | solution.py:25
  110.0 12.7 %collective-permute-start = (f32[8,64,128]{2,1,0:T(8,128)S(1)}, f32[8,64,128]{2,1,0:T(8,128)S(1)}, u32[]{:S(2)}, u32[]{:S(2)}) collective-permute-start(f32[8,64,128]{2,1,0:T(8,128)S(1)} %multiply_add_fusion.2), channel_id=1, source_target_pairs={{16,0},{32,16},{48,32},{64,48},{80,64},{96,80},{112,96},{128,112},... | collective-permute-start | bytes 786440 | tf_op jit(solution)/shard_map/while/body/eval_jaxpr/ppermute | solution.py:25
  122.8 14.9 %collective-permute-start = (f32[8,64,128]{2,1,0:T(8,128)S(1)}, f32[8,64,128]{2,1,0:T(8,128)S(1)}, u32[]{:S(2)}, u32[]{:S(2)}) collective-permute-start(f32[8,64,128]{2,1,0:T(8,128)S(1)} %multiply_add_fusion.2), channel_id=1, source_target_pairs={{16,0},{32,16},{48,32},{64,48},{80,64},{96,80},{112,96},{128,112},... | collective-permute-start | bytes 786440 | tf_op jit(solution)/shard_map/while/body/eval_jaxpr/ppermute | solution.py:25
  137.8 14.1 %collective-permute-start = (f32[8,64,128]{2,1,0:T(8,128)S(1)}, f32[8,64,128]{2,1,0:T(8,128)S(1)}, u32[]{:S(2)}, u32[]{:S(2)}) collective-permute-start(f32[8,64,128]{2,1,0:T(8,128)S(1)} %multiply_add_fusion.2), channel_id=1, source_target_pairs={{16,0},{32,16},{48,32},{64,48},{80,64},{96,80},{112,96},{128,112},... | collective-permute-start | bytes 786440 | tf_op jit(solution)/shard_map/while/body/eval_jaxpr/ppermute | solution.py:25
  152.1 13.3 %collective-permute-start = (f32[8,64,128]{2,1,0:T(8,128)S(1)}, f32[8,64,128]{2,1,0:T(8,128)S(1)}, u32[]{:S(2)}, u32[]{:S(2)}) collective-permute-start(f32[8,64,128]{2,1,0:T(8,128)S(1)} %multiply_add_fusion.2), channel_id=1, source_target_pairs={{16,0},{32,16},{48,32},{64,48},{80,64},{96,80},{112,96},{128,112},... | collective-permute-start | bytes 786440 | tf_op jit(solution)/shard_map/while/body/eval_jaxpr/ppermute | solution.py:25
  165.4 12.4 %collective-permute-start = (f32[8,64,128]{2,1,0:T(8,128)S(1)}, f32[8,64,128]{2,1,0:T(8,128)S(1)}, u32[]{:S(2)}, u32[]{:S(2)}) collective-permute-start(f32[8,64,128]{2,1,0:T(8,128)S(1)} %multiply_add_fusion.2), channel_id=1, source_target_pairs={{16,0},{32,16},{48,32},{64,48},{80,64},{96,80},{112,96},{128,112},... | collective-permute-start | bytes 786440 | tf_op jit(solution)/shard_map/while/body/eval_jaxpr/ppermute | solution.py:25
  178.0 12.2 %collective-permute-start = (f32[8,64,128]{2,1,0:T(8,128)S(1)}, f32[8,64,128]{2,1,0:T(8,128)S(1)}, u32[]{:S(2)}, u32[]{:S(2)}) collective-permute-start(f32[8,64,128]{2,1,0:T(8,128)S(1)} %multiply_add_fusion.2), channel_id=1, source_target_pairs={{16,0},{32,16},{48,32},{64,48},{80,64},{96,80},{112,96},{128,112},... | collective-permute-start | bytes 786440 | tf_op jit(solution)/shard_map/while/body/eval_jaxpr/ppermute | solution.py:25
  190.2 12.2 %collective-permute-start = (f32[8,64,128]{2,1,0:T(8,128)S(1)}, f32[8,64,128]{2,1,0:T(8,128)S(1)}, u32[]{:S(2)}, u32[]{:S(2)}) collective-permute-start(f32[8,64,128]{2,1,0:T(8,128)S(1)} %multiply_add_fusion.2), channel_id=1, source_target_pairs={{16,0},{32,16},{48,32},{64,48},{80,64},{96,80},{112,96},{128,112},... | collective-permute-start | bytes 786440 | tf_op jit(solution)/shard_map/while/body/eval_jaxpr/ppermute | solution.py:25
  202.5 12.2 %collective-permute-start = (f32[8,64,128]{2,1,0:T(8,128)S(1)}, f32[8,64,128]{2,1,0:T(8,128)S(1)}, u32[]{:S(2)}, u32[]{:S(2)}) collective-permute-start(f32[8,64,128]{2,1,0:T(8,128)S(1)} %multiply_add_fusion.2), channel_id=1, source_target_pairs={{16,0},{32,16},{48,32},{64,48},{80,64},{96,80},{112,96},{128,112},... | collective-permute-start | bytes 786440 | tf_op jit(solution)/shard_map/while/body/eval_jaxpr/ppermute | solution.py:25
  214.8 12.2 %collective-permute-start = (f32[8,64,128]{2,1,0:T(8,128)S(1)}, f32[8,64,128]{2,1,0:T(8,128)S(1)}, u32[]{:S(2)}, u32[]{:S(2)}) collective-permute-start(f32[8,64,128]{2,1,0:T(8,128)S(1)} %multiply_add_fusion.2), channel_id=1, source_target_pairs={{16,0},{32,16},{48,32},{64,48},{80,64},{96,80},{112,96},{128,112},... | collective-permute-start | bytes 786440 | tf_op jit(solution)/shard_map/while/body/eval_jaxpr/ppermute | solution.py:25
  227.0 12.2 %collective-permute-start = (f32[8,64,128]{2,1,0:T(8,128)S(1)}, f32[8,64,128]{2,1,0:T(8,128)S(1)}, u32[]{:S(2)}, u32[]{:S(2)}) collective-permute-start(f32[8,64,128]{2,1,0:T(8,128)S(1)} %multiply_add_fusion.2), channel_id=1, source_target_pairs={{16,0},{32,16},{48,32},{64,48},{80,64},{96,80},{112,96},{128,112},... | collective-permute-start | bytes 786440 | tf_op jit(solution)/shard_map/while/body/eval_jaxpr/ppermute | solution.py:25
  239.3 13.0 %collective-permute-start = (f32[8,64,128]{2,1,0:T(8,128)S(1)}, f32[8,64,128]{2,1,0:T(8,128)S(1)}, u32[]{:S(2)}, u32[]{:S(2)}) collective-permute-start(f32[8,64,128]{2,1,0:T(8,128)S(1)} %multiply_add_fusion.2), channel_id=1, source_target_pairs={{16,0},{32,16},{48,32},{64,48},{80,64},{96,80},{112,96},{128,112},... | collective-permute-start | bytes 786440 | tf_op jit(solution)/shard_map/while/body/eval_jaxpr/ppermute | solution.py:25
  252.4 14.2 %collective-permute-start = (f32[8,64,128]{2,1,0:T(8,128)S(1)}, f32[8,64,128]{2,1,0:T(8,128)S(1)}, u32[]{:S(2)}, u32[]{:S(2)}) collective-permute-start(f32[8,64,128]{2,1,0:T(8,128)S(1)} %multiply_add_fusion.2), channel_id=1, source_target_pairs={{16,0},{32,16},{48,32},{64,48},{80,64},{96,80},{112,96},{128,112},... | collective-permute-start | bytes 786440 | tf_op jit(solution)/shard_map/while/body/eval_jaxpr/ppermute | solution.py:25
  266.7 14.6 %collective-permute-start = (f32[8,64,128]{2,1,0:T(8,128)S(1)}, f32[8,64,128]{2,1,0:T(8,128)S(1)}, u32[]{:S(2)}, u32[]{:S(2)}) collective-permute-start(f32[8,64,128]{2,1,0:T(8,128)S(1)} %multiply_add_fusion.2), channel_id=1, source_target_pairs={{16,0},{32,16},{48,32},{64,48},{80,64},{96,80},{112,96},{128,112},... | collective-permute-start | bytes 786440 | tf_op jit(solution)/shard_map/while/body/eval_jaxpr/ppermute | solution.py:25
  281.5 13.8 %collective-permute-start = (f32[8,64,128]{2,1,0:T(8,128)S(1)}, f32[8,64,128]{2,1,0:T(8,128)S(1)}, u32[]{:S(2)}, u32[]{:S(2)}) collective-permute-start(f32[8,64,128]{2,1,0:T(8,128)S(1)} %multiply_add_fusion.2), channel_id=1, source_target_pairs={{16,0},{32,16},{48,32},{64,48},{80,64},{96,80},{112,96},{128,112},... | collective-permute-start | bytes 786440 | tf_op jit(solution)/shard_map/while/body/eval_jaxpr/ppermute | solution.py:25
  295.3 12.9 %collective-permute-start = (f32[8,64,128]{2,1,0:T(8,128)S(1)}, f32[8,64,128]{2,1,0:T(8,128)S(1)}, u32[]{:S(2)}, u32[]{:S(2)}) collective-permute-start(f32[8,64,128]{2,1,0:T(8,128)S(1)} %multiply_add_fusion.2), channel_id=1, source_target_pairs={{16,0},{32,16},{48,32},{64,48},{80,64},{96,80},{112,96},{128,112},... | collective-permute-start | bytes 786440 | tf_op jit(solution)/shard_map/while/body/eval_jaxpr/ppermute | solution.py:25
  308.4 12.2 %collective-permute-start = (f32[8,64,128]{2,1,0:T(8,128)S(1)}, f32[8,64,128]{2,1,0:T(8,128)S(1)}, u32[]{:S(2)}, u32[]{:S(2)}) collective-permute-start(f32[8,64,128]{2,1,0:T(8,128)S(1)} %multiply_add_fusion.2), channel_id=1, source_target_pairs={{16,0},{32,16},{48,32},{64,48},{80,64},{96,80},{112,96},{128,112},... | collective-permute-start | bytes 786440 | tf_op jit(solution)/shard_map/while/body/eval_jaxpr/ppermute | solution.py:25
  320.6 12.2 %collective-permute-start = (f32[8,64,128]{2,1,0:T(8,128)S(1)}, f32[8,64,128]{2,1,0:T(8,128)S(1)}, u32[]{:S(2)}, u32[]{:S(2)}) collective-permute-start(f32[8,64,128]{2,1,0:T(8,128)S(1)} %multiply_add_fusion.2), channel_id=1, source_target_pairs={{16,0},{32,16},{48,32},{64,48},{80,64},{96,80},{112,96},{128,112},... | collective-permute-start | bytes 786440 | tf_op jit(solution)/shard_map/while/body/eval_jaxpr/ppermute | solution.py:25
  332.9 12.2 %collective-permute-start = (f32[8,64,128]{2,1,0:T(8,128)S(1)}, f32[8,64,128]{2,1,0:T(8,128)S(1)}, u32[]{:S(2)}, u32[]{:S(2)}) collective-permute-start(f32[8,64,128]{2,1,0:T(8,128)S(1)} %multiply_add_fusion.2), channel_id=1, source_target_pairs={{16,0},{32,16},{48,32},{64,48},{80,64},{96,80},{112,96},{128,112},... | collective-permute-start | bytes 786440 | tf_op jit(solution)/shard_map/while/body/eval_jaxpr/ppermute | solution.py:25
  345.2 12.2 %collective-permute-start = (f32[8,64,128]{2,1,0:T(8,128)S(1)}, f32[8,64,128]{2,1,0:T(8,128)S(1)}, u32[]{:S(2)}, u32[]{:S(2)}) collective-permute-start(f32[8,64,128]{2,1,0:T(8,128)S(1)} %multiply_add_fusion.2), channel_id=1, source_target_pairs={{16,0},{32,16},{48,32},{64,48},{80,64},{96,80},{112,96},{128,112},... | collective-permute-start | bytes 786440 | tf_op jit(solution)/shard_map/while/body/eval_jaxpr/ppermute | solution.py:25
  357.5 12.2 %collective-permute-start = (f32[8,64,128]{2,1,0:T(8,128)S(1)}, f32[8,64,128]{2,1,0:T(8,128)S(1)}, u32[]{:S(2)}, u32[]{:S(2)}) collective-permute-start(f32[8,64,128]{2,1,0:T(8,128)S(1)} %multiply_add_fusion.2), channel_id=1, source_target_pairs={{16,0},{32,16},{48,32},{64,48},{80,64},{96,80},{112,96},{128,112},... | collective-permute-start | bytes 786440 | tf_op jit(solution)/shard_map/while/body/eval_jaxpr/ppermute | solution.py:25
  369.7 12.5 %collective-permute-start = (f32[8,64,128]{2,1,0:T(8,128)S(1)}, f32[8,64,128]{2,1,0:T(8,128)S(1)}, u32[]{:S(2)}, u32[]{:S(2)}) collective-permute-start(f32[8,64,128]{2,1,0:T(8,128)S(1)} %multiply_add_fusion.2), channel_id=1, source_target_pairs={{16,0},{32,16},{48,32},{64,48},{80,64},{96,80},{112,96},{128,112},... | collective-permute-start | bytes 786440 | tf_op jit(solution)/shard_map/while/body/eval_jaxpr/ppermute | solution.py:25
  382.3 13.7 %collective-permute-start = (f32[8,64,128]{2,1,0:T(8,128)S(1)}, f32[8,64,128]{2,1,0:T(8,128)S(1)}, u32[]{:S(2)}, u32[]{:S(2)}) collective-permute-start(f32[8,64,128]{2,1,0:T(8,128)S(1)} %multiply_add_fusion.2), channel_id=1, source_target_pairs={{16,0},{32,16},{48,32},{64,48},{80,64},{96,80},{112,96},{128,112},... | collective-permute-start | bytes 786440 | tf_op jit(solution)/shard_map/while/body/eval_jaxpr/ppermute | solution.py:25
  396.1 14.8 %collective-permute-start = (f32[8,64,128]{2,1,0:T(8,128)S(1)}, f32[8,64,128]{2,1,0:T(8,128)S(1)}, u32[]{:S(2)}, u32[]{:S(2)}) collective-permute-start(f32[8,64,128]{2,1,0:T(8,128)S(1)} %multiply_add_fusion.2), channel_id=1, source_target_pairs={{16,0},{32,16},{48,32},{64,48},{80,64},{96,80},{112,96},{128,112},... | collective-permute-start | bytes 786440 | tf_op jit(solution)/shard_map/while/body/eval_jaxpr/ppermute | solution.py:25
  411.0 14.1 %collective-permute-start = (f32[8,64,128]{2,1,0:T(8,128)S(1)}, f32[8,64,128]{2,1,0:T(8,128)S(1)}, u32[]{:S(2)}, u32[]{:S(2)}) collective-permute-start(f32[8,64,128]{2,1,0:T(8,128)S(1)} %multiply_add_fusion.2), channel_id=1, source_target_pairs={{16,0},{32,16},{48,32},{64,48},{80,64},{96,80},{112,96},{128,112},... | collective-permute-start | bytes 786440 | tf_op jit(solution)/shard_map/while/body/eval_jaxpr/ppermute | solution.py:25
  425.2 13.3 %collective-permute-start = (f32[8,64,128]{2,1,0:T(8,128)S(1)}, f32[8,64,128]{2,1,0:T(8,128)S(1)}, u32[]{:S(2)}, u32[]{:S(2)}) collective-permute-start(f32[8,64,128]{2,1,0:T(8,128)S(1)} %multiply_add_fusion.2), channel_id=1, source_target_pairs={{16,0},{32,16},{48,32},{64,48},{80,64},{96,80},{112,96},{128,112},... | collective-permute-start | bytes 786440 | tf_op jit(solution)/shard_map/while/body/eval_jaxpr/ppermute | solution.py:25
  438.6 12.4 %collective-permute-start = (f32[8,64,128]{2,1,0:T(8,128)S(1)}, f32[8,64,128]{2,1,0:T(8,128)S(1)}, u32[]{:S(2)}, u32[]{:S(2)}) collective-permute-start(f32[8,64,128]{2,1,0:T(8,128)S(1)} %multiply_add_fusion.2), channel_id=1, source_target_pairs={{16,0},{32,16},{48,32},{64,48},{80,64},{96,80},{112,96},{128,112},... | collective-permute-start | bytes 786440 | tf_op jit(solution)/shard_map/while/body/eval_jaxpr/ppermute | solution.py:25
  451.1 12.2 %collective-permute-start = (f32[8,64,128]{2,1,0:T(8,128)S(1)}, f32[8,64,128]{2,1,0:T(8,128)S(1)}, u32[]{:S(2)}, u32[]{:S(2)}) collective-permute-start(f32[8,64,128]{2,1,0:T(8,128)S(1)} %multiply_add_fusion.2), channel_id=1, source_target_pairs={{16,0},{32,16},{48,32},{64,48},{80,64},{96,80},{112,96},{128,112},... | collective-permute-start | bytes 786440 | tf_op jit(solution)/shard_map/while/body/eval_jaxpr/ppermute | solution.py:25
  463.4 12.2 %collective-permute-start = (f32[8,64,128]{2,1,0:T(8,128)S(1)}, f32[8,64,128]{2,1,0:T(8,128)S(1)}, u32[]{:S(2)}, u32[]{:S(2)}) collective-permute-start(f32[8,64,128]{2,1,0:T(8,128)S(1)} %multiply_add_fusion.2), channel_id=1, source_target_pairs={{16,0},{32,16},{48,32},{64,48},{80,64},{96,80},{112,96},{128,112},... | collective-permute-start | bytes 786440 | tf_op jit(solution)/shard_map/while/body/eval_jaxpr/ppermute | solution.py:25
  475.7 12.2 %collective-permute-start = (f32[8,64,128]{2,1,0:T(8,128)S(1)}, f32[8,64,128]{2,1,0:T(8,128)S(1)}, u32[]{:S(2)}, u32[]{:S(2)}) collective-permute-start(f32[8,64,128]{2,1,0:T(8,128)S(1)} %multiply_add_fusion.2), channel_id=1, source_target_pairs={{16,0},{32,16},{48,32},{64,48},{80,64},{96,80},{112,96},{128,112},... | collective-permute-start | bytes 786440 | tf_op jit(solution)/shard_map/while/body/eval_jaxpr/ppermute | solution.py:25
where the time goes:
time: 491 us; the launch traced here: 489 us
  starting transfers between devices  274 us (56%)
  waiting for transfers between devices  177 us (36%)
  other arithmetic  28.4 us (6%)
  local copies, waits for them, and re-layouts  7.42 us (2%)
    ppermute x31, starting transfers between devices, shifted(): lax.ppermute(value, axis, [(source, source + steps) for source in range(i...  249 us
    ppermute x31, waiting for transfers between devices, shifted(): lax.ppermute(value, axis, [(source, source + steps) for source in range(i...  148 us
    ppermute x4, waiting for transfers between devices, padded_2(): before = lax.ppermute(last, axis, up)  29.5 us
    mul x4, other arithmetic, on_device(): weighted = cond_cell * current  18.7 us
    ppermute x4, starting transfers between devices, padded_2(): after = lax.ppermute(initial, axis, down)  16.5 us
  transfers between devices with their start and end apart: 39, of which 35 were waited for; matrix products, arithmetic and copies ran while one was open for 1% of the time, Pallas kernels for 0%

commit v1 on v0

--- a/solution.py
+++ b/solution.py
@@ -83,15 +83,27 @@
     coarse_old = coarsen(adjoint)
     correction = current - refine(coarse_decay_rate * coarse_old)
     reduced = coarsen(correction)
-    is_last = lax.axis_index("tm") == lax.axis_size("tm") - 1
-
-    def advance(turn_index, chained):
-        outgoing = coarse_decay_rate * chained + reduced
-        arrived = shifted(outgoing, "tm", -1)
-        return jnp.where(is_last, coarse_old, arrived)
-
-    chained = lax.fori_loop(0, lax.axis_size("tm") - 1, advance, coarse_old)
-    adjoint_new = refine(coarse_decay_rate * chained) + correction
+    tm_size = lax.axis_size("tm")
+    is_last = lax.axis_index("tm") == tm_size - 1
+    per_cell = jnp.exp(-FINE_STEPS * coarse_baseline)
+    gain = jnp.exp(-FINE_STEPS * ventilation_heat_loss[0])
+    top = coarse_decay_rate * coarse_old + reduced
+    total = jnp.where(is_last, top, reduced)
+    shape = total.shape
+    rows = total.size // shape[-1]
+    power = per_cell
+    distance = 1
+    while distance < tm_size:
+        packed = jnp.concatenate(
+            [total.reshape(rows, shape[-1]), jnp.broadcast_to(gain, (8, shape[-1]))], axis=0
+        )
+        arrived = shifted(packed, "tm", -distance)
+        total = total + (power * gain) * arrived[:rows].reshape(shape)
+        gain = gain * arrived[rows, 0]
+        power = power * power
+        distance *= 2
+    decayed = jnp.where(is_last, coarse_decay_rate * coarse_old, total - reduced)
+    adjoint_new = refine(decayed) + correction
     return adjoint_new[None]
 
 

time: 491 us -> 169 us (0.34)
  the two profiles are of different devices: /device:TPU:38 before, /device:TPU:210 now
where the time goes in v1:
time: 169 us; the launch traced here: 168 us
  waiting for transfers between devices  89.4 us (53%)
  starting transfers between devices  34.4 us (20%)
  other arithmetic  30.5 us (18%)
  local copies, waits for them, and re-layouts  10.2 us (6%)
  between operations  3.78 us (2%)
    ppermute x5, waiting for transfers between devices, shifted(): lax.ppermute(value, axis, [(source, source + steps) for source in range(i...  60.9 us
    ppermute x4, waiting for transfers between devices, padded_2(): before = lax.ppermute(last, axis, up)  28.4 us
    mul x4, other arithmetic, on_device(): weighted = cond_cell * current  19.3 us
    ppermute x4, starting transfers between devices, padded_2(): after = lax.ppermute(initial, axis, down)  14.8 us
    ppermute x5, starting transfers between devices, shifted(): lax.ppermute(value, axis, [(source, source + steps) for source in range(i...  10.7 us
    ppermute x4, starting transfers between devices, padded_2(): before = lax.ppermute(last, axis, up)  8.83 us
  transfers between devices with their start and end apart: 13, of which 9 were waited for; matrix products, arithmetic and copies ran while one was open for 2% of the time, Pallas kernels for 0%

profile of v1, /device:TPU:210, one launch (start us, length us, event | category | flops | bytes accessed | tf_op | source)
XLA Modules:
  0.0 168.2 jit_solution(10461465959306044971)
XLA Ops:
  0.0 1.6 fusion.63
  1.6 0.7 compare_select_fusion
  2.3 2.0 %scatter_custom_fusion = f32[262144]{0:T(1024)} fusion(s32[64]{0:T(128)S(1)} %compare_select_fusion, f32[64]{0:T(128)} %bitcast.127, f32[]{:T(128)} %constant.5.clone.1), kind=kCustom, calls=%fused_computation.61 | custom fusion | flops 64 | bytes 1049088 | tf_op jit(solution)/shard_map/scatter-add | solution.py:71
  4.3 10.0 %fusion.30 = (f32[16,128,128]{2,1,0:T(8,128)S(1)}, f32[16,128,128]{2,1,0:T(8,128)S(1)}, pred[16,128,128]{2,1,0:T(8,128)(4,1)S(1)}, pred[16,128,128]{2,1,0:T(8,12...) fusion(f32[16,128,128]{2,1,0:T(8,128)} %bitcast.104, ...), kind=kLoop, calls=%fused_computation.71 | loop fusion | flops 6553600 | bytes 7340064 | tf_op jit(solution)/shard_map/mul | solution.py:77
  14.3 0.7 fusion.56
  15.0 7.6 %collective-permute-start = (f32[1,128,128]{2,1,0:T(8,128)}, f32[1,128,128]{2,1,0:T(8,128)S(1)}, u32[]{:S(2)}, u32[]{:S(2)}) collective-permute-start(f32[1,128,128]{2,1,0:T(8,128)} %get-tuple-element.35), channel_id=1, source_target_pairs={{1,0},{2,1},{3,2},{4,3},{5,4},{6,5},{7,6},{8,7},{9,8},{10,9},{11,1... | collective-permute-start | bytes 196616 | tf_op jit(solution)/shard_map/ppermute | solution.py:17
  22.6 1.9 %collective-permute-start.1 = (f32[1,128,128]{2,1,0:T(8,128)}, f32[1,128,128]{2,1,0:T(8,128)S(1)}, u32[]{:S(2)}, u32[]{:S(2)}) collective-permute-start(f32[1,128,128]{2,1,0:T(8,128)} %get-tuple-element.34), channel_id=1, source_target_pairs={{0,1},{1,2},{2,3},{3,4},{4,5},{5,6},{6,7},{7,8},{8,9},{9,10},{10,1... | collective-permute-start | bytes 196616 | tf_op jit(solution)/shard_map/ppermute | solution.py:16
  25.2 2.0 %fusion.57 = (f32[8,1,64,1,128]{4,3,2,1,0:T(1,128)}, f32[8,1,64,1,128]{4,3,2,1,0:T(1,128)}, f32[8,1,64,1,128]{4,3,2,1,0:T(1,128)}, f32[8,1,64,1,128]{4,3,2,1,0:T(1,128)}) fusion(f32[8,2,64,2,128]{4,3,2,1,0:T(2,128)S(1)} %bitcast.102), kind=kLoop, calls=%fused_computation.115 | loop fusion | bytes 2097152 | tf_op jit(solution)/shard_map/slice | solution.py:30
  27.2 0.7 fusion.62
  27.9 5.3 %collective-permute-done.1 = f32[1,128,128]{2,1,0:T(8,128)S(1)} collective-permute-done((f32[1,128,128]{2,1,0:T(8,128)}, f32[1,128,128]{2,1,0:T(8,128)S(1)}, u32[]{:S(2)}, u32[]{:S(2)}) %collective-permute-start.1) | collective-permute-done | bytes 65568 | tf_op jit(solution)/shard_map/ppermute | solution.py:16
  33.2 0.7 select_maximum_fusion.6
  34.0 6.9 %fusion.50 = (f32[16,128,128]{2,1,0:T(8,128)S(1)}, f32[16,128,128]{2,1,0:T(8,128)S(1)}, f32[16,128,128]{2,1,0:T(8,128)S(1)}) fusion(f32[16,128,128]{2,1,0:T(8,128)S(1)} %get-tuple-element.15, f32[]{:T(128)} %bitcast.96, f32[16,128,128]{2,1,0:T(8,128)S(1)} %get-tuple-element.14, f32[18,130,130]{2,1,0:T(8,128)S(1)} %select_maximum_fusion.6, ...), kind=kLoop, calls=%fused_computation.109 | loop fusion | flops 7864320 | bytes 13762596 | tf_op jit(solution)/shard_map/mul | solution.py:77
  40.9 3.4 %collective-permute-start.2 = (f32[1,128,128]{2,1,0:T(8,128)S(1)}, f32[1,128,128]{2,1,0:T(8,128)S(1)}, u32[]{:S(2)}, u32[]{:S(2)}) collective-permute-start(f32[1,128,128]{2,1,0:T(8,128)S(1)} %get-tuple-element.29), channel_id=1, source_target_pairs={{1,0},{2,1},{3,2},{4,3},{5,4},{6,5},{7,6},{8,7},{9,8},{10,9},{11,1... | collective-permute-start | bytes 196616 | tf_op jit(solution)/shard_map/ppermute | solution.py:17
  44.2 1.9 %collective-permute-start.3 = (f32[1,128,128]{2,1,0:T(8,128)S(1)}, f32[1,128,128]{2,1,0:T(8,128)S(1)}, u32[]{:S(2)}, u32[]{:S(2)}) collective-permute-start(f32[1,128,128]{2,1,0:T(8,128)S(1)} %get-tuple-element.28), channel_id=1, source_target_pairs={{0,1},{1,2},{2,3},{3,4},{4,5},{5,6},{6,7},{7,8},{8,9},{9,10},{10,1... | collective-permute-start | bytes 196616 | tf_op jit(solution)/shard_map/ppermute | solution.py:16
  46.2 0.7 fusion.55
  46.9 7.7 %collective-permute-done.3 = f32[1,128,128]{2,1,0:T(8,128)S(1)} collective-permute-done((f32[1,128,128]{2,1,0:T(8,128)S(1)}, f32[1,128,128]{2,1,0:T(8,128)S(1)}, u32[]{:S(2)}, u32[]{:S(2)}) %collective-permute-start.3) | collective-permute-done | bytes 65568 | tf_op jit(solution)/shard_map/ppermute | solution.py:16
  54.6 0.7 select_maximum_fusion.4
  55.3 1.2 fusion.48
  56.6 1.9 %collective-permute-start.4 = (f32[1,128,128]{2,1,0:T(8,128)S(1)}, f32[1,128,128]{2,1,0:T(8,128)S(1)}, u32[]{:S(2)}, u32[]{:S(2)}) collective-permute-start(f32[1,128,128]{2,1,0:T(8,128)S(1)} %get-tuple-element.27), channel_id=1, source_target_pairs={{1,0},{2,1},{3,2},{4,3},{5,4},{6,5},{7,6},{8,7},{9,8},{10,9},{11,1... | collective-permute-start | bytes 196616 | tf_op jit(solution)/shard_map/ppermute | solution.py:17
  58.5 2.4 %collective-permute-start.5 = (f32[1,128,128]{2,1,0:T(8,128)S(1)}, f32[1,128,128]{2,1,0:T(8,128)S(1)}, u32[]{:S(2)}, u32[]{:S(2)}) collective-permute-start(f32[1,128,128]{2,1,0:T(8,128)S(1)} %get-tuple-element.26), channel_id=1, source_target_pairs={{0,1},{1,2},{2,3},{3,4},{4,5},{5,6},{6,7},{7,8},{8,9},{9,10},{10,1... | collective-permute-start | bytes 196616 | tf_op jit(solution)/shard_map/ppermute | solution.py:16
  61.0 7.9 %collective-permute-done.5 = f32[1,128,128]{2,1,0:T(8,128)S(1)} collective-permute-done((f32[1,128,128]{2,1,0:T(8,128)S(1)}, f32[1,128,128]{2,1,0:T(8,128)S(1)}, u32[]{:S(2)}, u32[]{:S(2)}) %collective-permute-start.5) | collective-permute-done | bytes 65568 | tf_op jit(solution)/shard_map/ppermute | solution.py:16
  68.9 0.7 select_maximum_fusion.2
  69.7 1.3 fusion.46
  71.0 1.9 %collective-permute-start.6 = (f32[1,128,128]{2,1,0:T(8,128)S(1)}, f32[1,128,128]{2,1,0:T(8,128)S(1)}, u32[]{:S(2)}, u32[]{:S(2)}) collective-permute-start(f32[1,128,128]{2,1,0:T(8,128)S(1)} %get-tuple-element.25), channel_id=1, source_target_pairs={{1,0},{2,1},{3,2},{4,3},{5,4},{6,5},{7,6},{8,7},{9,8},{10,9},{11,1... | collective-permute-start | bytes 196616 | tf_op jit(solution)/shard_map/ppermute | solution.py:17
  72.9 2.6 %collective-permute-start.7 = (f32[1,128,128]{2,1,0:T(8,128)S(1)}, f32[1,128,128]{2,1,0:T(8,128)S(1)}, u32[]{:S(2)}, u32[]{:S(2)}) collective-permute-start(f32[1,128,128]{2,1,0:T(8,128)S(1)} %get-tuple-element.24), channel_id=1, source_target_pairs={{0,1},{1,2},{2,3},{3,4},{4,5},{5,6},{6,7},{7,8},{8,9},{9,10},{10,1... | collective-permute-start | bytes 196616 | tf_op jit(solution)/shard_map/ppermute | solution.py:16
  75.7 7.6 %collective-permute-done.7 = f32[1,128,128]{2,1,0:T(8,128)S(1)} collective-permute-done((f32[1,128,128]{2,1,0:T(8,128)S(1)}, f32[1,128,128]{2,1,0:T(8,128)S(1)}, u32[]{:S(2)}, u32[]{:S(2)}) %collective-permute-start.7) | collective-permute-done | bytes 65568 | tf_op jit(solution)/shard_map/ppermute | solution.py:16
  83.3 0.7 select_maximum_fusion
  84.4 1.2 fusion.7
  85.7 0.6 fusion.39
  86.3 3.2 %collective-permute-start.8 = (f32[520,128]{1,0:T(8,128)S(1)}, f32[520,128]{1,0:T(8,128)S(1)}, u32[]{:S(2)}, u32[]{:S(2)}) collective-permute-start(f32[520,128]{1,0:T(8,128)S(1)} %concatenate.63), channel_id=1, source_target_pairs={{16,0},{32,16},{48,32},{64,48},{80,64},{96,80},{112,96},{128,112},... | collective-permute-start | bytes 798728 | tf_op jit(solution)/shard_map/ppermute | solution.py:25
  89.6 12.2 %collective-permute-done.8 = f32[520,128]{1,0:T(8,128)S(1)} collective-permute-done((f32[520,128]{1,0:T(8,128)S(1)}, f32[520,128]{1,0:T(8,128)S(1)}, u32[]{:S(2)}, u32[]{:S(2)}) %collective-permute-start.8) | collective-permute-done | bytes 266272 | tf_op jit(solution)/shard_map/ppermute | solution.py:25
  101.8 0.5 slice.329
  103.0 1.9 %collective-permute-start.9 = (f32[520,128]{1,0:T(8,128)S(1)}, f32[520,128]{1,0:T(8,128)S(1)}, u32[]{:S(2)}, u32[]{:S(2)}) collective-permute-start(f32[520,128]{1,0:T(8,128)S(1)} %concatenate.64), channel_id=1, source_target_pairs={{32,0},{48,16},{64,32},{80,48},{96,64},{112,80},{128,96},{144,112}... | collective-permute-start | bytes 798728 | tf_op jit(solution)/shard_map/ppermute | solution.py:25
  105.0 8.1 %collective-permute-done.9 = f32[520,128]{1,0:T(8,128)S(1)} collective-permute-done((f32[520,128]{1,0:T(8,128)S(1)}, f32[520,128]{1,0:T(8,128)S(1)}, u32[]{:S(2)}, u32[]{:S(2)}) %collective-permute-start.9) | collective-permute-done | bytes 266272 | tf_op jit(solution)/shard_map/ppermute | solution.py:25
  113.1 0.5 slice.331
  114.4 2.4 %collective-permute-start.10 = (f32[520,128]{1,0:T(8,128)S(1)}, f32[520,128]{1,0:T(8,128)S(1)}, u32[]{:S(2)}, u32[]{:S(2)}) collective-permute-start(f32[520,128]{1,0:T(8,128)S(1)} %concatenate.65), channel_id=1, source_target_pairs={{64,0},{80,16},{96,32},{112,48},{128,64},{144,80},{160,96},{176,11... | collective-permute-start | bytes 798728 | tf_op jit(solution)/shard_map/ppermute | solution.py:25
  116.7 12.6 %collective-permute-done.10 = f32[520,128]{1,0:T(8,128)S(1)} collective-permute-done((f32[520,128]{1,0:T(8,128)S(1)}, f32[520,128]{1,0:T(8,128)S(1)}, u32[]{:S(2)}, u32[]{:S(2)}) %collective-permute-start.10) | collective-permute-done | bytes 266272 | tf_op jit(solution)/shard_map/ppermute | solution.py:25
  129.4 0.7 copy-done.13
  130.1 0.5 slice.333
  131.3 1.0 fusion.60
  132.3 1.9 %collective-permute-start.11 = (f32[520,128]{1,0:T(8,128)S(1)}, f32[520,128]{1,0:T(8,128)S(1)}, u32[]{:S(2)}, u32[]{:S(2)}) collective-permute-start(f32[520,128]{1,0:T(8,128)S(1)} %concatenate.66), channel_id=1, source_target_pairs={{128,0},{144,16},{160,32},{176,48},{192,64},{208,80},{224,96},{240... | collective-permute-start | bytes 798728 | tf_op jit(solution)/shard_map/ppermute | solution.py:25
  134.2 17.0 %collective-permute-done.11 = f32[520,128]{1,0:T(8,128)S(1)} collective-permute-done((f32[520,128]{1,0:T(8,128)S(1)}, f32[520,128]{1,0:T(8,128)S(1)}, u32[]{:S(2)}, u32[]{:S(2)}) %collective-permute-start.11) | collective-permute-done | bytes 266272 | tf_op jit(solution)/shard_map/ppermute | solution.py:25
  151.3 0.7 copy-done.14
  152.0 0.5 slice.335
  153.1 1.0 fusion.61
  154.2 1.3 collective-permute-start.12
  155.5 10.9 %collective-permute-done.12 = f32[520,128]{1,0:T(8,128)S(1)} collective-permute-done((f32[520,128]{1,0:T(8,128)S(1)}, f32[520,128]{1,0:T(8,128)S(1)}, u32[]{:S(2)}, u32[]{:S(2)}) %collective-permute-start.12) | collective-permute-done | bytes 266272 | tf_op jit(solution)/shard_map/ppermute | solution.py:25
  167.1 1.1 add_bitcast_fusion
  (56 shorter events, 1.8 us)
Async XLA Ops:
  4.3 20.9 %copy-start = (f32[1,16,128,128]{3,2,1,0:T(8,128)S(1)}, f32[1,16,128,128]{3,2,1,0:T(8,128)}, u32[]{:S(2)}) copy-start(f32[1,16,128,128]{3,2,1,0:T(8,128)} %param.7) | copy-start | bytes 3145732
  4.3 22.8 %copy-start.15 = (f32[8]{0:T(128)S(1)}, f32[8]{0:T(128)}, u32[]{:S(2)}) copy-start(f32[8]{0:T(128)} %param.13) | copy-start | bytes 100
  15.0 13.0 %collective-permute-start = (f32[1,128,128]{2,1,0:T(8,128)}, f32[1,128,128]{2,1,0:T(8,128)S(1)}, u32[]{:S(2)}, u32[]{:S(2)}) collective-permute-start(f32[1,128,128]{2,1,0:T(8,128)} %get-tuple-element.35), channel_id=1, source_target_pairs={{1,0},{2,1},{3,2},{4,3},{5,4},{6,5},{7,6},{8,7},{9,8},{10,9},{11,1... | collective-permute-start | bytes 196616 | tf_op jit(solution)/shard_map/ppermute | solution.py:17
  22.6 10.6 %collective-permute-start.1 = (f32[1,128,128]{2,1,0:T(8,128)}, f32[1,128,128]{2,1,0:T(8,128)S(1)}, u32[]{:S(2)}, u32[]{:S(2)}) collective-permute-start(f32[1,128,128]{2,1,0:T(8,128)} %get-tuple-element.34), channel_id=1, source_target_pairs={{0,1},{1,2},{2,3},{3,4},{4,5},{5,6},{6,7},{7,8},{8,9},{9,10},{10,1... | collective-permute-start | bytes 196616 | tf_op jit(solution)/shard_map/ppermute | solution.py:16
  27.2 6.7 %copy-start.1 = (f32[262144]{0:T(1024)S(1)}, f32[262144]{0:T(1024)}, u32[]{:S(2)}) copy-start(f32[262144]{0:T(1024)} %scatter_custom_fusion) | copy-start | bytes 3145732
  27.2 6.7 %copy-start.2 = (pred[16,128,128]{2,1,0:T(8,128)(4,1)S(1)}, pred[16,128,128]{2,1,0:T(8,128)(4,1)}, u32[]{:S(2)}) copy-start(pred[16,128,128]{2,1,0:T(8,128)(4,1)} %get-tuple-element.17) | copy-start | bytes 786436
  27.2 6.8 %copy-start.3 = (pred[16,128,128]{2,1,0:T(8,128)(4,1)S(1)}, pred[16,128,128]{2,1,0:T(8,128)(4,1)}, u32[]{:S(2)}) copy-start(pred[16,128,128]{2,1,0:T(8,128)(4,1)} %get-tuple-element.18) | copy-start | bytes 786436
  27.2 6.8 %copy-start.4 = (pred[16,128,128]{2,1,0:T(8,128)(4,1)S(1)}, pred[16,128,128]{2,1,0:T(8,128)(4,1)}, u32[]{:S(2)}) copy-start(pred[16,128,128]{2,1,0:T(8,128)(4,1)} %get-tuple-element.19) | copy-start | bytes 786436
  27.2 6.8 %copy-start.5 = (pred[16,128,128]{2,1,0:T(8,128)(4,1)S(1)}, pred[16,128,128]{2,1,0:T(8,128)(4,1)}, u32[]{:S(2)}) copy-start(pred[16,128,128]{2,1,0:T(8,128)(4,1)} %get-tuple-element.20) | copy-start | bytes 786436
  27.2 6.8 %copy-start.6 = (pred[16,128,128]{2,1,0:T(8,128)(4,1)S(1)}, pred[16,128,128]{2,1,0:T(8,128)(4,1)}, u32[]{:S(2)}) copy-start(pred[16,128,128]{2,1,0:T(8,128)(4,1)} %get-tuple-element.21) | copy-start | bytes 786436
  27.2 6.8 %copy-start.7 = (pred[16,128,128]{2,1,0:T(8,128)(4,1)S(1)}, pred[16,128,128]{2,1,0:T(8,128)(4,1)}, u32[]{:S(2)}) copy-start(pred[16,128,128]{2,1,0:T(8,128)(4,1)} %get-tuple-element.22) | copy-start | bytes 786436
  27.2 6.8 %copy-start.8 = (pred[16,128,128]{2,1,0:T(8,128)(4,1)S(1)}, pred[16,128,128]{2,1,0:T(8,128)(4,1)}, u32[]{:S(2)}) copy-start(pred[16,128,128]{2,1,0:T(8,128)(4,1)} %get-tuple-element.23) | copy-start | bytes 786436
  40.9 6.1 %collective-permute-start.2 = (f32[1,128,128]{2,1,0:T(8,128)S(1)}, f32[1,128,128]{2,1,0:T(8,128)S(1)}, u32[]{:S(2)}, u32[]{:S(2)}) collective-permute-start(f32[1,128,128]{2,1,0:T(8,128)S(1)} %get-tuple-element.29), channel_id=1, source_target_pairs={{1,0},{2,1},{3,2},{4,3},{5,4},{6,5},{7,6},{8,7},{9,8},{10,9},{11,1... | collective-permute-start | bytes 196616 | tf_op jit(solution)/shard_map/ppermute | solution.py:17
  44.2 10.4 %collective-permute-start.3 = (f32[1,128,128]{2,1,0:T(8,128)S(1)}, f32[1,128,128]{2,1,0:T(8,128)S(1)}, u32[]{:S(2)}, u32[]{:S(2)}) collective-permute-start(f32[1,128,128]{2,1,0:T(8,128)S(1)} %get-tuple-element.28), channel_id=1, source_target_pairs={{0,1},{1,2},{2,3},{3,4},{4,5},{5,6},{6,7},{7,8},{8,9},{9,10},{10,1... | collective-permute-start | bytes 196616 | tf_op jit(solution)/shard_map/ppermute | solution.py:16
  56.6 4.5 %collective-permute-start.4 = (f32[1,128,128]{2,1,0:T(8,128)S(1)}, f32[1,128,128]{2,1,0:T(8,128)S(1)}, u32[]{:S(2)}, u32[]{:S(2)}) collective-permute-start(f32[1,128,128]{2,1,0:T(8,128)S(1)} %get-tuple-element.27), channel_id=1, source_target_pairs={{1,0},{2,1},{3,2},{4,3},{5,4},{6,5},{7,6},{8,7},{9,8},{10,9},{11,1... | collective-permute-start | bytes 196616 | tf_op jit(solution)/shard_map/ppermute | solution.py:17
  58.5 10.4 %collective-permute-start.5 = (f32[1,128,128]{2,1,0:T(8,128)S(1)}, f32[1,128,128]{2,1,0:T(8,128)S(1)}, u32[]{:S(2)}, u32[]{:S(2)}) collective-permute-start(f32[1,128,128]{2,1,0:T(8,128)S(1)} %get-tuple-element.26), channel_id=1, source_target_pairs={{0,1},{1,2},{2,3},{3,4},{4,5},{5,6},{6,7},{7,8},{8,9},{9,10},{10,1... | collective-permute-start | bytes 196616 | tf_op jit(solution)/shard_map/ppermute | solution.py:16
  69.6 5.9 %copy-start.9 = (f32[8,1,64,1,128]{4,3,2,1,0:T(1,128)S(1)}, f32[8,1,64,1,128]{4,3,2,1,0:T(1,128)}, u32[]{:S(2)}) copy-start(f32[8,1,64,1,128]{4,3,2,1,0:T(1,128)} %get-tuple-element.36) | copy-start | bytes 786436
  69.6 5.9 %copy-start.10 = (f32[8,1,64,1,128]{4,3,2,1,0:T(1,128)S(1)}, f32[8,1,64,1,128]{4,3,2,1,0:T(1,128)}, u32[]{:S(2)}) copy-start(f32[8,1,64,1,128]{4,3,2,1,0:T(1,128)} %get-tuple-element.37) | copy-start | bytes 786436
  69.6 5.9 %copy-start.11 = (f32[8,1,64,1,128]{4,3,2,1,0:T(1,128)S(1)}, f32[8,1,64,1,128]{4,3,2,1,0:T(1,128)}, u32[]{:S(2)}) copy-start(f32[8,1,64,1,128]{4,3,2,1,0:T(1,128)} %get-tuple-element.38) | copy-start | bytes 786436
  69.6 5.9 %copy-start.12 = (f32[8,1,64,1,128]{4,3,2,1,0:T(1,128)S(1)}, f32[8,1,64,1,128]{4,3,2,1,0:T(1,128)}, u32[]{:S(2)}) copy-start(f32[8,1,64,1,128]{4,3,2,1,0:T(1,128)} %get-tuple-element.39) | copy-start | bytes 786436
  71.0 4.7 %collective-permute-start.6 = (f32[1,128,128]{2,1,0:T(8,128)S(1)}, f32[1,128,128]{2,1,0:T(8,128)S(1)}, u32[]{:S(2)}, u32[]{:S(2)}) collective-permute-start(f32[1,128,128]{2,1,0:T(8,128)S(1)} %get-tuple-element.25), channel_id=1, source_target_pairs={{1,0},{2,1},{3,2},{4,3},{5,4},{6,5},{7,6},{8,7},{9,8},{10,9},{11,1... | collective-permute-start | bytes 196616 | tf_op jit(solution)/shard_map/ppermute | solution.py:17
  72.9 10.4 %collective-permute-start.7 = (f32[1,128,128]{2,1,0:T(8,128)S(1)}, f32[1,128,128]{2,1,0:T(8,128)S(1)}, u32[]{:S(2)}, u32[]{:S(2)}) collective-permute-start(f32[1,128,128]{2,1,0:T(8,128)S(1)} %get-tuple-element.24), channel_id=1, source_target_pairs={{0,1},{1,2},{2,3},{3,4},{4,5},{5,6},{6,7},{7,8},{8,9},{9,10},{10,1... | collective-permute-start | bytes 196616 | tf_op jit(solution)/shard_map/ppermute | solution.py:16
  86.3 15.4 %collective-permute-start.8 = (f32[520,128]{1,0:T(8,128)S(1)}, f32[520,128]{1,0:T(8,128)S(1)}, u32[]{:S(2)}, u32[]{:S(2)}) collective-permute-start(f32[520,128]{1,0:T(8,128)S(1)} %concatenate.63), channel_id=1, source_target_pairs={{16,0},{32,16},{48,32},{64,48},{80,64},{96,80},{112,96},{128,112},... | collective-permute-start | bytes 798728 | tf_op jit(solution)/shard_map/ppermute | solution.py:25
  103.0 10.1 %collective-permute-start.9 = (f32[520,128]{1,0:T(8,128)S(1)}, f32[520,128]{1,0:T(8,128)S(1)}, u32[]{:S(2)}, u32[]{:S(2)}) collective-permute-start(f32[520,128]{1,0:T(8,128)S(1)} %concatenate.64), channel_id=1, source_target_pairs={{32,0},{48,16},{64,32},{80,48},{96,64},{112,80},{128,96},{144,112}... | collective-permute-start | bytes 798728 | tf_op jit(solution)/shard_map/ppermute | solution.py:25
  114.4 15.0 %collective-permute-start.10 = (f32[520,128]{1,0:T(8,128)S(1)}, f32[520,128]{1,0:T(8,128)S(1)}, u32[]{:S(2)}, u32[]{:S(2)}) collective-permute-start(f32[520,128]{1,0:T(8,128)S(1)} %concatenate.65), channel_id=1, source_target_pairs={{64,0},{80,16},{96,32},{112,48},{128,64},{144,80},{160,96},{176,11... | collective-permute-start | bytes 798728 | tf_op jit(solution)/shard_map/ppermute | solution.py:25
  129.4 0.7 copy-start.13
  132.3 19.0 %collective-permute-start.11 = (f32[520,128]{1,0:T(8,128)S(1)}, f32[520,128]{1,0:T(8,128)S(1)}, u32[]{:S(2)}, u32[]{:S(2)}) collective-permute-start(f32[520,128]{1,0:T(8,128)S(1)} %concatenate.66), channel_id=1, source_target_pairs={{128,0},{144,16},{160,32},{176,48},{192,64},{208,80},{224,96},{240... | collective-permute-start | bytes 798728 | tf_op jit(solution)/shard_map/ppermute | solution.py:25
  151.3 0.7 copy-start.14
  154.2 12.2 %collective-permute-start.12 = (f32[520,128]{1,0:T(8,128)S(1)}, f32[520,128]{1,0:T(8,128)S(1)}, u32[]{:S(2)}, u32[]{:S(2)}) collective-permute-start(f32[520,128]{1,0:T(8,128)S(1)} %concatenate.67), channel_id=1, source_target_pairs={{256,0},{272,16},{288,32},{304,48},{320,64},{336,80},{352,96},{368... | collective-permute-start | bytes 798728 | tf_op jit(solution)/shard_map/ppermute | solution.py:25

commit v2 on v1

--- a/solution.py
+++ b/solution.py
@@ -42,10 +42,11 @@
 
 
 def lookup(material, values):
-    summed = jnp.zeros(material.shape, jnp.float32)
-    for rock_type in range(values.shape[0]):
-        summed = summed + jnp.where(material == rock_type, values[rock_type], 0.0)
-    return summed
+    bits = [(material & (1 << b)) != 0 for b in range(3)]
+    level = [values[k] for k in range(values.shape[0])]
+    for bit in bits:
+        level = [jnp.where(bit, level[k + 1], level[k]) for k in range(0, len(level), 2)]
+    return level[0]
 
 
 def on_device(
@@ -61,8 +62,9 @@
     planes = adjoint.shape[0]
     across = adjoint.shape[1]
     depth = adjoint.shape[2]
-    cond_cell = lookup(material, conductance)
-    cell_heat_drain = lookup(material, rock_heat_drain)
+    cond_cell, cell_heat_drain = lax.optimization_barrier(
+        (lookup(material, conductance), lookup(material, rock_heat_drain))
+    )
     drain_amounts = cell_heat_drain + ventilation_heat_loss[0]
     local_cell = probe_cell_index - lax.axis_index("space") * (planes * across * depth)
     source = (

time: 169 us -> 169 us (level)
    select_n x0 -> x2, other arithmetic: none -> 12.5 us  [lookup(): jnp.where(bit, level[k + 1], level[k])]
    mul x4, other arithmetic: 19.3 us -> 7.03 us  [on_device(): weighted = cond_cell * current]
  transfers between devices with their start and end apart: 13 -> 13, of which waited for: 9 -> 9; matrix products, arithmetic and copies ran while one was open for 2% -> 3% of each run, Pallas kernels for 0% -> 0%
where the time goes in v2:
time: 169 us; the launch traced here: 168 us
  waiting for transfers between devices  88.7 us (52%)
  starting transfers between devices  33.7 us (20%)
  other arithmetic  30.5 us (18%)
  local copies, waits for them, and re-layouts  11.7 us (7%)
  between operations  3.77 us (2%)
    ppermute x5, waiting for transfers between devices, shifted(): lax.ppermute(value, axis, [(source, source + steps) for source in range(i...  61.3 us
    ppermute x4, waiting for transfers between devices, padded_2(): before = lax.ppermute(last, axis, up)  27.4 us
    ppermute x4, starting transfers between devices, padded_2(): after = lax.ppermute(initial, axis, down)  14.7 us
    select_n x2, other arithmetic, lookup(): jnp.where(bit, level[k + 1], level[k])  12.5 us
    ppermute x5, starting transfers between devices, shifted(): lax.ppermute(value, axis, [(source, source + steps) for source in range(i...  10.7 us
    ppermute x4, starting transfers between devices, padded_2(): before = lax.ppermute(last, axis, up)  8.35 us
    mul x4, other arithmetic, on_device(): weighted = cond_cell * current  7.03 us
    slice x2, local copies, waits for them, and re-layouts, coarsen(): split[:, 1, :, 0]  3.93 us
  transfers between devices with their start and end apart: 13, of which 9 were waited for; matrix products, arithmetic and copies ran while one was open for 3% of the time, Pallas kernels for 0%

profile of v2, /device:TPU:210, one launch (start us, length us, event | category | flops | bytes accessed | tf_op | source)
XLA Modules:
  0.0 168.4 jit_solution(4727463799027529076)
XLA Ops:
  0.0 1.6 fusion.63
  1.6 1.6 fusion.62
  3.3 7.0 %select_select_fusion = (f32[16,128,128]{2,1,0:T(8,128)S(1)}, pred[16,128,128]{2,1,0:T(8,128)(4,1)S(1)}, pred[16,128,128]{2,1,0:T(8,128)(4,1)S(1)}, pred[16,128,128]{2,1,0:T(8,128)(4,1)S(1)}) fusion(f32[]{:T(128)} %bitcast.15, f32[]{:T(128)} %bitcast.14, f32[]{:T(128)} %bitcast.13, f32[]{:T(128)} %bitcast.12, f32[]{:T(128)} %bitcast.11, f32[]{:T(128)} %bitcast.10, ...), kind=kLoop, calls=%fused_computation.59 | loop fusion | flops 3407872 | bytes 2883616 | tf_op jit(solution)/shard_map/jit(_where)/select_n | solution.py:48
  10.3 5.4 %select_select_fusion.1 = f32[16,128,128]{2,1,0:T(8,128)S(1)} fusion(pred[16,128,128]{2,1,0:T(8,128)(4,1)S(1)} %get-tuple-element.20, pred[16,128,128]{2,1,0:T(8,128)(4,1)S(1)} %get-tuple-element.19, pred[16,128,128]{2,1,0:T(8,128)(4,1)S(1)} %get-tuple-element.18, f32[]{:T(128)} %bitcast.7, f32[]{:T(128)} %bitcast.6, f32[]{:T(128)} %bitcast.5, f32[]{:T(128)} %bitcast.4, ...), kind=kLoop, calls=%fused_computation.60 | loop fusion | flops 1835008 | bytes 1835040 | tf_op jit(solution)/shard_map/jit(_where)/select_n | solution.py:48
  15.8 2.0 %scatter_custom_fusion = f32[262144]{0:T(1024)} fusion(s32[64]{0:T(128)S(1)} %compare_select_fusion, f32[64]{0:T(128)} %bitcast.127, f32[]{:T(128)} %constant.11.clone.1), kind=kCustom, calls=%fused_computation.64 | custom fusion | flops 64 | bytes 1049088 | tf_op jit(solution)/shard_map/scatter-add | solution.py:73
  17.8 1.4 fusion.30
  19.2 7.6 %collective-permute-start = (f32[1,128,128]{2,1,0:T(8,128)S(1)}, f32[1,128,128]{2,1,0:T(8,128)S(1)}, u32[]{:S(2)}, u32[]{:S(2)}) collective-permute-start(f32[1,128,128]{2,1,0:T(8,128)S(1)} %get-tuple-element.28), channel_id=1, source_target_pairs={{1,0},{2,1},{3,2},{4,3},{5,4},{6,5},{7,6},{8,7},{9,8},{10,9},{11,1... | collective-permute-start | bytes 196616 | tf_op jit(solution)/shard_map/ppermute | solution.py:17
  26.8 1.9 %collective-permute-start.1 = (f32[1,128,128]{2,1,0:T(8,128)S(1)}, f32[1,128,128]{2,1,0:T(8,128)S(1)}, u32[]{:S(2)}, u32[]{:S(2)}) collective-permute-start(f32[1,128,128]{2,1,0:T(8,128)S(1)} %get-tuple-element.27), channel_id=1, source_target_pairs={{0,1},{1,2},{2,3},{3,4},{4,5},{5,6},{6,7},{7,8},{8,9},{9,10},{10,1... | collective-permute-start | bytes 196616 | tf_op jit(solution)/shard_map/ppermute | solution.py:16
  28.8 2.0 %fusion.56 = (f32[8,1,64,1,128]{4,3,2,1,0:T(1,128)}, f32[8,1,64,1,128]{4,3,2,1,0:T(1,128)}, f32[8,1,64,1,128]{4,3,2,1,0:T(1,128)}, f32[8,1,64,1,128]{4,3,2,1,0:T(1,128)}) fusion(f32[8,2,64,2,128]{4,3,2,1,0:T(2,128)S(1)} %bitcast.101), kind=kLoop, calls=%fused_computation.109 | loop fusion | bytes 2097152 | tf_op jit(solution)/shard_map/slice | solution.py:30
  31.4 5.8 %collective-permute-done.1 = f32[1,128,128]{2,1,0:T(8,128)S(1)} collective-permute-done((f32[1,128,128]{2,1,0:T(8,128)S(1)}, f32[1,128,128]{2,1,0:T(8,128)S(1)}, u32[]{:S(2)}, u32[]{:S(2)}) %collective-permute-start.1) | collective-permute-done | bytes 65568 | tf_op jit(solution)/shard_map/ppermute | solution.py:16
  37.2 0.7 select_maximum_fusion.6
  38.0 2.2 %fusion.50 = (f32[16,128,128]{2,1,0:T(8,128)S(1)}, f32[16,128,128]{2,1,0:T(8,128)}) fusion(f32[16,128,128]{2,1,0:T(8,128)S(1)} %select_select_fusion.1, f32[16,128,128]{2,1,0:T(8,128)S(1)} %get-tuple-element.7, f32[]{:T(128)} %bitcast.96, f32[16,128,128]{2,1,0:T(8,128)S(1)} %fusion.30, f32[18,130,130]{2,1,0:T(8,128)S(1)} %select_maximum_fusion.6, ...), kind=kLoop, calls=%fused_computation.104 | loop fusion | flops 3932160 | bytes 11665412 | tf_op jit(solution)/shard_map/mul | solution.py:79
  40.2 2.6 %collective-permute-start.2 = (f32[1,128,128]{2,1,0:T(8,128)S(1)}, f32[1,128,128]{2,1,0:T(8,128)S(1)}, u32[]{:S(2)}, u32[]{:S(2)}) collective-permute-start(f32[1,128,128]{2,1,0:T(8,128)S(1)} %get-tuple-element.26), channel_id=1, source_target_pairs={{1,0},{2,1},{3,2},{4,3},{5,4},{6,5},{7,6},{8,7},{9,8},{10,9},{11,1... | collective-permute-start | bytes 196616 | tf_op jit(solution)/shard_map/ppermute | solution.py:17
  42.8 1.9 %collective-permute-start.3 = (f32[1,128,128]{2,1,0:T(8,128)S(1)}, f32[1,128,128]{2,1,0:T(8,128)S(1)}, u32[]{:S(2)}, u32[]{:S(2)}) collective-permute-start(f32[1,128,128]{2,1,0:T(8,128)S(1)} %get-tuple-element.25), channel_id=1, source_target_pairs={{0,1},{1,2},{2,3},{3,4},{4,5},{5,6},{6,7},{7,8},{8,9},{9,10},{10,1... | collective-permute-start | bytes 196616 | tf_op jit(solution)/shard_map/ppermute | solution.py:16
  44.7 2.0 %fusion.57 = (f32[8,1,64,1,128]{4,3,2,1,0:T(1,128)}, f32[8,1,64,1,128]{4,3,2,1,0:T(1,128)}, f32[8,1,64,1,128]{4,3,2,1,0:T(1,128)}, f32[8,1,64,1,128]{4,3,2,1,0:T(1,128)}) fusion(f32[8,2,64,2,128]{4,3,2,1,0:T(2,128)S(1)} %bitcast.103), kind=kLoop, calls=%fused_computation.110 | loop fusion | bytes 2097152 | tf_op jit(solution)/shard_map/slice | solution.py:30
  46.8 6.4 %collective-permute-done.3 = f32[1,128,128]{2,1,0:T(8,128)S(1)} collective-permute-done((f32[1,128,128]{2,1,0:T(8,128)S(1)}, f32[1,128,128]{2,1,0:T(8,128)S(1)}, u32[]{:S(2)}, u32[]{:S(2)}) %collective-permute-start.3) | collective-permute-done | bytes 65568 | tf_op jit(solution)/shard_map/ppermute | solution.py:16
  53.2 0.7 select_maximum_fusion.4
  54.0 1.2 fusion.48
  55.2 2.5 %collective-permute-start.4 = (f32[1,128,128]{2,1,0:T(8,128)S(1)}, f32[1,128,128]{2,1,0:T(8,128)S(1)}, u32[]{:S(2)}, u32[]{:S(2)}) collective-permute-start(f32[1,128,128]{2,1,0:T(8,128)S(1)} %get-tuple-element.24), channel_id=1, source_target_pairs={{1,0},{2,1},{3,2},{4,3},{5,4},{6,5},{7,6},{8,7},{9,8},{10,9},{11,1... | collective-permute-start | bytes 196616 | tf_op jit(solution)/shard_map/ppermute | solution.py:17
  57.7 1.9 %collective-permute-start.5 = (f32[1,128,128]{2,1,0:T(8,128)S(1)}, f32[1,128,128]{2,1,0:T(8,128)S(1)}, u32[]{:S(2)}, u32[]{:S(2)}) collective-permute-start(f32[1,128,128]{2,1,0:T(8,128)S(1)} %get-tuple-element.23), channel_id=1, source_target_pairs={{0,1},{1,2},{2,3},{3,4},{4,5},{5,6},{6,7},{7,8},{8,9},{9,10},{10,1... | collective-permute-start | bytes 196616 | tf_op jit(solution)/shard_map/ppermute | solution.py:16
  59.7 0.8 fusion.45
  60.5 7.6 %collective-permute-done.5 = f32[1,128,128]{2,1,0:T(8,128)S(1)} collective-permute-done((f32[1,128,128]{2,1,0:T(8,128)S(1)}, f32[1,128,128]{2,1,0:T(8,128)S(1)}, u32[]{:S(2)}, u32[]{:S(2)}) %collective-permute-start.5) | collective-permute-done | bytes 65568 | tf_op jit(solution)/shard_map/ppermute | solution.py:16
  68.1 0.7 select_maximum_fusion.2
  68.9 2.2 %fusion.46 = (f32[16,128,128]{2,1,0:T(8,128)S(1)}, f32[16,128,128]{2,1,0:T(8,128)}) fusion(f32[16,128,128]{2,1,0:T(8,128)S(1)} %select_select_fusion.1, f32[16,128,128]{2,1,0:T(8,128)S(1)} %get-tuple-element.14, f32[16,128,128]{2,1,0:T(8,128)S(1)} %get-tuple-element.7, f32[]{:T(128)} %bitcast.99, f32[16,128,128]{2,1,0:T(8,128)S(1)} %get-tuple-element.13, ...), kind=kLoop, calls=%fused_computation.102 | loop fusion | flops 3670016 | bytes 10616836 | tf_op jit(solution)/shard_map/mul | solution.py:79
  71.1 1.9 %collective-permute-start.6 = (f32[1,128,128]{2,1,0:T(8,128)S(1)}, f32[1,128,128]{2,1,0:T(8,128)S(1)}, u32[]{:S(2)}, u32[]{:S(2)}) collective-permute-start(f32[1,128,128]{2,1,0:T(8,128)S(1)} %get-tuple-element.22), channel_id=1, source_target_pairs={{1,0},{2,1},{3,2},{4,3},{5,4},{6,5},{7,6},{8,7},{9,8},{10,9},{11,1... | collective-permute-start | bytes 196616 | tf_op jit(solution)/shard_map/ppermute | solution.py:17
  73.0 2.6 %collective-permute-start.7 = (f32[1,128,128]{2,1,0:T(8,128)S(1)}, f32[1,128,128]{2,1,0:T(8,128)S(1)}, u32[]{:S(2)}, u32[]{:S(2)}) collective-permute-start(f32[1,128,128]{2,1,0:T(8,128)S(1)} %get-tuple-element.21), channel_id=1, source_target_pairs={{0,1},{1,2},{2,3},{3,4},{4,5},{5,6},{6,7},{7,8},{8,9},{9,10},{10,1... | collective-permute-start | bytes 196616 | tf_op jit(solution)/shard_map/ppermute | solution.py:16
  75.8 7.6 %collective-permute-done.7 = f32[1,128,128]{2,1,0:T(8,128)S(1)} collective-permute-done((f32[1,128,128]{2,1,0:T(8,128)S(1)}, f32[1,128,128]{2,1,0:T(8,128)S(1)}, u32[]{:S(2)}, u32[]{:S(2)}) %collective-permute-start.7) | collective-permute-done | bytes 65568 | tf_op jit(solution)/shard_map/ppermute | solution.py:16
  83.4 0.7 select_maximum_fusion
  84.6 1.1 fusion.7
  85.7 0.6 fusion.39
  86.4 3.2 %collective-permute-start.8 = (f32[520,128]{1,0:T(8,128)S(1)}, f32[520,128]{1,0:T(8,128)S(1)}, u32[]{:S(2)}, u32[]{:S(2)}) collective-permute-start(f32[520,128]{1,0:T(8,128)S(1)} %concatenate.63), channel_id=1, source_target_pairs={{16,0},{32,16},{48,32},{64,48},{80,64},{96,80},{112,96},{128,112},... | collective-permute-start | bytes 798728 | tf_op jit(solution)/shard_map/ppermute | solution.py:25
  89.6 12.3 %collective-permute-done.8 = f32[520,128]{1,0:T(8,128)S(1)} collective-permute-done((f32[520,128]{1,0:T(8,128)S(1)}, f32[520,128]{1,0:T(8,128)S(1)}, u32[]{:S(2)}, u32[]{:S(2)}) %collective-permute-start.8) | collective-permute-done | bytes 266272 | tf_op jit(solution)/shard_map/ppermute | solution.py:25
  101.9 0.5 slice.329
  103.1 1.9 %collective-permute-start.9 = (f32[520,128]{1,0:T(8,128)S(1)}, f32[520,128]{1,0:T(8,128)S(1)}, u32[]{:S(2)}, u32[]{:S(2)}) collective-permute-start(f32[520,128]{1,0:T(8,128)S(1)} %concatenate.64), channel_id=1, source_target_pairs={{32,0},{48,16},{64,32},{80,48},{96,64},{112,80},{128,96},{144,112}... | collective-permute-start | bytes 798728 | tf_op jit(solution)/shard_map/ppermute | solution.py:25
  105.1 8.1 %collective-permute-done.9 = f32[520,128]{1,0:T(8,128)S(1)} collective-permute-done((f32[520,128]{1,0:T(8,128)S(1)}, f32[520,128]{1,0:T(8,128)S(1)}, u32[]{:S(2)}, u32[]{:S(2)}) %collective-permute-start.9) | collective-permute-done | bytes 266272 | tf_op jit(solution)/shard_map/ppermute | solution.py:25
  113.2 0.5 slice.331
  114.5 2.4 %collective-permute-start.10 = (f32[520,128]{1,0:T(8,128)S(1)}, f32[520,128]{1,0:T(8,128)S(1)}, u32[]{:S(2)}, u32[]{:S(2)}) collective-permute-start(f32[520,128]{1,0:T(8,128)S(1)} %concatenate.65), channel_id=1, source_target_pairs={{64,0},{80,16},{96,32},{112,48},{128,64},{144,80},{160,96},{176,11... | collective-permute-start | bytes 798728 | tf_op jit(solution)/shard_map/ppermute | solution.py:25
  116.9 12.9 %collective-permute-done.10 = f32[520,128]{1,0:T(8,128)S(1)} collective-permute-done((f32[520,128]{1,0:T(8,128)S(1)}, f32[520,128]{1,0:T(8,128)S(1)}, u32[]{:S(2)}, u32[]{:S(2)}) %collective-permute-start.10) | collective-permute-done | bytes 266272 | tf_op jit(solution)/shard_map/ppermute | solution.py:25
  129.7 0.7 copy-done.17
  131.6 1.0 fusion.60
  132.6 1.9 %collective-permute-start.11 = (f32[520,128]{1,0:T(8,128)S(1)}, f32[520,128]{1,0:T(8,128)S(1)}, u32[]{:S(2)}, u32[]{:S(2)}) collective-permute-start(f32[520,128]{1,0:T(8,128)S(1)} %concatenate.66), channel_id=1, source_target_pairs={{128,0},{144,16},{160,32},{176,48},{192,64},{208,80},{224,96},{240... | collective-permute-start | bytes 798728 | tf_op jit(solution)/shard_map/ppermute | solution.py:25
  134.6 17.0 %collective-permute-done.11 = f32[520,128]{1,0:T(8,128)S(1)} collective-permute-done((f32[520,128]{1,0:T(8,128)S(1)}, f32[520,128]{1,0:T(8,128)S(1)}, u32[]{:S(2)}, u32[]{:S(2)}) %collective-permute-start.11) | collective-permute-done | bytes 266272 | tf_op jit(solution)/shard_map/ppermute | solution.py:25
  151.6 0.7 copy-done.18
  152.3 0.5 slice.335
  153.4 1.0 fusion.61
  154.4 1.3 collective-permute-start.12
  155.7 10.9 %collective-permute-done.12 = f32[520,128]{1,0:T(8,128)S(1)} collective-permute-done((f32[520,128]{1,0:T(8,128)S(1)}, f32[520,128]{1,0:T(8,128)S(1)}, u32[]{:S(2)}, u32[]{:S(2)}) %collective-permute-start.12) | collective-permute-done | bytes 266272 | tf_op jit(solution)/shard_map/ppermute | solution.py:25
  167.3 1.1 add_bitcast_fusion
  (66 shorter events, 2.2 us)
Async XLA Ops:
  0.0 15.7 %copy-start.19 = (s32[64]{0:T(128)S(1)}, s32[64]{0:T(128)}, u32[]{:S(2)}) copy-start(s32[64]{0:T(128)} %param.9) | copy-start | bytes 772
  3.3 14.5 %copy-start = (f32[1,16,128,128]{3,2,1,0:T(8,128)S(1)}, f32[1,16,128,128]{3,2,1,0:T(8,128)}, u32[]{:S(2)}) copy-start(f32[1,16,128,128]{3,2,1,0:T(8,128)} %param.7) | copy-start | bytes 3145732
  19.2 12.2 %collective-permute-start = (f32[1,128,128]{2,1,0:T(8,128)S(1)}, f32[1,128,128]{2,1,0:T(8,128)S(1)}, u32[]{:S(2)}, u32[]{:S(2)}) collective-permute-start(f32[1,128,128]{2,1,0:T(8,128)S(1)} %get-tuple-element.28), channel_id=1, source_target_pairs={{1,0},{2,1},{3,2},{4,3},{5,4},{6,5},{7,6},{8,7},{9,8},{10,9},{11,1... | collective-permute-start | bytes 196616 | tf_op jit(solution)/shard_map/ppermute | solution.py:17
  26.8 10.4 %collective-permute-start.1 = (f32[1,128,128]{2,1,0:T(8,128)S(1)}, f32[1,128,128]{2,1,0:T(8,128)S(1)}, u32[]{:S(2)}, u32[]{:S(2)}) collective-permute-start(f32[1,128,128]{2,1,0:T(8,128)S(1)} %get-tuple-element.27), channel_id=1, source_target_pairs={{0,1},{1,2},{2,3},{3,4},{4,5},{5,6},{6,7},{7,8},{8,9},{9,10},{10,1... | collective-permute-start | bytes 196616 | tf_op jit(solution)/shard_map/ppermute | solution.py:16
  28.8 9.2 %copy-start.1 = (f32[1,16,128,128]{3,2,1,0:T(8,128)S(1)}, f32[1,16,128,128]{3,2,1,0:T(8,128)}, u32[]{:S(2)}) copy-start(f32[1,16,128,128]{3,2,1,0:T(8,128)} %param.7) | copy-start | bytes 3145732
  28.8 9.2 %copy-start.2 = (f32[262144]{0:T(1024)S(1)}, f32[262144]{0:T(1024)}, u32[]{:S(2)}) copy-start(f32[262144]{0:T(1024)} %scatter_custom_fusion) | copy-start | bytes 3145732
  40.2 6.6 %collective-permute-start.2 = (f32[1,128,128]{2,1,0:T(8,128)S(1)}, f32[1,128,128]{2,1,0:T(8,128)S(1)}, u32[]{:S(2)}, u32[]{:S(2)}) collective-permute-start(f32[1,128,128]{2,1,0:T(8,128)S(1)} %get-tuple-element.26), channel_id=1, source_target_pairs={{1,0},{2,1},{3,2},{4,3},{5,4},{6,5},{7,6},{8,7},{9,8},{10,9},{11,1... | collective-permute-start | bytes 196616 | tf_op jit(solution)/shard_map/ppermute | solution.py:17
  42.8 10.4 %collective-permute-start.3 = (f32[1,128,128]{2,1,0:T(8,128)S(1)}, f32[1,128,128]{2,1,0:T(8,128)S(1)}, u32[]{:S(2)}, u32[]{:S(2)}) collective-permute-start(f32[1,128,128]{2,1,0:T(8,128)S(1)} %get-tuple-element.25), channel_id=1, source_target_pairs={{0,1},{1,2},{2,3},{3,4},{4,5},{5,6},{6,7},{7,8},{8,9},{9,10},{10,1... | collective-permute-start | bytes 196616 | tf_op jit(solution)/shard_map/ppermute | solution.py:16
  46.8 7.2 %copy-start.7 = (f32[16,128,128]{2,1,0:T(8,128)S(1)}, f32[16,128,128]{2,1,0:T(8,128)}, u32[]{:S(2)}) copy-start(f32[16,128,128]{2,1,0:T(8,128)} %get-tuple-element.16) | copy-start | bytes 3145732
  53.9 5.7 %copy-start.13 = (f32[8,1,64,1,128]{4,3,2,1,0:T(1,128)S(1)}, f32[8,1,64,1,128]{4,3,2,1,0:T(1,128)}, u32[]{:S(2)}) copy-start(f32[8,1,64,1,128]{4,3,2,1,0:T(1,128)} %get-tuple-element.29) | copy-start | bytes 786436
  53.9 5.7 %copy-start.14 = (f32[8,1,64,1,128]{4,3,2,1,0:T(1,128)S(1)}, f32[8,1,64,1,128]{4,3,2,1,0:T(1,128)}, u32[]{:S(2)}) copy-start(f32[8,1,64,1,128]{4,3,2,1,0:T(1,128)} %get-tuple-element.30) | copy-start | bytes 786436
  54.0 5.7 %copy-start.15 = (f32[8,1,64,1,128]{4,3,2,1,0:T(1,128)S(1)}, f32[8,1,64,1,128]{4,3,2,1,0:T(1,128)}, u32[]{:S(2)}) copy-start(f32[8,1,64,1,128]{4,3,2,1,0:T(1,128)} %get-tuple-element.31) | copy-start | bytes 786436
  54.0 5.7 %copy-start.16 = (f32[8,1,64,1,128]{4,3,2,1,0:T(1,128)S(1)}, f32[8,1,64,1,128]{4,3,2,1,0:T(1,128)}, u32[]{:S(2)}) copy-start(f32[8,1,64,1,128]{4,3,2,1,0:T(1,128)} %get-tuple-element.32) | copy-start | bytes 786436
  55.2 5.3 %collective-permute-start.4 = (f32[1,128,128]{2,1,0:T(8,128)S(1)}, f32[1,128,128]{2,1,0:T(8,128)S(1)}, u32[]{:S(2)}, u32[]{:S(2)}) collective-permute-start(f32[1,128,128]{2,1,0:T(8,128)S(1)} %get-tuple-element.24), channel_id=1, source_target_pairs={{1,0},{2,1},{3,2},{4,3},{5,4},{6,5},{7,6},{8,7},{9,8},{10,9},{11,1... | collective-permute-start | bytes 196616 | tf_op jit(solution)/shard_map/ppermute | solution.py:17
  57.7 10.4 %collective-permute-start.5 = (f32[1,128,128]{2,1,0:T(8,128)S(1)}, f32[1,128,128]{2,1,0:T(8,128)S(1)}, u32[]{:S(2)}, u32[]{:S(2)}) collective-permute-start(f32[1,128,128]{2,1,0:T(8,128)S(1)} %get-tuple-element.23), channel_id=1, source_target_pairs={{0,1},{1,2},{2,3},{3,4},{4,5},{5,6},{6,7},{7,8},{8,9},{9,10},{10,1... | collective-permute-start | bytes 196616 | tf_op jit(solution)/shard_map/ppermute | solution.py:16
  68.8 6.8 %copy-start.9 = (f32[8,1,64,1,128]{4,3,2,1,0:T(1,128)S(1)}, f32[8,1,64,1,128]{4,3,2,1,0:T(1,128)}, u32[]{:S(2)}) copy-start(f32[8,1,64,1,128]{4,3,2,1,0:T(1,128)} %get-tuple-element.33) | copy-start | bytes 786436
  68.9 6.8 %copy-start.10 = (f32[8,1,64,1,128]{4,3,2,1,0:T(1,128)S(1)}, f32[8,1,64,1,128]{4,3,2,1,0:T(1,128)}, u32[]{:S(2)}) copy-start(f32[8,1,64,1,128]{4,3,2,1,0:T(1,128)} %get-tuple-element.34) | copy-start | bytes 786436
  68.9 6.8 %copy-start.11 = (f32[8,1,64,1,128]{4,3,2,1,0:T(1,128)S(1)}, f32[8,1,64,1,128]{4,3,2,1,0:T(1,128)}, u32[]{:S(2)}) copy-start(f32[8,1,64,1,128]{4,3,2,1,0:T(1,128)} %get-tuple-element.35) | copy-start | bytes 786436
  68.9 6.8 %copy-start.12 = (f32[8,1,64,1,128]{4,3,2,1,0:T(1,128)S(1)}, f32[8,1,64,1,128]{4,3,2,1,0:T(1,128)}, u32[]{:S(2)}) copy-start(f32[8,1,64,1,128]{4,3,2,1,0:T(1,128)} %get-tuple-element.36) | copy-start | bytes 786436
  71.1 4.7 %collective-permute-start.6 = (f32[1,128,128]{2,1,0:T(8,128)S(1)}, f32[1,128,128]{2,1,0:T(8,128)S(1)}, u32[]{:S(2)}, u32[]{:S(2)}) collective-permute-start(f32[1,128,128]{2,1,0:T(8,128)S(1)} %get-tuple-element.22), channel_id=1, source_target_pairs={{1,0},{2,1},{3,2},{4,3},{5,4},{6,5},{7,6},{8,7},{9,8},{10,9},{11,1... | collective-permute-start | bytes 196616 | tf_op jit(solution)/shard_map/ppermute | solution.py:17
  73.0 10.4 %collective-permute-start.7 = (f32[1,128,128]{2,1,0:T(8,128)S(1)}, f32[1,128,128]{2,1,0:T(8,128)S(1)}, u32[]{:S(2)}, u32[]{:S(2)}) collective-permute-start(f32[1,128,128]{2,1,0:T(8,128)S(1)} %get-tuple-element.21), channel_id=1, source_target_pairs={{0,1},{1,2},{2,3},{3,4},{4,5},{5,6},{6,7},{7,8},{8,9},{9,10},{10,1... | collective-permute-start | bytes 196616 | tf_op jit(solution)/shard_map/ppermute | solution.py:16
  75.8 8.8 %copy-start.3 = (f32[8,1,64,1,128]{4,2,0,3,1:T(8,128)}, f32[8,1,64,1,128]{4,2,0,3,1:T(8,128)S(1)}, u32[]{:S(2)}) copy-start(f32[8,1,64,1,128]{4,2,0,3,1:T(8,128)S(1)} %exponential_multiply_fusion) | copy-start | bytes 786436
  75.8 8.8 %copy-start.6 = (f32[16,128,128]{2,1,0:T(8,128)S(1)}, f32[16,128,128]{2,1,0:T(8,128)}, u32[]{:S(2)}) copy-start(f32[16,128,128]{2,1,0:T(8,128)} %get-tuple-element.12) | copy-start | bytes 3145732
  84.6 1.7 %copy-start.4 = (f32[8,1,64,1,128]{4,2,0,3,1:T(8,128)S(1)}, f32[8,1,64,1,128]{4,2,0,3,1:T(8,128)}, u32[]{:S(2)}) copy-start(f32[8,1,64,1,128]{4,2,0,3,1:T(8,128)} %copy-done.3) | copy-start | bytes 786436
  85.7 17.4 %copy-start.8 = (f32[8,1,64,1,128]{4,2,0,3,1:T(8,128)S(1)}, f32[8,1,64,1,128]{4,2,0,3,1:T(8,128)}, u32[]{:S(2)}) copy-start(f32[8,1,64,1,128]{4,2,0,3,1:T(8,128)} %get-tuple-element.9) | copy-start | bytes 786436
  86.4 15.5 %collective-permute-start.8 = (f32[520,128]{1,0:T(8,128)S(1)}, f32[520,128]{1,0:T(8,128)S(1)}, u32[]{:S(2)}, u32[]{:S(2)}) collective-permute-start(f32[520,128]{1,0:T(8,128)S(1)} %concatenate.63), channel_id=1, source_target_pairs={{16,0},{32,16},{48,32},{64,48},{80,64},{96,80},{112,96},{128,112},... | collective-permute-start | bytes 798728 | tf_op jit(solution)/shard_map/ppermute | solution.py:25
  103.1 10.1 %collective-permute-start.9 = (f32[520,128]{1,0:T(8,128)S(1)}, f32[520,128]{1,0:T(8,128)S(1)}, u32[]{:S(2)}, u32[]{:S(2)}) collective-permute-start(f32[520,128]{1,0:T(8,128)S(1)} %concatenate.64), channel_id=1, source_target_pairs={{32,0},{48,16},{64,32},{80,48},{96,64},{112,80},{128,96},{144,112}... | collective-permute-start | bytes 798728 | tf_op jit(solution)/shard_map/ppermute | solution.py:25
  114.5 15.3 %collective-permute-start.10 = (f32[520,128]{1,0:T(8,128)S(1)}, f32[520,128]{1,0:T(8,128)S(1)}, u32[]{:S(2)}, u32[]{:S(2)}) collective-permute-start(f32[520,128]{1,0:T(8,128)S(1)} %concatenate.65), channel_id=1, source_target_pairs={{64,0},{80,16},{96,32},{112,48},{128,64},{144,80},{160,96},{176,11... | collective-permute-start | bytes 798728 | tf_op jit(solution)/shard_map/ppermute | solution.py:25
  129.7 0.7 copy-start.17
  131.5 35.1 %copy-start.5 = (f32[8,1,64,1,128]{4,2,0,3,1:T(8,128)S(1)}, f32[8,1,64,1,128]{4,2,0,3,1:T(8,128)}, u32[]{:S(2)}) copy-start(f32[8,1,64,1,128]{4,2,0,3,1:T(8,128)} %copy-done.3) | copy-start | bytes 786436
  132.6 19.0 %collective-permute-start.11 = (f32[520,128]{1,0:T(8,128)S(1)}, f32[520,128]{1,0:T(8,128)S(1)}, u32[]{:S(2)}, u32[]{:S(2)}) collective-permute-start(f32[520,128]{1,0:T(8,128)S(1)} %concatenate.66), channel_id=1, source_target_pairs={{128,0},{144,16},{160,32},{176,48},{192,64},{208,80},{224,96},{240... | collective-permute-start | bytes 798728 | tf_op jit(solution)/shard_map/ppermute | solution.py:25
  151.6 0.7 copy-start.18
  154.4 12.2 %collective-permute-start.12 = (f32[520,128]{1,0:T(8,128)S(1)}, f32[520,128]{1,0:T(8,128)S(1)}, u32[]{:S(2)}, u32[]{:S(2)}) collective-permute-start(f32[520,128]{1,0:T(8,128)S(1)} %concatenate.67), channel_id=1, source_target_pairs={{256,0},{272,16},{288,32},{304,48},{320,64},{336,80},{352,96},{368... | collective-permute-start | bytes 798728 | tf_op jit(solution)/shard_map/ppermute | solution.py:25

commit v3 on v2

--- a/solution.py
+++ b/solution.py
@@ -1,6 +1,8 @@
 import jax
 import jax.numpy as jnp
 from jax import lax
+from jax.experimental import pallas as pl
+from jax.experimental.pallas import tpu as pltpu
 from jax.sharding import PartitionSpec as P
 
 FINE_STEPS = 4
@@ -41,12 +43,33 @@
     return x_sides + y_sides + z_sides
 
 
-def lookup(material, values):
+def _select_tree(material, table_ref):
     bits = [(material & (1 << b)) != 0 for b in range(3)]
-    level = [values[k] for k in range(values.shape[0])]
+    level = [table_ref[k] for k in range(8)]
     for bit in bits:
         level = [jnp.where(bit, level[k + 1], level[k]) for k in range(0, len(level), 2)]
     return level[0]
+
+
+def _lookup_kernel(cond_table, drain_table, material_ref, cond_ref, drain_ref):
+    material = material_ref[...]
+    cond_ref[...] = _select_tree(material, cond_table)
+    drain_ref[...] = _select_tree(material, drain_table)
+
+
+def lookup_both(material, conductance, rock_heat_drain):
+    planes = material.shape[0]
+    block = (4,) + material.shape[1:]
+    spec = pl.BlockSpec(block, lambda i: (i, 0, 0))
+    smem = pl.BlockSpec(memory_space=pltpu.SMEM)
+    out = jax.ShapeDtypeStruct(material.shape, jnp.float32)
+    return pl.pallas_call(
+        _lookup_kernel,
+        grid=(planes // block[0],),
+        in_specs=[smem, smem, spec],
+        out_specs=[spec, spec],
+        out_shape=[out, out],
+    )(conductance, rock_heat_drain, material)
 
 
 def on_device(
@@ -62,9 +85,7 @@
     planes = adjoint.shape[0]
     across = adjoint.shape[1]
     depth = adjoint.shape[2]
-    cond_cell, cell_heat_drain = lax.optimization_barrier(
-        (lookup(material, conductance), lookup(material, rock_heat_drain))
-    )
+    cond_cell, cell_heat_drain = lookup_both(material, conductance, rock_heat_drain)
     drain_amounts = cell_heat_drain + ventilation_heat_loss[0]
     local_cell = probe_cell_index - lax.axis_index("space") * (planes * across * depth)
     source = (

time: 169 us -> 159 us (0.941)
  the two profiles are of different devices: /device:TPU:210 before, /device:TPU:214 now
where the time goes in v3:
time: 159 us; the launch traced here: 158 us
  waiting for transfers between devices  88.4 us (56%)
  starting transfers between devices  34.8 us (22%)
  other arithmetic  18.6 us (12%)
  local copies, waits for them, and re-layouts  8.47 us (5%)
  Pallas kernels  3.85 us (2%)
  between operations  3.79 us (2%)
    ppermute x5, waiting for transfers between devices, shifted(): lax.ppermute(value, axis, [(source, source + steps) for source in range(i...  61 us
    ppermute x4, waiting for transfers between devices, padded_2(): before = lax.ppermute(last, axis, up)  27.4 us
    ppermute x4, starting transfers between devices, padded_2(): after = lax.ppermute(initial, axis, down)  15.4 us
    ppermute x5, starting transfers between devices, shifted(): lax.ppermute(value, axis, [(source, source + steps) for source in range(i...  11 us
    ppermute x4, starting transfers between devices, padded_2(): before = lax.ppermute(last, axis, up)  8.35 us
    mul x4, other arithmetic, on_device(): weighted = cond_cell * current  7.4 us
    slice x2, local copies, waits for them, and re-layouts, coarsen(): split[:, 1, :, 0]  3.93 us
    pallas_call x1, Pallas kernels, lookup_both(): pl.pallas_call(_lookup_kernel, grid=(planes // block[0],), in_specs=[smem...  3.85 us
  transfers between devices with their start and end apart: 13, of which 9 were waited for; matrix products, arithmetic and copies ran while one was open for 3% of the time, Pallas kernels for 0%

profile of v3, /device:TPU:214, one launch (start us, length us, event | category | flops | bytes accessed | tf_op | source)
XLA Modules:
  0.0 157.9 jit_solution(12774482522900824968)
XLA Ops:
  0.0 0.7 compare_select_fusion
  0.8 3.8 %shard_map.73 = (f32[16,128,128]{2,1,0:T(8,128)}, f32[16,128,128]{2,1,0:T(8,128)}) custom-call(f32[8]{0:T(128)} %cond_table.1, f32[8]{0:T(128)} %drain_table.1, s32[16,128,128]{2,1,0:T(8,128)} %material_ref.1), custom_call_target="tpu_custom_call" | custom-call | tf_op jit(solution)/shard_map/pallas_call | solution.py:66
  4.6 1.4 scatter_custom_fusion
  6.1 1.8 %fusion.30 = f32[16,128,128]{2,1,0:T(8,128)S(1)} fusion(f32[16,128,128]{2,1,0:T(8,128)} %get-tuple-element.8, f32[16,128,128]{2,1,0:T(8,128)S(1)} %bitcast.88, f32[1,16,128,128]{3,2,1,0:T(8,128)S(1)} %copy-done.2), kind=kLoop, calls=%fused_computation.61 | loop fusion | flops 524288 | bytes 4194304 | tf_op jit(solution)/shard_map/mul | solution.py:100
  7.9 7.9 %collective-permute-start = (f32[1,128,128]{2,1,0:T(8,128)S(1)}, f32[1,128,128]{2,1,0:T(8,128)S(1)}, u32[]{:S(2)}, u32[]{:S(2)}) collective-permute-start(f32[1,128,128]{2,1,0:T(8,128)S(1)} %get-tuple-element.24), channel_id=1, source_target_pairs={{1,0},{2,1},{3,2},{4,3},{5,4},{6,5},{7,6},{8,7},{9,8},{10,9},{11,1... | collective-permute-start | bytes 196616 | tf_op jit(solution)/shard_map/ppermute | solution.py:19
  15.8 1.9 %collective-permute-start.1 = (f32[1,128,128]{2,1,0:T(8,128)S(1)}, f32[1,128,128]{2,1,0:T(8,128)S(1)}, u32[]{:S(2)}, u32[]{:S(2)}) collective-permute-start(f32[1,128,128]{2,1,0:T(8,128)S(1)} %get-tuple-element.23), channel_id=1, source_target_pairs={{0,1},{1,2},{2,3},{3,4},{4,5},{5,6},{6,7},{7,8},{8,9},{9,10},{10,1... | collective-permute-start | bytes 196616 | tf_op jit(solution)/shard_map/ppermute | solution.py:18
  17.7 1.9 %fusion.56 = (f32[8,1,64,1,128]{4,3,2,1,0:T(1,128)}, f32[8,1,64,1,128]{4,3,2,1,0:T(1,128)}, f32[8,1,64,1,128]{4,3,2,1,0:T(1,128)}, f32[8,1,64,1,128]{4,3,2,1,0:T(1,128)}) fusion(f32[8,2,64,2,128]{4,3,2,1,0:T(2,128)S(1)} %bitcast.85), kind=kLoop, calls=%fused_computation.104 | loop fusion | bytes 2097152 | tf_op jit(solution)/shard_map/slice | solution.py:32
  20.4 5.8 %collective-permute-done.1 = f32[1,128,128]{2,1,0:T(8,128)S(1)} collective-permute-done((f32[1,128,128]{2,1,0:T(8,128)S(1)}, f32[1,128,128]{2,1,0:T(8,128)S(1)}, u32[]{:S(2)}, u32[]{:S(2)}) %collective-permute-start.1) | collective-permute-done | bytes 65568 | tf_op jit(solution)/shard_map/ppermute | solution.py:18
  26.2 0.7 select_maximum_fusion.6
  26.9 2.2 %fusion.50 = (f32[16,128,128]{2,1,0:T(8,128)S(1)}, f32[16,128,128]{2,1,0:T(8,128)}) fusion(f32[16,128,128]{2,1,0:T(8,128)S(1)} %copy-done.1, f32[16,128,128]{2,1,0:T(8,128)S(1)} %copy-done, f32[]{:T(128)} %bitcast.80, f32[16,128,128]{2,1,0:T(8,128)S(1)} %fusion.30, f32[18,130,130]{2,1,0:T(8,128)S(1)} %select_maximum_fusion.6, ...), kind=kLoop, calls=%fused_computation.99 | loop fusion | flops 3932160 | bytes 11665412 | tf_op jit(solution)/shard_map/mul | solution.py:100
  29.1 3.1 %collective-permute-start.2 = (f32[1,128,128]{2,1,0:T(8,128)S(1)}, f32[1,128,128]{2,1,0:T(8,128)S(1)}, u32[]{:S(2)}, u32[]{:S(2)}) collective-permute-start(f32[1,128,128]{2,1,0:T(8,128)S(1)} %get-tuple-element.22), channel_id=1, source_target_pairs={{1,0},{2,1},{3,2},{4,3},{5,4},{6,5},{7,6},{8,7},{9,8},{10,9},{11,1... | collective-permute-start | bytes 196616 | tf_op jit(solution)/shard_map/ppermute | solution.py:19
  32.2 1.9 %collective-permute-start.3 = (f32[1,128,128]{2,1,0:T(8,128)S(1)}, f32[1,128,128]{2,1,0:T(8,128)S(1)}, u32[]{:S(2)}, u32[]{:S(2)}) collective-permute-start(f32[1,128,128]{2,1,0:T(8,128)S(1)} %get-tuple-element.21), channel_id=1, source_target_pairs={{0,1},{1,2},{2,3},{3,4},{4,5},{5,6},{6,7},{7,8},{8,9},{9,10},{10,1... | collective-permute-start | bytes 196616 | tf_op jit(solution)/shard_map/ppermute | solution.py:18
  34.2 2.0 %fusion.57 = (f32[8,1,64,1,128]{4,3,2,1,0:T(1,128)}, f32[8,1,64,1,128]{4,3,2,1,0:T(1,128)}, f32[8,1,64,1,128]{4,3,2,1,0:T(1,128)}, f32[8,1,64,1,128]{4,3,2,1,0:T(1,128)}) fusion(f32[8,2,64,2,128]{4,3,2,1,0:T(2,128)S(1)} %bitcast.87), kind=kLoop, calls=%fused_computation.105 | loop fusion | bytes 2097152 | tf_op jit(solution)/shard_map/slice | solution.py:32
  36.2 6.4 %collective-permute-done.3 = f32[1,128,128]{2,1,0:T(8,128)S(1)} collective-permute-done((f32[1,128,128]{2,1,0:T(8,128)S(1)}, f32[1,128,128]{2,1,0:T(8,128)S(1)}, u32[]{:S(2)}, u32[]{:S(2)}) %collective-permute-start.3) | collective-permute-done | bytes 65568 | tf_op jit(solution)/shard_map/ppermute | solution.py:18
  42.6 0.7 select_maximum_fusion.4
  43.4 1.2 fusion.48
  44.6 2.5 %collective-permute-start.4 = (f32[1,128,128]{2,1,0:T(8,128)S(1)}, f32[1,128,128]{2,1,0:T(8,128)S(1)}, u32[]{:S(2)}, u32[]{:S(2)}) collective-permute-start(f32[1,128,128]{2,1,0:T(8,128)S(1)} %get-tuple-element.20), channel_id=1, source_target_pairs={{1,0},{2,1},{3,2},{4,3},{5,4},{6,5},{7,6},{8,7},{9,8},{10,9},{11,1... | collective-permute-start | bytes 196616 | tf_op jit(solution)/shard_map/ppermute | solution.py:19
  47.1 1.9 %collective-permute-start.5 = (f32[1,128,128]{2,1,0:T(8,128)S(1)}, f32[1,128,128]{2,1,0:T(8,128)S(1)}, u32[]{:S(2)}, u32[]{:S(2)}) collective-permute-start(f32[1,128,128]{2,1,0:T(8,128)S(1)} %get-tuple-element.19), channel_id=1, source_target_pairs={{0,1},{1,2},{2,3},{3,4},{4,5},{5,6},{6,7},{7,8},{8,9},{9,10},{10,1... | collective-permute-start | bytes 196616 | tf_op jit(solution)/shard_map/ppermute | solution.py:18
  49.1 0.8 fusion.45
  49.9 7.6 %collective-permute-done.5 = f32[1,128,128]{2,1,0:T(8,128)S(1)} collective-permute-done((f32[1,128,128]{2,1,0:T(8,128)S(1)}, f32[1,128,128]{2,1,0:T(8,128)S(1)}, u32[]{:S(2)}, u32[]{:S(2)}) %collective-permute-start.5) | collective-permute-done | bytes 65568 | tf_op jit(solution)/shard_map/ppermute | solution.py:18
  57.5 0.7 select_maximum_fusion.2
  58.3 2.2 %fusion.46 = (f32[16,128,128]{2,1,0:T(8,128)S(1)}, f32[16,128,128]{2,1,0:T(8,128)}) fusion(f32[16,128,128]{2,1,0:T(8,128)S(1)} %copy-done.1, f32[16,128,128]{2,1,0:T(8,128)S(1)} %get-tuple-element.14, f32[16,128,128]{2,1,0:T(8,128)S(1)} %copy-done, f32[]{:T(128)} %bitcast.83, f32[16,128,128]{2,1,0:T(8,128)S(1)} %get-tuple-element.13, ...), kind=kLoop, calls=%fused_computation.97 | loop fusion | flops 3670016 | bytes 10616836 | tf_op jit(solution)/shard_map/mul | solution.py:100
  60.5 1.9 %collective-permute-start.6 = (f32[1,128,128]{2,1,0:T(8,128)S(1)}, f32[1,128,128]{2,1,0:T(8,128)S(1)}, u32[]{:S(2)}, u32[]{:S(2)}) collective-permute-start(f32[1,128,128]{2,1,0:T(8,128)S(1)} %get-tuple-element.18), channel_id=1, source_target_pairs={{1,0},{2,1},{3,2},{4,3},{5,4},{6,5},{7,6},{8,7},{9,8},{10,9},{11,1... | collective-permute-start | bytes 196616 | tf_op jit(solution)/shard_map/ppermute | solution.py:19
  62.5 2.6 %collective-permute-start.7 = (f32[1,128,128]{2,1,0:T(8,128)S(1)}, f32[1,128,128]{2,1,0:T(8,128)S(1)}, u32[]{:S(2)}, u32[]{:S(2)}) collective-permute-start(f32[1,128,128]{2,1,0:T(8,128)S(1)} %get-tuple-element.17), channel_id=1, source_target_pairs={{0,1},{1,2},{2,3},{3,4},{4,5},{5,6},{6,7},{7,8},{8,9},{9,10},{10,1... | collective-permute-start | bytes 196616 | tf_op jit(solution)/shard_map/ppermute | solution.py:18
  65.2 7.6 %collective-permute-done.7 = f32[1,128,128]{2,1,0:T(8,128)S(1)} collective-permute-done((f32[1,128,128]{2,1,0:T(8,128)S(1)}, f32[1,128,128]{2,1,0:T(8,128)S(1)}, u32[]{:S(2)}, u32[]{:S(2)}) %collective-permute-start.7) | collective-permute-done | bytes 65568 | tf_op jit(solution)/shard_map/ppermute | solution.py:18
  72.8 0.7 select_maximum_fusion
  73.6 0.4 broadcast_in_dim.29
  74.0 1.1 fusion.7
  75.1 0.6 fusion.39
  75.8 3.5 %collective-permute-start.8 = (f32[520,128]{1,0:T(8,128)S(1)}, f32[520,128]{1,0:T(8,128)S(1)}, u32[]{:S(2)}, u32[]{:S(2)}) collective-permute-start(f32[520,128]{1,0:T(8,128)S(1)} %concatenate.63), channel_id=1, source_target_pairs={{16,0},{32,16},{48,32},{64,48},{80,64},{96,80},{112,96},{128,112},... | collective-permute-start | bytes 798728 | tf_op jit(solution)/shard_map/ppermute | solution.py:27
  79.3 12.0 %collective-permute-done.8 = f32[520,128]{1,0:T(8,128)S(1)} collective-permute-done((f32[520,128]{1,0:T(8,128)S(1)}, f32[520,128]{1,0:T(8,128)S(1)}, u32[]{:S(2)}, u32[]{:S(2)}) %collective-permute-start.8) | collective-permute-done | bytes 266272 | tf_op jit(solution)/shard_map/ppermute | solution.py:27
  91.3 0.5 slice.265
  92.5 1.9 %collective-permute-start.9 = (f32[520,128]{1,0:T(8,128)S(1)}, f32[520,128]{1,0:T(8,128)S(1)}, u32[]{:S(2)}, u32[]{:S(2)}) collective-permute-start(f32[520,128]{1,0:T(8,128)S(1)} %concatenate.64), channel_id=1, source_target_pairs={{32,0},{48,16},{64,32},{80,48},{96,64},{112,80},{128,96},{144,112}... | collective-permute-start | bytes 798728 | tf_op jit(solution)/shard_map/ppermute | solution.py:27
  94.5 8.1 %collective-permute-done.9 = f32[520,128]{1,0:T(8,128)S(1)} collective-permute-done((f32[520,128]{1,0:T(8,128)S(1)}, f32[520,128]{1,0:T(8,128)S(1)}, u32[]{:S(2)}, u32[]{:S(2)}) %collective-permute-start.9) | collective-permute-done | bytes 266272 | tf_op jit(solution)/shard_map/ppermute | solution.py:27
  102.7 0.5 slice.267
  103.9 2.4 %collective-permute-start.10 = (f32[520,128]{1,0:T(8,128)S(1)}, f32[520,128]{1,0:T(8,128)S(1)}, u32[]{:S(2)}, u32[]{:S(2)}) collective-permute-start(f32[520,128]{1,0:T(8,128)S(1)} %concatenate.65), channel_id=1, source_target_pairs={{64,0},{80,16},{96,32},{112,48},{128,64},{144,80},{160,96},{176,11... | collective-permute-start | bytes 798728 | tf_op jit(solution)/shard_map/ppermute | solution.py:27
  106.3 12.9 %collective-permute-done.10 = f32[520,128]{1,0:T(8,128)S(1)} collective-permute-done((f32[520,128]{1,0:T(8,128)S(1)}, f32[520,128]{1,0:T(8,128)S(1)}, u32[]{:S(2)}, u32[]{:S(2)}) %collective-permute-start.10) | collective-permute-done | bytes 266272 | tf_op jit(solution)/shard_map/ppermute | solution.py:27
  119.2 0.7 copy-done.20
  119.9 0.5 slice.269
  121.0 1.0 fusion.60
  122.1 1.9 %collective-permute-start.11 = (f32[520,128]{1,0:T(8,128)S(1)}, f32[520,128]{1,0:T(8,128)S(1)}, u32[]{:S(2)}, u32[]{:S(2)}) collective-permute-start(f32[520,128]{1,0:T(8,128)S(1)} %concatenate.66), channel_id=1, source_target_pairs={{128,0},{144,16},{160,32},{176,48},{192,64},{208,80},{224,96},{240... | collective-permute-start | bytes 798728 | tf_op jit(solution)/shard_map/ppermute | solution.py:27
  124.0 17.0 %collective-permute-done.11 = f32[520,128]{1,0:T(8,128)S(1)} collective-permute-done((f32[520,128]{1,0:T(8,128)S(1)}, f32[520,128]{1,0:T(8,128)S(1)}, u32[]{:S(2)}, u32[]{:S(2)}) %collective-permute-start.11) | collective-permute-done | bytes 266272 | tf_op jit(solution)/shard_map/ppermute | solution.py:27
  141.0 0.7 copy-done.21
  141.7 0.5 slice.271
  142.8 1.0 fusion.61
  143.8 1.3 collective-permute-start.12
  145.1 10.9 %collective-permute-done.12 = f32[520,128]{1,0:T(8,128)S(1)} collective-permute-done((f32[520,128]{1,0:T(8,128)S(1)}, f32[520,128]{1,0:T(8,128)S(1)}, u32[]{:S(2)}, u32[]{:S(2)}) %collective-permute-start.12) | collective-permute-done | bytes 266272 | tf_op jit(solution)/shard_map/ppermute | solution.py:27
  156.7 1.1 add_bitcast_fusion
  (67 shorter events, 1.3 us)
Async XLA Ops:
  0.0 6.1 %copy-start.2 = (f32[1,16,128,128]{3,2,1,0:T(8,128)S(1)}, f32[1,16,128,128]{3,2,1,0:T(8,128)}, u32[]{:S(2)}) copy-start(f32[1,16,128,128]{3,2,1,0:T(8,128)} %param.7) | copy-start | bytes 3145732
  4.6 13.1 %copy-start = (f32[16,128,128]{2,1,0:T(8,128)S(1)}, f32[16,128,128]{2,1,0:T(8,128)}, u32[]{:S(2)}) copy-start(f32[16,128,128]{2,1,0:T(8,128)} %get-tuple-element.7) | copy-start | bytes 3145732
  6.0 13.7 %copy-start.4 = (f32[262144]{0:T(1024)}, f32[262144]{0:T(1024)S(1)}, u32[]{:S(2)}) copy-start(f32[262144]{0:T(1024)S(1)} %scatter_custom_fusion) | copy-start | bytes 3145732
  7.9 12.5 %collective-permute-start = (f32[1,128,128]{2,1,0:T(8,128)S(1)}, f32[1,128,128]{2,1,0:T(8,128)S(1)}, u32[]{:S(2)}, u32[]{:S(2)}) collective-permute-start(f32[1,128,128]{2,1,0:T(8,128)S(1)} %get-tuple-element.24), channel_id=1, source_target_pairs={{1,0},{2,1},{3,2},{4,3},{5,4},{6,5},{7,6},{8,7},{9,8},{10,9},{11,1... | collective-permute-start | bytes 196616 | tf_op jit(solution)/shard_map/ppermute | solution.py:19
  15.8 10.4 %collective-permute-start.1 = (f32[1,128,128]{2,1,0:T(8,128)S(1)}, f32[1,128,128]{2,1,0:T(8,128)S(1)}, u32[]{:S(2)}, u32[]{:S(2)}) collective-permute-start(f32[1,128,128]{2,1,0:T(8,128)S(1)} %get-tuple-element.23), channel_id=1, source_target_pairs={{0,1},{1,2},{2,3},{3,4},{4,5},{5,6},{6,7},{7,8},{8,9},{9,10},{10,1... | collective-permute-start | bytes 196616 | tf_op jit(solution)/shard_map/ppermute | solution.py:18
  17.7 9.2 %copy-start.1 = (f32[16,128,128]{2,1,0:T(8,128)S(1)}, f32[16,128,128]{2,1,0:T(8,128)}, u32[]{:S(2)}) copy-start(f32[16,128,128]{2,1,0:T(8,128)} %get-tuple-element.8) | copy-start | bytes 3145732
  17.7 9.2 %copy-start.3 = (f32[1,16,128,128]{3,2,1,0:T(8,128)S(1)}, f32[1,16,128,128]{3,2,1,0:T(8,128)}, u32[]{:S(2)}) copy-start(f32[1,16,128,128]{3,2,1,0:T(8,128)} %param.7) | copy-start | bytes 3145732
  20.4 6.6 %copy-start.5 = (f32[262144]{0:T(1024)S(1)}, f32[262144]{0:T(1024)}, u32[]{:S(2)}) copy-start(f32[262144]{0:T(1024)} %copy-done.4) | copy-start | bytes 3145732
  29.1 7.1 %collective-permute-start.2 = (f32[1,128,128]{2,1,0:T(8,128)S(1)}, f32[1,128,128]{2,1,0:T(8,128)S(1)}, u32[]{:S(2)}, u32[]{:S(2)}) collective-permute-start(f32[1,128,128]{2,1,0:T(8,128)S(1)} %get-tuple-element.22), channel_id=1, source_target_pairs={{1,0},{2,1},{3,2},{4,3},{5,4},{6,5},{7,6},{8,7},{9,8},{10,9},{11,1... | collective-permute-start | bytes 196616 | tf_op jit(solution)/shard_map/ppermute | solution.py:19
  32.2 10.4 %collective-permute-start.3 = (f32[1,128,128]{2,1,0:T(8,128)S(1)}, f32[1,128,128]{2,1,0:T(8,128)S(1)}, u32[]{:S(2)}, u32[]{:S(2)}) collective-permute-start(f32[1,128,128]{2,1,0:T(8,128)S(1)} %get-tuple-element.21), channel_id=1, source_target_pairs={{0,1},{1,2},{2,3},{3,4},{4,5},{5,6},{6,7},{7,8},{8,9},{9,10},{10,1... | collective-permute-start | bytes 196616 | tf_op jit(solution)/shard_map/ppermute | solution.py:18
  36.2 7.2 %copy-start.10 = (f32[16,128,128]{2,1,0:T(8,128)S(1)}, f32[16,128,128]{2,1,0:T(8,128)}, u32[]{:S(2)}) copy-start(f32[16,128,128]{2,1,0:T(8,128)} %get-tuple-element.16) | copy-start | bytes 3145732
  43.3 5.7 %copy-start.16 = (f32[8,1,64,1,128]{4,3,2,1,0:T(1,128)S(1)}, f32[8,1,64,1,128]{4,3,2,1,0:T(1,128)}, u32[]{:S(2)}) copy-start(f32[8,1,64,1,128]{4,3,2,1,0:T(1,128)} %get-tuple-element.25) | copy-start | bytes 786436
  43.4 5.7 %copy-start.17 = (f32[8,1,64,1,128]{4,3,2,1,0:T(1,128)S(1)}, f32[8,1,64,1,128]{4,3,2,1,0:T(1,128)}, u32[]{:S(2)}) copy-start(f32[8,1,64,1,128]{4,3,2,1,0:T(1,128)} %get-tuple-element.26) | copy-start | bytes 786436
  43.4 5.7 %copy-start.18 = (f32[8,1,64,1,128]{4,3,2,1,0:T(1,128)S(1)}, f32[8,1,64,1,128]{4,3,2,1,0:T(1,128)}, u32[]{:S(2)}) copy-start(f32[8,1,64,1,128]{4,3,2,1,0:T(1,128)} %get-tuple-element.27) | copy-start | bytes 786436
  43.4 5.7 %copy-start.19 = (f32[8,1,64,1,128]{4,3,2,1,0:T(1,128)S(1)}, f32[8,1,64,1,128]{4,3,2,1,0:T(1,128)}, u32[]{:S(2)}) copy-start(f32[8,1,64,1,128]{4,3,2,1,0:T(1,128)} %get-tuple-element.28) | copy-start | bytes 786436
  44.6 5.3 %collective-permute-start.4 = (f32[1,128,128]{2,1,0:T(8,128)S(1)}, f32[1,128,128]{2,1,0:T(8,128)S(1)}, u32[]{:S(2)}, u32[]{:S(2)}) collective-permute-start(f32[1,128,128]{2,1,0:T(8,128)S(1)} %get-tuple-element.20), channel_id=1, source_target_pairs={{1,0},{2,1},{3,2},{4,3},{5,4},{6,5},{7,6},{8,7},{9,8},{10,9},{11,1... | collective-permute-start | bytes 196616 | tf_op jit(solution)/shard_map/ppermute | solution.py:19
  47.1 10.4 %collective-permute-start.5 = (f32[1,128,128]{2,1,0:T(8,128)S(1)}, f32[1,128,128]{2,1,0:T(8,128)S(1)}, u32[]{:S(2)}, u32[]{:S(2)}) collective-permute-start(f32[1,128,128]{2,1,0:T(8,128)S(1)} %get-tuple-element.19), channel_id=1, source_target_pairs={{0,1},{1,2},{2,3},{3,4},{4,5},{5,6},{6,7},{7,8},{8,9},{9,10},{10,1... | collective-permute-start | bytes 196616 | tf_op jit(solution)/shard_map/ppermute | solution.py:18
  58.3 6.8 %copy-start.12 = (f32[8,1,64,1,128]{4,3,2,1,0:T(1,128)S(1)}, f32[8,1,64,1,128]{4,3,2,1,0:T(1,128)}, u32[]{:S(2)}) copy-start(f32[8,1,64,1,128]{4,3,2,1,0:T(1,128)} %get-tuple-element.29) | copy-start | bytes 786436
  58.3 6.8 %copy-start.13 = (f32[8,1,64,1,128]{4,3,2,1,0:T(1,128)S(1)}, f32[8,1,64,1,128]{4,3,2,1,0:T(1,128)}, u32[]{:S(2)}) copy-start(f32[8,1,64,1,128]{4,3,2,1,0:T(1,128)} %get-tuple-element.30) | copy-start | bytes 786436
  58.3 6.8 %copy-start.14 = (f32[8,1,64,1,128]{4,3,2,1,0:T(1,128)S(1)}, f32[8,1,64,1,128]{4,3,2,1,0:T(1,128)}, u32[]{:S(2)}) copy-start(f32[8,1,64,1,128]{4,3,2,1,0:T(1,128)} %get-tuple-element.31) | copy-start | bytes 786436
  58.3 6.8 %copy-start.15 = (f32[8,1,64,1,128]{4,3,2,1,0:T(1,128)S(1)}, f32[8,1,64,1,128]{4,3,2,1,0:T(1,128)}, u32[]{:S(2)}) copy-start(f32[8,1,64,1,128]{4,3,2,1,0:T(1,128)} %get-tuple-element.32) | copy-start | bytes 786436
  60.5 4.7 %collective-permute-start.6 = (f32[1,128,128]{2,1,0:T(8,128)S(1)}, f32[1,128,128]{2,1,0:T(8,128)S(1)}, u32[]{:S(2)}, u32[]{:S(2)}) collective-permute-start(f32[1,128,128]{2,1,0:T(8,128)S(1)} %get-tuple-element.18), channel_id=1, source_target_pairs={{1,0},{2,1},{3,2},{4,3},{5,4},{6,5},{7,6},{8,7},{9,8},{10,9},{11,1... | collective-permute-start | bytes 196616 | tf_op jit(solution)/shard_map/ppermute | solution.py:19
  62.5 10.4 %collective-permute-start.7 = (f32[1,128,128]{2,1,0:T(8,128)S(1)}, f32[1,128,128]{2,1,0:T(8,128)S(1)}, u32[]{:S(2)}, u32[]{:S(2)}) collective-permute-start(f32[1,128,128]{2,1,0:T(8,128)S(1)} %get-tuple-element.17), channel_id=1, source_target_pairs={{0,1},{1,2},{2,3},{3,4},{4,5},{5,6},{6,7},{7,8},{8,9},{9,10},{10,1... | collective-permute-start | bytes 196616 | tf_op jit(solution)/shard_map/ppermute | solution.py:18
  65.2 8.8 %copy-start.6 = (f32[8,1,64,1,128]{4,2,0,3,1:T(8,128)}, f32[8,1,64,1,128]{4,2,0,3,1:T(8,128)S(1)}, u32[]{:S(2)}) copy-start(f32[8,1,64,1,128]{4,2,0,3,1:T(8,128)S(1)} %exponential_multiply_fusion) | copy-start | bytes 786436
  65.2 8.8 %copy-start.9 = (f32[16,128,128]{2,1,0:T(8,128)S(1)}, f32[16,128,128]{2,1,0:T(8,128)}, u32[]{:S(2)}) copy-start(f32[16,128,128]{2,1,0:T(8,128)} %get-tuple-element.12) | copy-start | bytes 3145732
  74.0 1.7 %copy-start.7 = (f32[8,1,64,1,128]{4,2,0,3,1:T(8,128)S(1)}, f32[8,1,64,1,128]{4,2,0,3,1:T(8,128)}, u32[]{:S(2)}) copy-start(f32[8,1,64,1,128]{4,2,0,3,1:T(8,128)} %copy-done.6) | copy-start | bytes 786436
  75.1 17.4 %copy-start.11 = (f32[8,1,64,1,128]{4,2,0,3,1:T(8,128)S(1)}, f32[8,1,64,1,128]{4,2,0,3,1:T(8,128)}, u32[]{:S(2)}) copy-start(f32[8,1,64,1,128]{4,2,0,3,1:T(8,128)} %get-tuple-element.9) | copy-start | bytes 786436
  75.8 15.5 %collective-permute-start.8 = (f32[520,128]{1,0:T(8,128)S(1)}, f32[520,128]{1,0:T(8,128)S(1)}, u32[]{:S(2)}, u32[]{:S(2)}) collective-permute-start(f32[520,128]{1,0:T(8,128)S(1)} %concatenate.63), channel_id=1, source_target_pairs={{16,0},{32,16},{48,32},{64,48},{80,64},{96,80},{112,96},{128,112},... | collective-permute-start | bytes 798728 | tf_op jit(solution)/shard_map/ppermute | solution.py:27
  92.5 10.1 %collective-permute-start.9 = (f32[520,128]{1,0:T(8,128)S(1)}, f32[520,128]{1,0:T(8,128)S(1)}, u32[]{:S(2)}, u32[]{:S(2)}) collective-permute-start(f32[520,128]{1,0:T(8,128)S(1)} %concatenate.64), channel_id=1, source_target_pairs={{32,0},{48,16},{64,32},{80,48},{96,64},{112,80},{128,96},{144,112}... | collective-permute-start | bytes 798728 | tf_op jit(solution)/shard_map/ppermute | solution.py:27
  103.9 15.3 %collective-permute-start.10 = (f32[520,128]{1,0:T(8,128)S(1)}, f32[520,128]{1,0:T(8,128)S(1)}, u32[]{:S(2)}, u32[]{:S(2)}) collective-permute-start(f32[520,128]{1,0:T(8,128)S(1)} %concatenate.65), channel_id=1, source_target_pairs={{64,0},{80,16},{96,32},{112,48},{128,64},{144,80},{160,96},{176,11... | collective-permute-start | bytes 798728 | tf_op jit(solution)/shard_map/ppermute | solution.py:27
  119.2 0.7 copy-start.20
  120.9 35.1 %copy-start.8 = (f32[8,1,64,1,128]{4,2,0,3,1:T(8,128)S(1)}, f32[8,1,64,1,128]{4,2,0,3,1:T(8,128)}, u32[]{:S(2)}) copy-start(f32[8,1,64,1,128]{4,2,0,3,1:T(8,128)} %copy-done.6) | copy-start | bytes 786436
  122.1 19.0 %collective-permute-start.11 = (f32[520,128]{1,0:T(8,128)S(1)}, f32[520,128]{1,0:T(8,128)S(1)}, u32[]{:S(2)}, u32[]{:S(2)}) collective-permute-start(f32[520,128]{1,0:T(8,128)S(1)} %concatenate.66), channel_id=1, source_target_pairs={{128,0},{144,16},{160,32},{176,48},{192,64},{208,80},{224,96},{240... | collective-permute-start | bytes 798728 | tf_op jit(solution)/shard_map/ppermute | solution.py:27
  141.0 0.7 copy-start.21
  143.8 12.2 %collective-permute-start.12 = (f32[520,128]{1,0:T(8,128)S(1)}, f32[520,128]{1,0:T(8,128)S(1)}, u32[]{:S(2)}, u32[]{:S(2)}) collective-permute-start(f32[520,128]{1,0:T(8,128)S(1)} %concatenate.67), channel_id=1, source_target_pairs={{256,0},{272,16},{288,32},{304,48},{320,64},{336,80},{352,96},{368... | collective-permute-start | bytes 798728 | tf_op jit(solution)/shard_map/ppermute | solution.py:27

commit v4 on v3

--- a/solution.py
+++ b/solution.py
@@ -85,8 +85,6 @@
     planes = adjoint.shape[0]
     across = adjoint.shape[1]
     depth = adjoint.shape[2]
-    cond_cell, cell_heat_drain = lookup_both(material, conductance, rock_heat_drain)
-    drain_amounts = cell_heat_drain + ventilation_heat_loss[0]
     local_cell = probe_cell_index - lax.axis_index("space") * (planes * across * depth)
     source = (
         jnp.zeros((planes * across * depth,), jnp.float32)
@@ -95,12 +93,36 @@
         .reshape(planes, across, depth)
     )
     seeded = adjoint + source
-    current = seeded
+    halo = FINE_STEPS
+    space_size = lax.axis_size("space")
+    up = [(i, i + 1) for i in range(space_size - 1)]
+    down = [(i + 1, i) for i in range(space_size - 1)]
+    material_f = material.astype(jnp.float32)
+    to_next = jnp.concatenate([seeded[-halo:], material_f[-halo:]], axis=0)
+    to_prev = jnp.concatenate([seeded[:halo], material_f[:halo]], axis=0)
+    from_prev = lax.ppermute(to_next, "space", up)
+    from_next = lax.ppermute(to_prev, "space", down)
+    current = jnp.concatenate([from_prev[:halo], seeded, from_next[:halo]], axis=0)
+    material_ext = jnp.concatenate(
+        [from_prev[halo:], material_f, from_next[halo:]], axis=0
+    ).astype(jnp.int32)
+    cond_ext, drain_ext = lookup_both(material_ext, conductance, rock_heat_drain)
+    extended = planes + 2 * halo
+    plane = lax.axis_index("space") * planes - halo + lax.iota(jnp.int32, extended)
+    inside = (plane >= 0) & (plane < space_size * planes)
+    cond_ext = jnp.where(inside[:, None, None], cond_ext, 0.0)
+    losses_ext = drain_ext + ventilation_heat_loss[0]
     for sweep_index in range(FINE_STEPS):
-        weighted = cond_cell * current
-        padded_x = padded_2(weighted, (("space", 0),), 1)
-        padded = jnp.pad(padded_x, ((0, 0), (1, 1), (1, 1)))
-        current = current + (neighbours(padded) - 6.0 * weighted) - drain_amounts * current
+        lo, hi = sweep_index, extended - sweep_index
+        weighted = cond_ext[lo:hi] * current
+        x_sides = weighted[2:] + weighted[:-2]
+        inner = weighted[1:-1]
+        padded = jnp.pad(inner, ((0, 0), (1, 1), (1, 1)))
+        y_sides = padded[:, 2:, 1:-1] + padded[:, :-2, 1:-1]
+        z_sides = padded[:, 1:-1, 2:] + padded[:, 1:-1, :-2]
+        kept = current[1:-1]
+        current = kept + ((x_sides + y_sides + z_sides) - 6.0 * inner) - losses_ext[lo + 1 : hi - 1] * kept
+    cell_heat_drain = drain_ext[halo : halo + planes]
     coarse_baseline = coarsen(cell_heat_drain)
     coarse_decay_rate = jnp.exp(-FINE_STEPS * (coarse_baseline + ventilation_heat_loss[0]))
     coarse_old = coarsen(adjoint)

time: 159 us -> 142 us (0.89)
  the two profiles are of different devices: /device:TPU:214 before, /device:TPU:19 now
where the time goes in v4:
time: 142 us
  waiting for transfers between devices  79.7 us (56%)
  starting transfers between devices  23.1 us (16%)
  other arithmetic  18.8 us (13%)
  local copies, waits for them, and re-layouts  11.2 us (8%)
  Pallas kernels  5.2 us (4%)
  between operations  3.71 us (3%)
    ppermute x5, waiting for transfers between devices, shifted(): lax.ppermute(value, axis, [(source, source + steps) for source in range(i...  59.4 us
    ppermute x1, waiting for transfers between devices, on_device(): from_prev = lax.ppermute(to_next, 'space', up)  11.3 us
    ppermute x1, starting transfers between devices, on_device(): from_prev = lax.ppermute(to_next, 'space', up)  11.2 us
    ppermute x5, starting transfers between devices, shifted(): lax.ppermute(value, axis, [(source, source + steps) for source in range(i...  9.99 us
    ppermute x1, waiting for transfers between devices, on_device(): from_next = lax.ppermute(to_prev, 'space', down)  9.01 us
    mul x4, other arithmetic, on_device(): weighted = cond_ext[lo:hi] * current  5.66 us
    pallas_call x1, Pallas kernels, lookup_both(): pl.pallas_call(_lookup_kernel, grid=(planes // block[0],), in_specs=[smem...  5.2 us
    slice x4, local copies, waits for them, and re-layouts, on_device(): gain = gain * arrived[rows, 0]  3.41 us
  transfers between devices with their start and end apart: 7, of which 7 were waited for; matrix products, arithmetic and copies ran while one was open for 3% of the time, Pallas kernels for 0%

profile of v4, /device:TPU:19, one launch (start us, length us, event | category | flops | bytes accessed | tf_op | source)
XLA Modules:
  0.0 141.7 jit_solution(14466508072093632880)
XLA Ops:
  0.0 1.4 convert_element_type.14
  1.4 2.0 %scatter_custom_fusion = f32[262144]{0:T(1024)} fusion(s32[64]{0:T(128)S(1)} %compare_select_fusion, f32[64]{0:T(128)} %bitcast.102, f32[]{:T(128)} %constant.17.clone.1), kind=kCustom, calls=%fused_computation.65 | custom fusion | flops 64 | bytes 1049088 | tf_op jit(solution)/shard_map/scatter-add | solution.py:92
  3.5 1.3 bitcast_add_fusion
  4.9 0.8 pad_maximum_fusion.1
  5.7 11.2 %collective-permute-start = (f32[8,128,128]{2,1,0:T(8,128)}, f32[8,128,128]{2,1,0:T(8,128)}, u32[]{:S(2)}, u32[]{:S(2)}) collective-permute-start(f32[8,128,128]{2,1,0:T(8,128)} %pad_maximum_fusion.1), channel_id=1, source_target_pairs={{0,1},{1,2},{2,3},{3,4},{4,5},{5,6},{6,7},{7,8},{8,9},{9,10},{10,1... | collective-permute-start | bytes 1572872 | tf_op jit(solution)/shard_map/ppermute | solution.py:103
  16.9 0.8 pad_maximum_fusion.2
  17.8 1.9 %collective-permute-start.1 = (f32[8,128,128]{2,1,0:T(8,128)}, f32[8,128,128]{2,1,0:T(8,128)}, u32[]{:S(2)}, u32[]{:S(2)}) collective-permute-start(f32[8,128,128]{2,1,0:T(8,128)} %pad_maximum_fusion.2), channel_id=1, source_target_pairs={{1,0},{2,1},{3,2},{4,3},{5,4},{6,5},{7,6},{8,7},{9,8},{10,9},{11,1... | collective-permute-start | bytes 1572872 | tf_op jit(solution)/shard_map/ppermute | solution.py:104
  20.4 1.8 %fusion.53 = (f32[8,1,64,1,128]{4,3,2,1,0:T(1,128)S(1)}, f32[8,1,64,1,128]{4,3,2,1,0:T(1,128)}, f32[8,1,64,1,128]{4,3,2,1,0:T(1,128)}, f32[8,1,64,1,128]{4,3,2,1,0:T(1,128)}) fusion(f32[8,2,64,2,128]{4,3,2,1,0:T(2,128)S(1)} %bitcast.78), kind=kLoop, calls=%fused_computation.107 | loop fusion | bytes 2097152 | tf_op jit(solution)/shard_map/slice | solution.py:32
  22.2 11.3 %collective-permute-done = f32[8,128,128]{2,1,0:T(8,128)} collective-permute-done((f32[8,128,128]{2,1,0:T(8,128)}, f32[8,128,128]{2,1,0:T(8,128)}, u32[]{:S(2)}, u32[]{:S(2)}) %collective-permute-start) | collective-permute-done | bytes 524320 | tf_op jit(solution)/shard_map/ppermute | solution.py:103
  33.4 1.1 fusion.54
  34.5 9.0 %collective-permute-done.1 = f32[8,128,128]{2,1,0:T(8,128)} collective-permute-done((f32[8,128,128]{2,1,0:T(8,128)}, f32[8,128,128]{2,1,0:T(8,128)}, u32[]{:S(2)}, u32[]{:S(2)}) %collective-permute-start.1) | collective-permute-done | bytes 524320 | tf_op jit(solution)/shard_map/ppermute | solution.py:104
  43.5 1.1 fusion.55
  44.6 1.4 maximum_convert_fusion.material_ref
  45.9 5.2 %shard_map.73 = (f32[24,128,128]{2,1,0:T(8,128)}, f32[24,128,128]{2,1,0:T(8,128)}) custom-call(f32[8]{0:T(128)} %cond_table.1, f32[8]{0:T(128)} %drain_table.1, s32[24,128,128]{2,1,0:T(8,128)} %maximum_convert_fusion.material_ref), custom_call_target="tpu_custom_call" | custom-call | tf_op jit(solution)/shard_map/pallas_call | solution.py:66
  51.1 1.7 %fusion.46 = (f32[24,128,128]{2,1,0:T(8,128)S(1)}, f32[24,128,128]{2,1,0:T(8,128)S(1)}, f32[24,128,128]{2,1,0:T(8,128)S(1)}) fusion(f32[4,128,128]{2,1,0:T(8,128)S(1)} %get-tuple-element.34, f32[16,128,128]{2,1,0:T(8,128)S(1)} %bitcast_add_fusion, f32[4,128,128]{2,1,0:T(8,128)S(1)} %get-tuple-element.32, f32[24,128,128]{2,1,0:T(8,128)} %get-tuple-element.8, ...), kind=kLoop, calls=%fused_computation.103 | loop fusion | flops 1572864 | bytes 7864344 | tf_op jit(solution)/shard_map/mul | solution.py:117
  52.9 0.1 slice.295
  53.0 1.3 copy-done
  54.4 0.1 broadcast_add_fusion
  54.5 1.4 slice_multiply_fusion
  55.9 0.1 slice.301
  56.0 1.3 slice_multiply_fusion.2
  57.3 0.1 slice.307
  57.4 1.2 slice_multiply_fusion.4
  58.7 0.1 slice.313
  58.8 1.1 fusion.50
  60.0 0.1 exponential_multiply_fusion
  60.2 0.4 broadcast_in_dim.44
  60.6 0.9 fusion.27
  61.5 0.6 fusion.39
  62.1 1.9 %collective-permute-start.2 = (f32[520,128]{1,0:T(8,128)S(1)}, f32[520,128]{1,0:T(8,128)S(1)}, u32[]{:S(2)}, u32[]{:S(2)}) collective-permute-start(f32[520,128]{1,0:T(8,128)S(1)} %concatenate.31), channel_id=1, source_target_pairs={{16,0},{32,16},{48,32},{64,48},{80,64},{96,80},{112,96},{128,112},... | collective-permute-start | bytes 798728 | tf_op jit(solution)/shard_map/ppermute | solution.py:27
  64.1 5.7 %collective-permute-done.2 = f32[520,128]{1,0:T(8,128)S(1)} collective-permute-done((f32[520,128]{1,0:T(8,128)S(1)}, f32[520,128]{1,0:T(8,128)S(1)}, u32[]{:S(2)}, u32[]{:S(2)}) %collective-permute-start.2) | collective-permute-done | bytes 266272 | tf_op jit(solution)/shard_map/ppermute | solution.py:27
  69.8 0.5 slice.320
  71.0 2.7 %collective-permute-start.3 = (f32[520,128]{1,0:T(8,128)S(1)}, f32[520,128]{1,0:T(8,128)S(1)}, u32[]{:S(2)}, u32[]{:S(2)}) collective-permute-start(f32[520,128]{1,0:T(8,128)S(1)} %concatenate.32), channel_id=1, source_target_pairs={{32,0},{48,16},{64,32},{80,48},{96,64},{112,80},{128,96},{144,112}... | collective-permute-start | bytes 798728 | tf_op jit(solution)/shard_map/ppermute | solution.py:27
  73.8 13.1 %collective-permute-done.3 = f32[520,128]{1,0:T(8,128)S(1)} collective-permute-done((f32[520,128]{1,0:T(8,128)S(1)}, f32[520,128]{1,0:T(8,128)S(1)}, u32[]{:S(2)}, u32[]{:S(2)}) %collective-permute-start.3) | collective-permute-done | bytes 266272 | tf_op jit(solution)/shard_map/ppermute | solution.py:27
  86.9 0.5 slice.322
  88.2 2.1 %collective-permute-start.4 = (f32[520,128]{1,0:T(8,128)S(1)}, f32[520,128]{1,0:T(8,128)}, u32[]{:S(2)}, u32[]{:S(2)}) collective-permute-start(f32[520,128]{1,0:T(8,128)S(1)} %concatenate.33), channel_id=1, source_target_pairs={{64,0},{80,16},{96,32},{112,48},{128,64},{144,80},{160,96},{176,11... | collective-permute-start | bytes 798728 | tf_op jit(solution)/shard_map/ppermute | solution.py:27
  90.3 7.9 %collective-permute-done.4 = f32[520,128]{1,0:T(8,128)} collective-permute-done((f32[520,128]{1,0:T(8,128)S(1)}, f32[520,128]{1,0:T(8,128)}, u32[]{:S(2)}, u32[]{:S(2)}) %collective-permute-start.4) | collective-permute-done | bytes 266272 | tf_op jit(solution)/shard_map/ppermute | solution.py:27
  98.1 1.2 slice.324
  100.1 1.0 fusion.58
  101.1 2.0 %collective-permute-start.5 = (f32[520,128]{1,0:T(8,128)S(1)}, f32[520,128]{1,0:T(8,128)}, u32[]{:S(2)}, u32[]{:S(2)}) collective-permute-start(f32[520,128]{1,0:T(8,128)S(1)} %concatenate.34), channel_id=1, source_target_pairs={{128,0},{144,16},{160,32},{176,48},{192,64},{208,80},{224,96},{240... | collective-permute-start | bytes 798728 | tf_op jit(solution)/shard_map/ppermute | solution.py:27
  103.1 15.0 %collective-permute-done.5 = f32[520,128]{1,0:T(8,128)} collective-permute-done((f32[520,128]{1,0:T(8,128)S(1)}, f32[520,128]{1,0:T(8,128)}, u32[]{:S(2)}, u32[]{:S(2)}) %collective-permute-start.5) | collective-permute-done | bytes 266272 | tf_op jit(solution)/shard_map/ppermute | solution.py:27
  118.0 1.2 slice.326
  119.9 1.0 fusion.59
  120.9 1.3 collective-permute-start.6
  122.2 17.7 %collective-permute-done.6 = f32[520,128]{1,0:T(8,128)S(1)} collective-permute-done((f32[520,128]{1,0:T(8,128)S(1)}, f32[520,128]{1,0:T(8,128)S(1)}, u32[]{:S(2)}, u32[]{:S(2)}) %collective-permute-start.6) | collective-permute-done | bytes 266272 | tf_op jit(solution)/shard_map/ppermute | solution.py:27
  139.9 0.2 fusion.37
  140.2 0.4 broadcast_in_dim.46
  140.6 1.1 add_bitcast_fusion
  (30 shorter events, 0.7 us)
Async XLA Ops:
  0.0 1.4 copy-start.5
  0.0 3.5 %copy-start.1 = (f32[1,16,128,128]{3,2,1,0:T(8,128)S(1)}, f32[1,16,128,128]{3,2,1,0:T(8,128)}, u32[]{:S(2)}) copy-start(f32[1,16,128,128]{3,2,1,0:T(8,128)} %param.7) | copy-start | bytes 3145732
  5.7 27.7 %collective-permute-start = (f32[8,128,128]{2,1,0:T(8,128)}, f32[8,128,128]{2,1,0:T(8,128)}, u32[]{:S(2)}, u32[]{:S(2)}) collective-permute-start(f32[8,128,128]{2,1,0:T(8,128)} %pad_maximum_fusion.1), channel_id=1, source_target_pairs={{0,1},{1,2},{2,3},{3,4},{4,5},{5,6},{6,7},{7,8},{8,9},{9,10},{10,1... | collective-permute-start | bytes 1572872 | tf_op jit(solution)/shard_map/ppermute | solution.py:103
  17.8 25.7 %collective-permute-start.1 = (f32[8,128,128]{2,1,0:T(8,128)}, f32[8,128,128]{2,1,0:T(8,128)}, u32[]{:S(2)}, u32[]{:S(2)}) collective-permute-start(f32[8,128,128]{2,1,0:T(8,128)} %pad_maximum_fusion.2), channel_id=1, source_target_pairs={{1,0},{2,1},{3,2},{4,3},{5,4},{6,5},{7,6},{8,7},{9,8},{10,9},{11,1... | collective-permute-start | bytes 1572872 | tf_op jit(solution)/shard_map/ppermute | solution.py:104
  52.9 1.4 copy-start
  58.8 1.2 copy-start.2
  58.8 1.2 copy-start.3
  58.8 1.2 copy-start.4
  62.1 7.6 %collective-permute-start.2 = (f32[520,128]{1,0:T(8,128)S(1)}, f32[520,128]{1,0:T(8,128)S(1)}, u32[]{:S(2)}, u32[]{:S(2)}) collective-permute-start(f32[520,128]{1,0:T(8,128)S(1)} %concatenate.31), channel_id=1, source_target_pairs={{16,0},{32,16},{48,32},{64,48},{80,64},{96,80},{112,96},{128,112},... | collective-permute-start | bytes 798728 | tf_op jit(solution)/shard_map/ppermute | solution.py:27
  71.0 15.9 %collective-permute-start.3 = (f32[520,128]{1,0:T(8,128)S(1)}, f32[520,128]{1,0:T(8,128)S(1)}, u32[]{:S(2)}, u32[]{:S(2)}) collective-permute-start(f32[520,128]{1,0:T(8,128)S(1)} %concatenate.32), channel_id=1, source_target_pairs={{32,0},{48,16},{64,32},{80,48},{96,64},{112,80},{128,96},{144,112}... | collective-permute-start | bytes 798728 | tf_op jit(solution)/shard_map/ppermute | solution.py:27
  88.2 10.0 %collective-permute-start.4 = (f32[520,128]{1,0:T(8,128)S(1)}, f32[520,128]{1,0:T(8,128)}, u32[]{:S(2)}, u32[]{:S(2)}) collective-permute-start(f32[520,128]{1,0:T(8,128)S(1)} %concatenate.33), channel_id=1, source_target_pairs={{64,0},{80,16},{96,32},{112,48},{128,64},{144,80},{160,96},{176,11... | collective-permute-start | bytes 798728 | tf_op jit(solution)/shard_map/ppermute | solution.py:27
  101.1 17.0 %collective-permute-start.5 = (f32[520,128]{1,0:T(8,128)S(1)}, f32[520,128]{1,0:T(8,128)}, u32[]{:S(2)}, u32[]{:S(2)}) collective-permute-start(f32[520,128]{1,0:T(8,128)S(1)} %concatenate.34), channel_id=1, source_target_pairs={{128,0},{144,16},{160,32},{176,48},{192,64},{208,80},{224,96},{240... | collective-permute-start | bytes 798728 | tf_op jit(solution)/shard_map/ppermute | solution.py:27
  120.9 19.0 %collective-permute-start.6 = (f32[520,128]{1,0:T(8,128)S(1)}, f32[520,128]{1,0:T(8,128)S(1)}, u32[]{:S(2)}, u32[]{:S(2)}) collective-permute-start(f32[520,128]{1,0:T(8,128)S(1)} %concatenate.35), channel_id=1, source_target_pairs={{256,0},{272,16},{288,32},{304,48},{320,64},{336,80},{352,96},{368... | collective-permute-start | bytes 798728 | tf_op jit(solution)/shard_map/ppermute | solution.py:27

commit v5 on v4

--- a/solution.py
+++ b/solution.py
@@ -70,6 +70,59 @@
         out_specs=[spec, spec],
         out_shape=[out, out],
     )(conductance, rock_heat_drain, material)
+
+
+def pack(field, scalar):
+    return jnp.concatenate([field, jnp.broadcast_to(scalar, (8, field.shape[-1]))], axis=0)
+
+
+def grouped_scan(total, gain, per_cell, group):
+    tm_size = lax.axis_size("tm")
+    member = lax.axis_index("tm") % group
+    rows = total.shape[0]
+    block_b, block_e = total, gain
+    suffix_b, suffix_e, suffix_p = total, gain, per_cell
+    power = per_cell
+    bit = 1
+    while bit < group:
+        pairs = [(i, i ^ bit) for i in range(tm_size)]
+        arrived = lax.ppermute(pack(block_b, block_e), "tm", pairs)
+        other_b, other_e = arrived[:rows], arrived[rows, 0]
+        above = (member & bit) == 0
+        suffix_b = jnp.where(above, suffix_b + (suffix_p * suffix_e) * other_b, suffix_b)
+        suffix_p = jnp.where(above, suffix_p * power, suffix_p)
+        suffix_e = jnp.where(above, suffix_e * other_e, suffix_e)
+        block_b = jnp.where(
+            above, block_b + (power * block_e) * other_b, other_b + (power * other_e) * block_b
+        )
+        block_e = block_e * other_e
+        power = power * power
+        bit *= 2
+    part = rows // group
+    chain_b = lax.dynamic_slice_in_dim(block_b, member * part, part, 0)
+    chain_p = lax.dynamic_slice_in_dim(power, member * part, part, 0)
+    pairs = [(i + group, i) for i in range(tm_size - group)]
+    arrived = lax.ppermute(pack(chain_b, block_e), "tm", pairs)
+    chain_b, chain_e = arrived[:part], arrived[part, 0]
+    distance = group
+    while distance < tm_size:
+        pairs = [(i + distance, i) for i in range(tm_size - distance)]
+        arrived = lax.ppermute(pack(chain_b, chain_e), "tm", pairs)
+        chain_b = chain_b + (chain_p * chain_e) * arrived[:part]
+        chain_e = chain_e * arrived[part, 0]
+        chain_p = chain_p * chain_p
+        distance *= 2
+    piece = chain_b
+    bit = 1
+    while bit < group:
+        pairs = [(i, i ^ bit) for i in range(tm_size)]
+        other = lax.ppermute(piece, "tm", pairs)
+        low = (member & bit) == 0
+        piece = jnp.where(
+            low, jnp.concatenate([piece, other], axis=0), jnp.concatenate([other, piece], axis=0)
+        )
+        bit *= 2
+    return suffix_b + (suffix_p * suffix_e) * piece
 
 
 def on_device(
@@ -135,18 +188,21 @@
     top = coarse_decay_rate * coarse_old + reduced
     total = jnp.where(is_last, top, reduced)
     shape = total.shape
-    rows = total.size // shape[-1]
-    power = per_cell
-    distance = 1
-    while distance < tm_size:
-        packed = jnp.concatenate(
-            [total.reshape(rows, shape[-1]), jnp.broadcast_to(gain, (8, shape[-1]))], axis=0
-        )
-        arrived = shifted(packed, "tm", -distance)
-        total = total + (power * gain) * arrived[:rows].reshape(shape)
-        gain = gain * arrived[rows, 0]
-        power = power * power
-        distance *= 2
+    width = shape[-1]
+    rows = total.size // width
+    group = 4
+    if tm_size % group == 0 and rows % group == 0 and tm_size > group:
+        total = grouped_scan(total.reshape(rows, width), gain, per_cell.reshape(rows, width), group)
+        total = total.reshape(shape)
+    else:
+        power = per_cell
+        distance = 1
+        while distance < tm_size:
+            arrived = shifted(pack(total.reshape(rows, width), gain), "tm", -distance)
+            total = total + (power * gain) * arrived[:rows].reshape(shape)
+            gain = gain * arrived[rows, 0]
+            power = power * power
+            distance *= 2
     decayed = jnp.where(is_last, coarse_decay_rate * coarse_old, total - reduced)
     adjoint_new = refine(decayed) + correction
     return adjoint_new[None]

time: 142 us -> 145 us (1.021)
  the two profiles are of different devices: /device:TPU:19 before, /device:TPU:30 now
where the time goes in v5:
time: 145 us; the launch traced here: 144 us
  waiting for transfers between devices  58.3 us (40%)
  starting transfers between devices  46.3 us (32%)
  other arithmetic  19.3 us (13%)
  local copies, waits for them, and re-layouts  10.3 us (7%)
  Pallas kernels  5.2 us (4%)
  between operations  4.93 us (3%)
    ppermute x3, waiting for transfers between devices, grouped_scan(): arrived = lax.ppermute(pack(chain_b, chain_e), 'tm', pairs)  20.8 us
    ppermute x2, starting transfers between devices, grouped_scan(): arrived = lax.ppermute(pack(block_b, block_e), 'tm', pairs)  20.6 us
    ppermute x2, waiting for transfers between devices, grouped_scan(): arrived = lax.ppermute(pack(block_b, block_e), 'tm', pairs)  17.4 us
    ppermute x1, starting transfers between devices, on_device(): from_next = lax.ppermute(to_prev, 'space', down)  10.6 us
    ppermute x2, waiting for transfers between devices, grouped_scan(): other = lax.ppermute(piece, 'tm', pairs)  8.97 us
    mul x4, other arithmetic, on_device(): weighted = cond_ext[lo:hi] * current  5.66 us
    ppermute x2, starting transfers between devices, grouped_scan(): other = lax.ppermute(piece, 'tm', pairs)  5.64 us
    pallas_call x1, Pallas kernels, lookup_both(): pl.pallas_call(_lookup_kernel, grid=(planes // block[0],), in_specs=[smem...  5.2 us
  transfers between devices with their start and end apart: 10, of which 10 were waited for; matrix products, arithmetic and copies ran while one was open for 3% of the time, Pallas kernels for 0%

profile of v5, /device:TPU:30, one launch (start us, length us, event | category | flops | bytes accessed | tf_op | source)
XLA Modules:
  0.0 144.3 jit_solution(1288516884465524240)
XLA Ops:
  0.0 1.4 convert_element_type.14
  1.4 2.0 %scatter_custom_fusion = f32[262144]{0:T(1024)} fusion(s32[64]{0:T(128)S(1)} %compare_select_fusion, f32[64]{0:T(128)} %bitcast.82, f32[]{:T(128)} %constant.24.clone.1), kind=kCustom, calls=%fused_computation.65 | custom fusion | flops 64 | bytes 1049088 | tf_op jit(solution)/shard_map/scatter-add | solution.py:145
  3.5 1.3 bitcast_add_fusion
  4.9 0.8 pad_maximum_fusion.1
  5.7 1.9 %collective-permute-start = (f32[8,128,128]{2,1,0:T(8,128)}, f32[8,128,128]{2,1,0:T(8,128)}, u32[]{:S(2)}, u32[]{:S(2)}) collective-permute-start(f32[8,128,128]{2,1,0:T(8,128)} %pad_maximum_fusion.1), channel_id=1, source_target_pairs={{0,1},{1,2},{2,3},{3,4},{4,5},{5,6},{6,7},{7,8},{8,9},{9,10},{10,1... | collective-permute-start | bytes 1572872 | tf_op jit(solution)/shard_map/ppermute | solution.py:156
  7.7 0.8 pad_maximum_fusion.2
  8.5 10.6 %collective-permute-start.1 = (f32[8,128,128]{2,1,0:T(8,128)}, f32[8,128,128]{2,1,0:T(8,128)}, u32[]{:S(2)}, u32[]{:S(2)}) collective-permute-start(f32[8,128,128]{2,1,0:T(8,128)} %pad_maximum_fusion.2), channel_id=1, source_target_pairs={{1,0},{2,1},{3,2},{4,3},{5,4},{6,5},{7,6},{8,7},{9,8},{10,9},{11,1... | collective-permute-start | bytes 1572872 | tf_op jit(solution)/shard_map/ppermute | solution.py:157
  19.8 1.8 %fusion.51 = (f32[8,1,64,1,128]{4,3,2,1,0:T(1,128)S(1)}, f32[8,1,64,1,128]{4,3,2,1,0:T(1,128)}, f32[8,1,64,1,128]{4,3,2,1,0:T(1,128)}, f32[8,1,64,1,128]{4,3,2,1,0:T(1,128)}) fusion(f32[8,2,64,2,128]{4,3,2,1,0:T(2,128)S(1)} %bitcast.62), kind=kLoop, calls=%fused_computation.107 | loop fusion | bytes 2097152 | tf_op jit(solution)/shard_map/slice | solution.py:32
  21.6 2.0 %collective-permute-done = f32[8,128,128]{2,1,0:T(8,128)} collective-permute-done((f32[8,128,128]{2,1,0:T(8,128)}, f32[8,128,128]{2,1,0:T(8,128)}, u32[]{:S(2)}, u32[]{:S(2)}) %collective-permute-start) | collective-permute-done | bytes 524320 | tf_op jit(solution)/shard_map/ppermute | solution.py:156
  23.6 1.1 fusion.52
  24.7 4.1 %collective-permute-done.1 = f32[8,128,128]{2,1,0:T(8,128)} collective-permute-done((f32[8,128,128]{2,1,0:T(8,128)}, f32[8,128,128]{2,1,0:T(8,128)}, u32[]{:S(2)}, u32[]{:S(2)}) %collective-permute-start.1) | collective-permute-done | bytes 524320 | tf_op jit(solution)/shard_map/ppermute | solution.py:157
  28.8 1.1 fusion.53
  29.8 1.4 maximum_convert_fusion.material_ref
  31.2 5.2 %shard_map.73 = (f32[24,128,128]{2,1,0:T(8,128)}, f32[24,128,128]{2,1,0:T(8,128)}) custom-call(f32[8]{0:T(128)} %cond_table.1, f32[8]{0:T(128)} %drain_table.1, s32[24,128,128]{2,1,0:T(8,128)} %maximum_convert_fusion.material_ref), custom_call_target="tpu_custom_call" | custom-call | tf_op jit(solution)/shard_map/pallas_call | solution.py:66
  36.4 1.7 %fusion.44 = (f32[24,128,128]{2,1,0:T(8,128)S(1)}, f32[24,128,128]{2,1,0:T(8,128)S(1)}, f32[24,128,128]{2,1,0:T(8,128)S(1)}) fusion(f32[4,128,128]{2,1,0:T(8,128)S(1)} %get-tuple-element.34, f32[16,128,128]{2,1,0:T(8,128)S(1)} %bitcast_add_fusion, f32[4,128,128]{2,1,0:T(8,128)S(1)} %get-tuple-element.32, f32[24,128,128]{2,1,0:T(8,128)} %get-tuple-element.8, ...), kind=kLoop, calls=%fused_computation.103 | loop fusion | flops 1572864 | bytes 7864344 | tf_op jit(solution)/shard_map/mul | solution.py:170
  38.3 1.3 copy-done
  39.8 1.4 slice_multiply_fusion
  41.3 1.3 slice_multiply_fusion.2
  42.7 1.2 slice_multiply_fusion.4
  44.1 0.9 fusion.48
  45.7 0.9 fusion.27
  46.6 0.6 fusion.35
  47.3 14.5 %collective-permute-start.2 = (f32[520,128]{1,0:T(8,128)S(1)}, f32[520,128]{1,0:T(8,128)S(1)}, u32[]{:S(2)}, u32[]{:S(2)}) collective-permute-start(f32[520,128]{1,0:T(8,128)S(1)} %concatenate.46), channel_id=1, source_target_pairs={{0,16},{16,0},{32,48},{48,32},{64,80},{80,64},{96,112},{112,96},{1... | collective-permute-start | bytes 798728 | tf_op jit(solution)/shard_map/ppermute | solution.py:89
  61.8 5.8 %collective-permute-done.2 = f32[520,128]{1,0:T(8,128)S(1)} collective-permute-done((f32[520,128]{1,0:T(8,128)S(1)}, f32[520,128]{1,0:T(8,128)S(1)}, u32[]{:S(2)}, u32[]{:S(2)}) %collective-permute-start.2) | collective-permute-done | bytes 266272 | tf_op jit(solution)/shard_map/ppermute | solution.py:89
  67.6 0.5 slice.329
  68.8 0.7 bitcast_multiply_fusion.1
  69.5 6.1 %collective-permute-start.3 = (f32[520,128]{1,0:T(8,128)S(1)}, f32[520,128]{1,0:T(8,128)S(1)}, u32[]{:S(2)}, u32[]{:S(2)}) collective-permute-start(f32[520,128]{1,0:T(8,128)S(1)} %concatenate.47), channel_id=1, source_target_pairs={{0,32},{16,48},{32,0},{48,16},{64,96},{80,112},{96,64},{112,80},{1... | collective-permute-start | bytes 798728 | tf_op jit(solution)/shard_map/ppermute | solution.py:89
  75.7 11.6 %collective-permute-done.3 = f32[520,128]{1,0:T(8,128)S(1)} collective-permute-done((f32[520,128]{1,0:T(8,128)S(1)}, f32[520,128]{1,0:T(8,128)S(1)}, u32[]{:S(2)}, u32[]{:S(2)}) %collective-permute-start.3) | collective-permute-done | bytes 266272 | tf_op jit(solution)/shard_map/ppermute | solution.py:89
  87.3 0.5 slice.331
  88.5 0.7 add_select_fusion.2
  89.2 2.4 %collective-permute-start.4 = (f32[136,128]{1,0:T(8,128)S(1)}, f32[136,128]{1,0:T(8,128)S(1)}, u32[]{:S(2)}, u32[]{:S(2)}) collective-permute-start(f32[136,128]{1,0:T(8,128)S(1)} %concatenate.48), channel_id=1, source_target_pairs={{64,0},{80,16},{96,32},{112,48},{128,64},{144,80},{160,96},{176,11... | collective-permute-start | bytes 208904 | tf_op jit(solution)/shard_map/ppermute | solution.py:105
  91.5 5.0 %collective-permute-done.4 = f32[136,128]{1,0:T(8,128)S(1)} collective-permute-done((f32[136,128]{1,0:T(8,128)S(1)}, f32[136,128]{1,0:T(8,128)S(1)}, u32[]{:S(2)}, u32[]{:S(2)}) %collective-permute-start.4) | collective-permute-done | bytes 69664 | tf_op jit(solution)/shard_map/ppermute | solution.py:105
  96.6 0.5 slice.333
  97.1 0.7 broadcast_select_fusion.1
  97.8 1.9 %collective-permute-start.5 = (f32[136,128]{1,0:T(8,128)S(1)}, f32[136,128]{1,0:T(8,128)S(1)}, u32[]{:S(2)}, u32[]{:S(2)}) collective-permute-start(f32[136,128]{1,0:T(8,128)S(1)} %broadcast_select_fusion.1), channel_id=1, source_target_pairs={{64,0},{80,16},{96,32},{112,48},{128,64},{144,80},{160,96},{176,11... | collective-permute-start | bytes 208904 | tf_op jit(solution)/shard_map/ppermute | solution.py:110
  99.7 5.5 %collective-permute-done.5 = f32[136,128]{1,0:T(8,128)S(1)} collective-permute-done((f32[136,128]{1,0:T(8,128)S(1)}, f32[136,128]{1,0:T(8,128)S(1)}, u32[]{:S(2)}, u32[]{:S(2)}) %collective-permute-start.5) | collective-permute-done | bytes 69664 | tf_op jit(solution)/shard_map/ppermute | solution.py:110
  105.2 0.6 slice.335
  107.0 0.6 fusion.43
  107.6 1.9 %collective-permute-start.6 = (f32[136,128]{1,0:T(8,128)S(1)}, f32[136,128]{1,0:T(8,128)S(1)}, u32[]{:S(2)}, u32[]{:S(2)}) collective-permute-start(f32[136,128]{1,0:T(8,128)S(1)} %concatenate.50), channel_id=1, source_target_pairs={{128,0},{144,16},{160,32},{176,48},{192,64},{208,80},{224,96},{240... | collective-permute-start | bytes 208904 | tf_op jit(solution)/shard_map/ppermute | solution.py:110
  109.6 6.5 %collective-permute-done.6 = f32[136,128]{1,0:T(8,128)S(1)} collective-permute-done((f32[136,128]{1,0:T(8,128)S(1)}, f32[136,128]{1,0:T(8,128)S(1)}, u32[]{:S(2)}, u32[]{:S(2)}) %collective-permute-start.6) | collective-permute-done | bytes 69664 | tf_op jit(solution)/shard_map/ppermute | solution.py:110
  116.0 0.5 slice.337
  117.2 1.3 collective-permute-start.7
  118.5 8.8 %collective-permute-done.7 = f32[136,128]{1,0:T(8,128)S(1)} collective-permute-done((f32[136,128]{1,0:T(8,128)S(1)}, f32[136,128]{1,0:T(8,128)S(1)}, u32[]{:S(2)}, u32[]{:S(2)}) %collective-permute-start.7) | collective-permute-done | bytes 69664 | tf_op jit(solution)/shard_map/ppermute | solution.py:110
  127.3 1.9 %collective-permute-start.8 = (f32[128,128]{1,0:T(8,128)S(1)}, f32[128,128]{1,0:T(8,128)S(1)}, u32[]{:S(2)}, u32[]{:S(2)}) collective-permute-start(f32[128,128]{1,0:T(8,128)S(1)} %fusion.41), channel_id=1, source_target_pairs={{0,16},{16,0},{32,48},{48,32},{64,80},{80,64},{96,112},{112,96},{1... | collective-permute-start | bytes 196616 | tf_op jit(solution)/shard_map/ppermute | solution.py:119
  129.2 4.3 %collective-permute-done.8 = f32[128,128]{1,0:T(8,128)S(1)} collective-permute-done((f32[128,128]{1,0:T(8,128)S(1)}, f32[128,128]{1,0:T(8,128)S(1)}, u32[]{:S(2)}, u32[]{:S(2)}) %collective-permute-start.8) | collective-permute-done | bytes 65568 | tf_op jit(solution)/shard_map/ppermute | solution.py:119
  133.5 3.7 %collective-permute-start.9 = (f32[256,128]{1,0:T(8,128)S(1)}, f32[256,128]{1,0:T(8,128)S(1)}, u32[]{:S(2)}, u32[]{:S(2)}) collective-permute-start(f32[256,128]{1,0:T(8,128)S(1)} %maximum_select_fusion.1), channel_id=1, source_target_pairs={{0,32},{16,48},{32,0},{48,16},{64,96},{80,112},{96,64},{112,80},{1... | collective-permute-start | bytes 393224 | tf_op jit(solution)/shard_map/ppermute | solution.py:119
  137.9 4.7 %collective-permute-done.9 = f32[256,128]{1,0:T(8,128)S(1)} collective-permute-done((f32[256,128]{1,0:T(8,128)S(1)}, f32[256,128]{1,0:T(8,128)S(1)}, u32[]{:S(2)}, u32[]{:S(2)}) %collective-permute-start.9) | collective-permute-done | bytes 131104 | tf_op jit(solution)/shard_map/ppermute | solution.py:119
  143.2 1.1 add_bitcast_fusion
  (41 shorter events, 2.2 us)
Async XLA Ops:
  0.0 1.4 copy-start.6
  0.0 3.5 %copy-start.1 = (f32[1,16,128,128]{3,2,1,0:T(8,128)S(1)}, f32[1,16,128,128]{3,2,1,0:T(8,128)}, u32[]{:S(2)}) copy-start(f32[1,16,128,128]{3,2,1,0:T(8,128)} %param.7) | copy-start | bytes 3145732
  5.7 17.9 %collective-permute-start = (f32[8,128,128]{2,1,0:T(8,128)}, f32[8,128,128]{2,1,0:T(8,128)}, u32[]{:S(2)}, u32[]{:S(2)}) collective-permute-start(f32[8,128,128]{2,1,0:T(8,128)} %pad_maximum_fusion.1), channel_id=1, source_target_pairs={{0,1},{1,2},{2,3},{3,4},{4,5},{5,6},{6,7},{7,8},{8,9},{9,10},{10,1... | collective-permute-start | bytes 1572872 | tf_op jit(solution)/shard_map/ppermute | solution.py:156
  8.5 20.3 %collective-permute-start.1 = (f32[8,128,128]{2,1,0:T(8,128)}, f32[8,128,128]{2,1,0:T(8,128)}, u32[]{:S(2)}, u32[]{:S(2)}) collective-permute-start(f32[8,128,128]{2,1,0:T(8,128)} %pad_maximum_fusion.2), channel_id=1, source_target_pairs={{1,0},{2,1},{3,2},{4,3},{5,4},{6,5},{7,6},{8,7},{9,8},{10,9},{11,1... | collective-permute-start | bytes 1572872 | tf_op jit(solution)/shard_map/ppermute | solution.py:157
  38.2 1.4 copy-start
  44.0 1.0 copy-start.2
  44.1 1.0 copy-start.3
  44.1 1.1 copy-start.4
  47.3 49.9 %copy-start.5 = (pred[136]{0:T(512)(128)(4,1)S(1)}, pred[136]{0:T(512)(128)(4,1)}, u32[]{:S(2)}) copy-start(pred[136]{0:T(512)(128)(4,1)} %constant.61.clone.1) | copy-start | bytes 412
  47.3 20.3 %collective-permute-start.2 = (f32[520,128]{1,0:T(8,128)S(1)}, f32[520,128]{1,0:T(8,128)S(1)}, u32[]{:S(2)}, u32[]{:S(2)}) collective-permute-start(f32[520,128]{1,0:T(8,128)S(1)} %concatenate.46), channel_id=1, source_target_pairs={{0,16},{16,0},{32,48},{48,32},{64,80},{80,64},{96,112},{112,96},{1... | collective-permute-start | bytes 798728 | tf_op jit(solution)/shard_map/ppermute | solution.py:89
  69.5 17.7 %collective-permute-start.3 = (f32[520,128]{1,0:T(8,128)S(1)}, f32[520,128]{1,0:T(8,128)S(1)}, u32[]{:S(2)}, u32[]{:S(2)}) collective-permute-start(f32[520,128]{1,0:T(8,128)S(1)} %concatenate.47), channel_id=1, source_target_pairs={{0,32},{16,48},{32,0},{48,16},{64,96},{80,112},{96,64},{112,80},{1... | collective-permute-start | bytes 798728 | tf_op jit(solution)/shard_map/ppermute | solution.py:89
  89.2 7.4 %collective-permute-start.4 = (f32[136,128]{1,0:T(8,128)S(1)}, f32[136,128]{1,0:T(8,128)S(1)}, u32[]{:S(2)}, u32[]{:S(2)}) collective-permute-start(f32[136,128]{1,0:T(8,128)S(1)} %concatenate.48), channel_id=1, source_target_pairs={{64,0},{80,16},{96,32},{112,48},{128,64},{144,80},{160,96},{176,11... | collective-permute-start | bytes 208904 | tf_op jit(solution)/shard_map/ppermute | solution.py:105
  97.8 7.4 %collective-permute-start.5 = (f32[136,128]{1,0:T(8,128)S(1)}, f32[136,128]{1,0:T(8,128)S(1)}, u32[]{:S(2)}, u32[]{:S(2)}) collective-permute-start(f32[136,128]{1,0:T(8,128)S(1)} %broadcast_select_fusion.1), channel_id=1, source_target_pairs={{64,0},{80,16},{96,32},{112,48},{128,64},{144,80},{160,96},{176,11... | collective-permute-start | bytes 208904 | tf_op jit(solution)/shard_map/ppermute | solution.py:110
  107.6 8.4 %collective-permute-start.6 = (f32[136,128]{1,0:T(8,128)S(1)}, f32[136,128]{1,0:T(8,128)S(1)}, u32[]{:S(2)}, u32[]{:S(2)}) collective-permute-start(f32[136,128]{1,0:T(8,128)S(1)} %concatenate.50), channel_id=1, source_target_pairs={{128,0},{144,16},{160,32},{176,48},{192,64},{208,80},{224,96},{240... | collective-permute-start | bytes 208904 | tf_op jit(solution)/shard_map/ppermute | solution.py:110
  117.2 10.1 %collective-permute-start.7 = (f32[136,128]{1,0:T(8,128)S(1)}, f32[136,128]{1,0:T(8,128)S(1)}, u32[]{:S(2)}, u32[]{:S(2)}) collective-permute-start(f32[136,128]{1,0:T(8,128)S(1)} %concatenate.51), channel_id=1, source_target_pairs={{256,0},{272,16},{288,32},{304,48},{320,64},{336,80},{352,96},{368... | collective-permute-start | bytes 208904 | tf_op jit(solution)/shard_map/ppermute | solution.py:110
  127.3 6.2 %collective-permute-start.8 = (f32[128,128]{1,0:T(8,128)S(1)}, f32[128,128]{1,0:T(8,128)S(1)}, u32[]{:S(2)}, u32[]{:S(2)}) collective-permute-start(f32[128,128]{1,0:T(8,128)S(1)} %fusion.41), channel_id=1, source_target_pairs={{0,16},{16,0},{32,48},{48,32},{64,80},{80,64},{96,112},{112,96},{1... | collective-permute-start | bytes 196616 | tf_op jit(solution)/shard_map/ppermute | solution.py:119
  133.5 9.0 %collective-permute-start.9 = (f32[256,128]{1,0:T(8,128)S(1)}, f32[256,128]{1,0:T(8,128)S(1)}, u32[]{:S(2)}, u32[]{:S(2)}) collective-permute-start(f32[256,128]{1,0:T(8,128)S(1)} %maximum_select_fusion.1), channel_id=1, source_target_pairs={{0,32},{16,48},{32,0},{48,16},{64,96},{80,112},{96,64},{112,80},{1... | collective-permute-start | bytes 393224 | tf_op jit(solution)/shard_map/ppermute | solution.py:119

commit v6 on v4

--- a/solution.py
+++ b/solution.py
@@ -98,15 +98,16 @@
     up = [(i, i + 1) for i in range(space_size - 1)]
     down = [(i + 1, i) for i in range(space_size - 1)]
     material_f = material.astype(jnp.float32)
-    to_next = jnp.concatenate([seeded[-halo:], material_f[-halo:]], axis=0)
-    to_prev = jnp.concatenate([seeded[:halo], material_f[:halo]], axis=0)
-    from_prev = lax.ppermute(to_next, "space", up)
-    from_next = lax.ppermute(to_prev, "space", down)
-    current = jnp.concatenate([from_prev[:halo], seeded, from_next[:halo]], axis=0)
-    material_ext = jnp.concatenate(
-        [from_prev[halo:], material_f, from_next[halo:]], axis=0
-    ).astype(jnp.int32)
-    cond_ext, drain_ext = lookup_both(material_ext, conductance, rock_heat_drain)
+    material_prev = lax.ppermute(material_f[-halo:], "space", up)
+    material_next = lax.ppermute(material_f[:halo], "space", down)
+    seeded_prev = lax.ppermute(seeded[-halo:], "space", up)
+    seeded_next = lax.ppermute(seeded[:halo], "space", down)
+    cond_own, drain_own = lookup_both(material, conductance, rock_heat_drain)
+    halo_material = jnp.concatenate([material_prev, material_next], axis=0).astype(jnp.int32)
+    cond_halo, drain_halo = lookup_both(halo_material, conductance, rock_heat_drain)
+    current = jnp.concatenate([seeded_prev, seeded, seeded_next], axis=0)
+    cond_ext = jnp.concatenate([cond_halo[:halo], cond_own, cond_halo[halo:]], axis=0)
+    drain_ext = jnp.concatenate([drain_halo[:halo], drain_own, drain_halo[halo:]], axis=0)
     extended = planes + 2 * halo
     plane = lax.axis_index("space") * planes - halo + lax.iota(jnp.int32, extended)
     inside = (plane >= 0) & (plane < space_size * planes)
@@ -122,7 +123,7 @@
         z_sides = padded[:, 1:-1, 2:] + padded[:, 1:-1, :-2]
         kept = current[1:-1]
         current = kept + ((x_sides + y_sides + z_sides) - 6.0 * inner) - losses_ext[lo + 1 : hi - 1] * kept
-    cell_heat_drain = drain_ext[halo : halo + planes]
+    cell_heat_drain = drain_own
     coarse_baseline = coarsen(cell_heat_drain)
     coarse_decay_rate = jnp.exp(-FINE_STEPS * (coarse_baseline + ventilation_heat_loss[0]))
     coarse_old = coarsen(adjoint)

time: 142 us -> 130 us (0.915)
  the two profiles are of different devices: /device:TPU:19 before, /device:TPU:478 now
where the time goes in v6:
time: 130 us
  waiting for transfers between devices  61.6 us (47%)
  starting transfers between devices  28.4 us (22%)
  other arithmetic  15.5 us (12%)
  local copies, waits for them, and re-layouts  14.4 us (11%)
  Pallas kernels  6.08 us (5%)
  between operations  3.74 us (3%)
    ppermute x5, waiting for transfers between devices, shifted(): lax.ppermute(value, axis, [(source, source + steps) for source in range(i...  61.6 us
    ppermute x5, starting transfers between devices, shifted(): lax.ppermute(value, axis, [(source, source + steps) for source in range(i...  9.52 us
    ppermute x1, starting transfers between devices, on_device(): material_next = lax.ppermute(material_f[:halo], 'space', down)  7.55 us
    ppermute x1, starting transfers between devices, on_device(): seeded_next = lax.ppermute(seeded[:halo], 'space', down)  7.55 us
    pallas_call x2, Pallas kernels, lookup_both(): pl.pallas_call(_lookup_kernel, grid=(planes // block[0],), in_specs=[smem...  6.08 us
    mul x4, other arithmetic, on_device(): weighted = cond_ext[lo:hi] * current  5.22 us
    slice x2, local copies, waits for them, and re-layouts, coarsen(): split[:, 1, :, 0]  4.55 us
    slice x4, local copies, waits for them, and re-layouts, on_device(): gain = gain * arrived[rows, 0]  3.39 us
  transfers between devices with their start and end apart: 9, of which 5 were waited for; matrix products, arithmetic and copies ran while one was open for 8% of the time, Pallas kernels for 5%

profile of v6, /device:TPU:478, one launch (start us, length us, event | category | flops | bytes accessed | tf_op | source)
XLA Modules:
  0.0 129.7 jit_solution(11683049819319617407)
XLA Ops:
  0.0 1.3 %convert_element_type.14 = f32[16,128,128]{2,1,0:T(8,128)S(1)} convert(s32[16,128,128]{2,1,0:T(8,128)} %material_ref.1) | non-fusion elementwise | flops 262144 | bytes 2097152 | tf_op jit(solution)/shard_map/convert_element_type | solution.py:100
  1.3 0.8 fusion.50
  2.2 1.9 %collective-permute-start.2 = (f32[4,128,128]{2,1,0:T(8,128)}, f32[4,128,128]{2,1,0:T(8,128)}, u32[]{:S(2)}, u32[]{:S(2)}) collective-permute-start(f32[4,128,128]{2,1,0:T(8,128)} %get-tuple-element.24), channel_id=1, source_target_pairs={{0,1},{1,2},{2,3},{3,4},{4,5},{5,6},{6,7},{7,8},{8,9},{9,10},{10,1... | collective-permute-start | bytes 786440 | tf_op jit(solution)/shard_map/ppermute | solution.py:101
  4.1 7.6 %collective-permute-start.3 = (f32[4,128,128]{2,1,0:T(8,128)}, f32[4,128,128]{2,1,0:T(8,128)}, u32[]{:S(2)}, u32[]{:S(2)}) collective-permute-start(f32[4,128,128]{2,1,0:T(8,128)} %get-tuple-element.25), channel_id=1, source_target_pairs={{1,0},{2,1},{3,2},{4,3},{5,4},{6,5},{7,6},{8,7},{9,8},{10,9},{11,1... | collective-permute-start | bytes 786440 | tf_op jit(solution)/shard_map/ppermute | solution.py:102
  11.7 1.3 %scatter_custom_fusion = f32[262144]{0:T(1024)S(1)} fusion(s32[64]{0:T(128)S(1)} %compare_select_fusion, f32[64]{0:T(128)} %bitcast.102, f32[]{:T(128)} %constant.19.clone.1), kind=kCustom, calls=%fused_computation.63 | custom fusion | flops 64 | bytes 1049088 | tf_op jit(solution)/shard_map/scatter-add | solution.py:92
  13.0 0.1 bitcast_add_fusion
  13.1 0.8 fusion.51
  14.0 1.9 %collective-permute-start = (f32[4,128,128]{2,1,0:T(8,128)}, f32[4,128,128]{2,1,0:T(8,128)}, u32[]{:S(2)}, u32[]{:S(2)}) collective-permute-start(f32[4,128,128]{2,1,0:T(8,128)} %get-tuple-element.26), channel_id=1, source_target_pairs={{0,1},{1,2},{2,3},{3,4},{4,5},{5,6},{6,7},{7,8},{8,9},{9,10},{10,1... | collective-permute-start | bytes 786440 | tf_op jit(solution)/shard_map/ppermute | solution.py:103
  15.9 7.6 %collective-permute-start.1 = (f32[4,128,128]{2,1,0:T(8,128)}, f32[4,128,128]{2,1,0:T(8,128)}, u32[]{:S(2)}, u32[]{:S(2)}) collective-permute-start(f32[4,128,128]{2,1,0:T(8,128)} %get-tuple-element.27), channel_id=1, source_target_pairs={{1,0},{2,1},{3,2},{4,3},{5,4},{6,5},{7,6},{8,7},{9,8},{10,9},{11,1... | collective-permute-start | bytes 786440 | tf_op jit(solution)/shard_map/ppermute | solution.py:104
  24.1 3.8 %shard_map.73 = (f32[16,128,128]{2,1,0:T(8,128)}, f32[16,128,128]{2,1,0:T(8,128)}) custom-call(f32[8]{0:T(128)} %cond_table.3, f32[8]{0:T(128)} %drain_table.3, s32[16,128,128]{2,1,0:T(8,128)} %material_ref.1), custom_call_target="tpu_custom_call" | custom-call | tf_op jit(solution)/shard_map/pallas_call | solution.py:66
  28.0 2.6 %fusion.52 = (f32[8,1,64,1,128]{4,3,2,1,0:T(1,128)S(1)}, f32[8,1,64,1,128]{4,3,2,1,0:T(1,128)S(1)}, f32[8,1,64,1,128]{4,3,2,1,0:T(1,128)S(1)}, f32[8,1,64,1,128]{4,3,2,1,0:T(1,128)S(1)}) fusion(f32[8,2,64,2,128]{4,3,2,1,0:T(2,128)} %bitcast.82), kind=kLoop, calls=%fused_computation.104 | loop fusion | bytes 2097152 | tf_op jit(solution)/shard_map/slice | solution.py:32
  30.6 1.9 %fusion.53 = (f32[8,1,64,1,128]{4,3,2,1,0:T(1,128)}, f32[8,1,64,1,128]{4,3,2,1,0:T(1,128)}, f32[8,1,64,1,128]{4,3,2,1,0:T(1,128)}, f32[8,1,64,1,128]{4,3,2,1,0:T(1,128)}) fusion(f32[8,2,64,2,128]{4,3,2,1,0:T(2,128)S(1)} %bitcast.78), kind=kLoop, calls=%fused_computation.105 | loop fusion | bytes 2097152 | tf_op jit(solution)/shard_map/slice | solution.py:32
  32.7 0.8 copy-done.3
  33.8 0.1 exponential_multiply_fusion
  33.9 1.9 %maximum_convert_fusion.material_ref = s32[8,128,128]{2,1,0:T(8,128)} fusion(f32[4,128,128]{2,1,0:T(8,128)} %collective-permute-done.3, f32[4,128,128]{2,1,0:T(8,128)} %collective-permute-done.2), kind=kLoop, calls=%fused_computation.62 | loop fusion | flops 262144 | bytes 1048576 | tf_op jit(solution)/shard_map/convert_element_type | solution.py:106
  35.9 2.2 %shard_map.74 = (f32[8,128,128]{2,1,0:T(8,128)}, f32[8,128,128]{2,1,0:T(8,128)}) custom-call(f32[8]{0:T(128)} %cond_table.3, f32[8]{0:T(128)} %drain_table.3, s32[8,128,128]{2,1,0:T(8,128)} %maximum_convert_fusion.material_ref), custom_call_target="tpu_custom_call" | custom-call | tf_op jit(solution)/shard_map/pallas_call | solution.py:66
  38.1 1.1 fusion.55
  39.2 1.4 %fusion.46 = (f32[24,128,128]{2,1,0:T(8,128)S(1)}, f32[24,128,128]{2,1,0:T(8,128)S(1)}, f32[24,128,128]{2,1,0:T(8,128)S(1)}) fusion(f32[4,128,128]{2,1,0:T(8,128)} %collective-permute-done.1, f32[16,128,128]{2,1,0:T(8,128)S(1)} %bitcast_add_fusion, f32[4,128,128]{2,1,0:T(8,128)} %collective-permute-done, f32[4,128,128]{2,1,0:T(8,128)S(1)} %get-tuple-element.39, ...), kind=kLoop, calls=%fused_computation.101 | loop fusion | flops 2359296 | bytes 7864344 | tf_op jit(solution)/shard_map/mul | solution.py:118
  40.6 0.1 slice.287
  40.7 0.9 copy-done.7
  41.6 0.3 copy-done.1
  42.0 0.1 maximum_add_fusion
  42.1 1.4 %slice_multiply_fusion = (f32[22,128,128]{2,1,0:T(8,128)S(1)}, f32[22,128,128]{2,1,0:T(8,128)S(1)}) fusion(f32[24,128,128]{2,1,0:T(8,128)S(1)} %get-tuple-element.22, f32[24,128,128]{2,1,0:T(8,128)S(1)} %maximum_add_fusion, f32[22,128,128]{2,1,0:T(8,128)S(1)} %slice.287, f32[24,128,128]{2,1,0:T(8,128)S(1)} %get-tuple-element.21, ...), kind=kLoop, calls=%fused_computation.27 | loop fusion | flops 3964928 | bytes 11534336 | tf_op jit(solution)/shard_map/mul | solution.py:118
  43.5 0.1 slice.293
  43.6 1.3 slice_multiply_fusion.2
  45.0 1.2 slice_multiply_fusion.4
  46.4 0.4 broadcast_in_dim.44
  46.7 1.0 fusion.27
  47.8 0.6 fusion.39
  48.4 2.5 %collective-permute-start.4 = (f32[520,128]{1,0:T(8,128)S(1)}, f32[520,128]{1,0:T(8,128)S(1)}, u32[]{:S(2)}, u32[]{:S(2)}) collective-permute-start(f32[520,128]{1,0:T(8,128)S(1)} %concatenate.31), channel_id=1, source_target_pairs={{16,0},{32,16},{48,32},{64,48},{80,64},{96,80},{112,96},{128,112},... | collective-permute-start | bytes 798728 | tf_op jit(solution)/shard_map/ppermute | solution.py:27
  50.9 10.5 %collective-permute-done.4 = f32[520,128]{1,0:T(8,128)S(1)} collective-permute-done((f32[520,128]{1,0:T(8,128)S(1)}, f32[520,128]{1,0:T(8,128)S(1)}, u32[]{:S(2)}, u32[]{:S(2)}) %collective-permute-start.4) | collective-permute-done | bytes 266272 | tf_op jit(solution)/shard_map/ppermute | solution.py:27
  61.4 0.5 slice.312
  62.7 1.9 %collective-permute-start.5 = (f32[520,128]{1,0:T(8,128)S(1)}, f32[520,128]{1,0:T(8,128)S(1)}, u32[]{:S(2)}, u32[]{:S(2)}) collective-permute-start(f32[520,128]{1,0:T(8,128)S(1)} %concatenate.32), channel_id=1, source_target_pairs={{32,0},{48,16},{64,32},{80,48},{96,64},{112,80},{128,96},{144,112}... | collective-permute-start | bytes 798728 | tf_op jit(solution)/shard_map/ppermute | solution.py:27
  64.6 12.1 %collective-permute-done.5 = f32[520,128]{1,0:T(8,128)S(1)} collective-permute-done((f32[520,128]{1,0:T(8,128)S(1)}, f32[520,128]{1,0:T(8,128)S(1)}, u32[]{:S(2)}, u32[]{:S(2)}) %collective-permute-start.5) | collective-permute-done | bytes 266272 | tf_op jit(solution)/shard_map/ppermute | solution.py:27
  76.7 0.5 slice.314
  78.0 1.9 %collective-permute-start.6 = (f32[520,128]{1,0:T(8,128)S(1)}, f32[520,128]{1,0:T(8,128)}, u32[]{:S(2)}, u32[]{:S(2)}) collective-permute-start(f32[520,128]{1,0:T(8,128)S(1)} %concatenate.33), channel_id=1, source_target_pairs={{64,0},{80,16},{96,32},{112,48},{128,64},{144,80},{160,96},{176,11... | collective-permute-start | bytes 798728 | tf_op jit(solution)/shard_map/ppermute | solution.py:27
  79.9 12.3 %collective-permute-done.6 = f32[520,128]{1,0:T(8,128)} collective-permute-done((f32[520,128]{1,0:T(8,128)S(1)}, f32[520,128]{1,0:T(8,128)}, u32[]{:S(2)}, u32[]{:S(2)}) %collective-permute-start.6) | collective-permute-done | bytes 266272 | tf_op jit(solution)/shard_map/ppermute | solution.py:27
  92.2 1.2 slice.316
  94.1 1.0 fusion.58
  95.1 1.9 %collective-permute-start.7 = (f32[520,128]{1,0:T(8,128)S(1)}, f32[520,128]{1,0:T(8,128)}, u32[]{:S(2)}, u32[]{:S(2)}) collective-permute-start(f32[520,128]{1,0:T(8,128)S(1)} %concatenate.34), channel_id=1, source_target_pairs={{128,0},{144,16},{160,32},{176,48},{192,64},{208,80},{224,96},{240... | collective-permute-start | bytes 798728 | tf_op jit(solution)/shard_map/ppermute | solution.py:27
  97.1 15.8 %collective-permute-done.7 = f32[520,128]{1,0:T(8,128)} collective-permute-done((f32[520,128]{1,0:T(8,128)S(1)}, f32[520,128]{1,0:T(8,128)}, u32[]{:S(2)}, u32[]{:S(2)}) %collective-permute-start.7) | collective-permute-done | bytes 266272 | tf_op jit(solution)/shard_map/ppermute | solution.py:27
  112.9 1.2 slice.318
  114.7 1.0 fusion.59
  115.7 1.3 collective-permute-start.8
  117.0 10.9 %collective-permute-done.8 = f32[520,128]{1,0:T(8,128)S(1)} collective-permute-done((f32[520,128]{1,0:T(8,128)S(1)}, f32[520,128]{1,0:T(8,128)S(1)}, u32[]{:S(2)}, u32[]{:S(2)}) %collective-permute-start.8) | collective-permute-done | bytes 266272 | tf_op jit(solution)/shard_map/ppermute | solution.py:27
  128.0 0.2 fusion.37
  128.3 0.4 broadcast_in_dim.46
  128.6 1.1 add_bitcast_fusion
  (39 shorter events, 1.1 us)
Async XLA Ops:
  0.0 11.7 %copy-start.8 = (s32[64]{0:T(128)S(1)}, s32[64]{0:T(128)}, u32[]{:S(2)}) copy-start(s32[64]{0:T(128)} %param.9) | copy-start | bytes 772
  1.3 11.7 %copy-start = (f32[1,16,128,128]{3,2,1,0:T(8,128)S(1)}, f32[1,16,128,128]{3,2,1,0:T(8,128)}, u32[]{:S(2)}) copy-start(f32[1,16,128,128]{3,2,1,0:T(8,128)} %param.7) | copy-start | bytes 3145732
  2.2 31.7 %collective-permute-start.2 = (f32[4,128,128]{2,1,0:T(8,128)}, f32[4,128,128]{2,1,0:T(8,128)}, u32[]{:S(2)}, u32[]{:S(2)}) collective-permute-start(f32[4,128,128]{2,1,0:T(8,128)} %get-tuple-element.24), channel_id=1, source_target_pairs={{0,1},{1,2},{2,3},{3,4},{4,5},{5,6},{6,7},{7,8},{8,9},{9,10},{10,1... | collective-permute-start | bytes 786440 | tf_op jit(solution)/shard_map/ppermute | solution.py:101
  4.1 29.8 %collective-permute-start.3 = (f32[4,128,128]{2,1,0:T(8,128)}, f32[4,128,128]{2,1,0:T(8,128)}, u32[]{:S(2)}, u32[]{:S(2)}) collective-permute-start(f32[4,128,128]{2,1,0:T(8,128)} %get-tuple-element.25), channel_id=1, source_target_pairs={{1,0},{2,1},{3,2},{4,3},{5,4},{6,5},{7,6},{8,7},{9,8},{10,9},{11,1... | collective-permute-start | bytes 786440 | tf_op jit(solution)/shard_map/ppermute | solution.py:102
  14.0 25.2 %collective-permute-start = (f32[4,128,128]{2,1,0:T(8,128)}, f32[4,128,128]{2,1,0:T(8,128)}, u32[]{:S(2)}, u32[]{:S(2)}) collective-permute-start(f32[4,128,128]{2,1,0:T(8,128)} %get-tuple-element.26), channel_id=1, source_target_pairs={{0,1},{1,2},{2,3},{3,4},{4,5},{5,6},{6,7},{7,8},{8,9},{9,10},{10,1... | collective-permute-start | bytes 786440 | tf_op jit(solution)/shard_map/ppermute | solution.py:103
  15.9 23.3 %collective-permute-start.1 = (f32[4,128,128]{2,1,0:T(8,128)}, f32[4,128,128]{2,1,0:T(8,128)}, u32[]{:S(2)}, u32[]{:S(2)}) collective-permute-start(f32[4,128,128]{2,1,0:T(8,128)} %get-tuple-element.27), channel_id=1, source_target_pairs={{1,0},{2,1},{3,2},{4,3},{5,4},{6,5},{7,6},{8,7},{9,8},{10,9},{11,1... | collective-permute-start | bytes 786440 | tf_op jit(solution)/shard_map/ppermute | solution.py:104
  32.6 0.9 copy-start.3
  32.6 1.0 copy-start.4
  32.6 1.1 copy-start.5
  32.6 1.2 copy-start.6
  33.9 5.3 %copy-start.2 = (f32[16,128,128]{2,1,0:T(8,128)S(1)}, f32[16,128,128]{2,1,0:T(8,128)}, u32[]{:S(2)}) copy-start(f32[16,128,128]{2,1,0:T(8,128)} %get-tuple-element.11) | copy-start | bytes 3145732
  40.6 1.0 copy-start.7
  40.6 1.4 %copy-start.1 = (f32[16,128,128]{2,1,0:T(8,128)S(1)}, f32[16,128,128]{2,1,0:T(8,128)}, u32[]{:S(2)}) copy-start(f32[16,128,128]{2,1,0:T(8,128)} %get-tuple-element.9) | copy-start | bytes 3145732
  48.4 13.0 %collective-permute-start.4 = (f32[520,128]{1,0:T(8,128)S(1)}, f32[520,128]{1,0:T(8,128)S(1)}, u32[]{:S(2)}, u32[]{:S(2)}) collective-permute-start(f32[520,128]{1,0:T(8,128)S(1)} %concatenate.31), channel_id=1, source_target_pairs={{16,0},{32,16},{48,32},{64,48},{80,64},{96,80},{112,96},{128,112},... | collective-permute-start | bytes 798728 | tf_op jit(solution)/shard_map/ppermute | solution.py:27
  62.7 14.1 %collective-permute-start.5 = (f32[520,128]{1,0:T(8,128)S(1)}, f32[520,128]{1,0:T(8,128)S(1)}, u32[]{:S(2)}, u32[]{:S(2)}) collective-permute-start(f32[520,128]{1,0:T(8,128)S(1)} %concatenate.32), channel_id=1, source_target_pairs={{32,0},{48,16},{64,32},{80,48},{96,64},{112,80},{128,96},{144,112}... | collective-permute-start | bytes 798728 | tf_op jit(solution)/shard_map/ppermute | solution.py:27
  78.0 14.2 %collective-permute-start.6 = (f32[520,128]{1,0:T(8,128)S(1)}, f32[520,128]{1,0:T(8,128)}, u32[]{:S(2)}, u32[]{:S(2)}) collective-permute-start(f32[520,128]{1,0:T(8,128)S(1)} %concatenate.33), channel_id=1, source_target_pairs={{64,0},{80,16},{96,32},{112,48},{128,64},{144,80},{160,96},{176,11... | collective-permute-start | bytes 798728 | tf_op jit(solution)/shard_map/ppermute | solution.py:27
  95.1 17.7 %collective-permute-start.7 = (f32[520,128]{1,0:T(8,128)S(1)}, f32[520,128]{1,0:T(8,128)}, u32[]{:S(2)}, u32[]{:S(2)}) collective-permute-start(f32[520,128]{1,0:T(8,128)S(1)} %concatenate.34), channel_id=1, source_target_pairs={{128,0},{144,16},{160,32},{176,48},{192,64},{208,80},{224,96},{240... | collective-permute-start | bytes 798728 | tf_op jit(solution)/shard_map/ppermute | solution.py:27
  115.7 12.2 %collective-permute-start.8 = (f32[520,128]{1,0:T(8,128)S(1)}, f32[520,128]{1,0:T(8,128)S(1)}, u32[]{:S(2)}, u32[]{:S(2)}) collective-permute-start(f32[520,128]{1,0:T(8,128)S(1)} %concatenate.35), channel_id=1, source_target_pairs={{256,0},{272,16},{288,32},{304,48},{320,64},{336,80},{352,96},{368... | collective-permute-start | bytes 798728 | tf_op jit(solution)/shard_map/ppermute | solution.py:27

commit v7 on v6

--- a/solution.py
+++ b/solution.py
@@ -70,6 +70,25 @@
         out_specs=[spec, spec],
         out_shape=[out, out],
     )(conductance, rock_heat_drain, material)
+
+
+def pack(field, scalar):
+    return jnp.concatenate([field, jnp.broadcast_to(scalar, (8, field.shape[-1]))], axis=0)
+
+
+def fine_steps(current, cond, losses):
+    planes = current.shape[0]
+    for sweep_index in range(FINE_STEPS):
+        lo, hi = sweep_index, planes - sweep_index
+        weighted = cond[lo:hi] * current
+        x_sides = weighted[2:] + weighted[:-2]
+        inner = weighted[1:-1]
+        padded = jnp.pad(inner, ((0, 0), (1, 1), (1, 1)))
+        y_sides = padded[:, 2:, 1:-1] + padded[:, :-2, 1:-1]
+        z_sides = padded[:, 1:-1, 2:] + padded[:, 1:-1, :-2]
+        kept = current[1:-1]
+        current = kept + ((x_sides + y_sides + z_sides) - 6.0 * inner) - losses[lo + 1 : hi - 1] * kept
+    return current
 
 
 def on_device(
@@ -113,42 +132,56 @@
     inside = (plane >= 0) & (plane < space_size * planes)
     cond_ext = jnp.where(inside[:, None, None], cond_ext, 0.0)
     losses_ext = drain_ext + ventilation_heat_loss[0]
-    for sweep_index in range(FINE_STEPS):
-        lo, hi = sweep_index, extended - sweep_index
-        weighted = cond_ext[lo:hi] * current
-        x_sides = weighted[2:] + weighted[:-2]
-        inner = weighted[1:-1]
-        padded = jnp.pad(inner, ((0, 0), (1, 1), (1, 1)))
-        y_sides = padded[:, 2:, 1:-1] + padded[:, :-2, 1:-1]
-        z_sides = padded[:, 1:-1, 2:] + padded[:, 1:-1, :-2]
-        kept = current[1:-1]
-        current = kept + ((x_sides + y_sides + z_sides) - 6.0 * inner) - losses_ext[lo + 1 : hi - 1] * kept
-    cell_heat_drain = drain_own
-    coarse_baseline = coarsen(cell_heat_drain)
+    losses_own = drain_own + ventilation_heat_loss[0]
+    middle = fine_steps(seeded, cond_own, losses_own)
+    coarse_baseline = coarsen(drain_own)
     coarse_decay_rate = jnp.exp(-FINE_STEPS * (coarse_baseline + ventilation_heat_loss[0]))
     coarse_old = coarsen(adjoint)
-    correction = current - refine(coarse_decay_rate * coarse_old)
-    reduced = coarsen(correction)
+    decayed_old = coarse_decay_rate * coarse_old
+    edge = halo // 2
+    coarse_planes = coarse_old.shape[0]
+    inner = slice(edge, coarse_planes - edge)
+    correction_mid = middle - refine(decayed_old[inner])
+    reduced_mid = coarsen(correction_mid)
+    decayed_edge = jnp.concatenate([decayed_old[:edge], decayed_old[-edge:]], axis=0)
     tm_size = lax.axis_size("tm")
     is_last = lax.axis_index("tm") == tm_size - 1
     per_cell = jnp.exp(-FINE_STEPS * coarse_baseline)
     gain = jnp.exp(-FINE_STEPS * ventilation_heat_loss[0])
-    top = coarse_decay_rate * coarse_old + reduced
-    total = jnp.where(is_last, top, reduced)
-    shape = total.shape
-    rows = total.size // shape[-1]
-    power = per_cell
+    total_mid = jnp.where(is_last, decayed_old[inner] + reduced_mid, reduced_mid)
+    power_mid = per_cell[inner]
+    power_edge = jnp.concatenate([per_cell[:edge], per_cell[-edge:]], axis=0)
+    shape = total_mid.shape
+    width = shape[-1]
+    rows = total_mid.size // width
+    gains = []
     distance = 1
     while distance < tm_size:
-        packed = jnp.concatenate(
-            [total.reshape(rows, shape[-1]), jnp.broadcast_to(gain, (8, shape[-1]))], axis=0
-        )
-        arrived = shifted(packed, "tm", -distance)
-        total = total + (power * gain) * arrived[:rows].reshape(shape)
+        gains.append(gain)
+        arrived = shifted(pack(total_mid.reshape(rows, width), gain), "tm", -distance)
+        total_mid = total_mid + (power_mid * gain) * arrived[:rows].reshape(shape)
         gain = gain * arrived[rows, 0]
-        power = power * power
+        power_mid = power_mid * power_mid
         distance *= 2
-    decayed = jnp.where(is_last, coarse_decay_rate * coarse_old, total - reduced)
+    current, cond_ext, losses_ext, total_mid = lax.optimization_barrier(
+        (current, cond_ext, losses_ext, total_mid)
+    )
+    low = fine_steps(current[: 3 * halo], cond_ext[: 3 * halo], losses_ext[: 3 * halo])
+    high = fine_steps(current[-3 * halo :], cond_ext[-3 * halo :], losses_ext[-3 * halo :])
+    correction_low = low - refine(decayed_old[:edge])
+    correction_high = high - refine(decayed_old[-edge:])
+    reduced_edge = jnp.concatenate([coarsen(correction_low), coarsen(correction_high)], axis=0)
+    total_edge = jnp.where(is_last, decayed_edge + reduced_edge, reduced_edge)
+    distance = 1
+    for own_gain in gains:
+        arrived = shifted(total_edge, "tm", -distance)
+        total_edge = total_edge + (power_edge * own_gain) * arrived
+        power_edge = power_edge * power_edge
+        distance *= 2
+    total = jnp.concatenate([total_edge[:edge], total_mid, total_edge[edge:]], axis=0)
+    reduced = jnp.concatenate([reduced_edge[:edge], reduced_mid, reduced_edge[edge:]], axis=0)
+    correction = jnp.concatenate([correction_low, correction_mid, correction_high], axis=0)
+    decayed = jnp.where(is_last, decayed_old, total - reduced)
     adjoint_new = refine(decayed) + correction
     return adjoint_new[None]
 

time: 130 us -> 166 us (1.28)
  the two profiles are of different devices: /device:TPU:478 before, /device:TPU:22 now
where the time goes in v7:
time: 166 us; the launch traced here: 165 us
  waiting for transfers between devices  70.7 us (43%)
  starting transfers between devices  46.1 us (28%)
  other arithmetic  19.9 us (12%)
  local copies, waits for them, and re-layouts  18.1 us (11%)
  Pallas kernels  6.02 us (4%)
  between operations  4.27 us (3%)
    ppermute x10, waiting for transfers between devices, shifted(): lax.ppermute(value, axis, [(source, source + steps) for source in range(i...  58.9 us
    ppermute x10, starting transfers between devices, shifted(): lax.ppermute(value, axis, [(source, source + steps) for source in range(i...  25.3 us
    ppermute x1, waiting for transfers between devices, on_device(): material_prev = lax.ppermute(material_f[-halo:], 'space', up)  11.8 us
    ppermute x1, starting transfers between devices, on_device(): seeded_next = lax.ppermute(seeded[:halo], 'space', down)  8.58 us
    ppermute x1, starting transfers between devices, on_device(): material_next = lax.ppermute(material_f[:halo], 'space', down)  8.45 us
    mul x8, other arithmetic, fine_steps(): weighted = cond[lo:hi] * current  7.53 us
    pallas_call x2, Pallas kernels, lookup_both(): pl.pallas_call(_lookup_kernel, grid=(planes // block[0],), in_specs=[smem...  6.02 us
    unnamed x30, local copies, waits for them, and re-layouts  3.88 us
  transfers between devices with their start and end apart: 14, of which 9 were waited for; matrix products, arithmetic and copies ran while one was open for 8% of the time, Pallas kernels for 1%

profile of v7, /device:TPU:22, one launch (start us, length us, event | category | flops | bytes accessed | tf_op | source)
XLA Modules:
  0.0 165.2 jit_solution(4079825504786089849)
XLA Ops:
  1.4 3.8 %shard_map.73 = (f32[16,128,128]{2,1,0:T(8,128)}, f32[16,128,128]{2,1,0:T(8,128)}) custom-call(f32[8]{0:T(128)} %cond_table.3, f32[8]{0:T(128)} %drain_table.3, s32[16,128,128]{2,1,0:T(8,128)} %material_ref.1), custom_call_target="tpu_custom_call" | custom-call | tf_op jit(solution)/shard_map/pallas_call | solution.py:66
  5.2 2.2 %scatter_custom_fusion = f32[262144]{0:T(1024)} fusion(s32[64]{0:T(128)S(1)} %compare_select_fusion, f32[64]{0:T(128)} %bitcast.143, f32[]{:T(128)} %constant.19.clone.1), kind=kCustom, calls=%fused_computation.134 | custom fusion | flops 64 | bytes 1049088 | tf_op jit(solution)/shard_map/scatter-add | solution.py:111
  7.4 1.8 %fusion.107 = (f32[16,128,128]{2,1,0:T(8,128)S(1)}, f32[16,128,128]{2,1,0:T(8,128)S(1)}, f32[16,128,128]{2,1,0:T(8,128)S(1)}) fusion(f32[16,128,128]{2,1,0:T(8,128)S(1)} %copy-done, f32[16,128,128]{2,1,0:T(8,128)} %bitcast.102, f32[1,16,128,128]{3,2,1,0:T(8,128)S(1)} %copy-done.7, f32[16,128,128]{2,1,0:T(8,128)} %get-tuple-element.13, f32[]{:T(128)} %bitcast.95), kind=kLoop, calls=%fused_computation.211 | loop fusion | flops 786432 | bytes 7340036 | tf_op jit(solution)/shard_map/mul | solution.py:83
  9.4 0.9 slice_multiply_fusion.1
  10.3 0.8 slice_multiply_fusion.5
  11.9 1.2 copy-done.3
  13.0 1.1 fusion.110
  14.1 1.1 fusion.111
  16.2 0.8 copy-done.4
  17.1 1.2 fusion.112
  18.3 1.9 %add_select_fusion.1 = (f32[4,64,128]{2,1,0:T(8,128)S(1)}, f32[4,64,128]{2,1,0:T(8,128)}) fusion(pred[]{:T(512)S(6)} %eq.3, f32[8,1,64,1,128]{4,2,0,3,1:T(8,128)} %copy-done.8, f32[4,1,64,1,128]{4,2,0,3,1:T(8,128)} %bitcast.135, f32[4,1,64,1,128]{4,2,0,3,1:T(8,128)} %bitcast.137, f32[4,1,64,1,128]{4,2,0,3,1:T(8,128)} %bitcast.136, ...), kind=kLoop, calls=%fused_computation.178 | loop fusion | flops 196608 | bytes 917505 | tf_op jit(solution)/shard_map/jit(_where)/select_n | solution.py:151
  20.9 7.8 %collective-permute-start.4 = (f32[264,128]{1,0:T(8,128)}, f32[264,128]{1,0:T(8,128)}, u32[]{:S(2)}, u32[]{:S(2)}) collective-permute-start(f32[264,128]{1,0:T(8,128)} %concatenate.63), channel_id=1, source_target_pairs={{16,0},{32,16},{48,32},{64,48},{80,64},{96,80},{112,96},{128,112},... | collective-permute-start | bytes 405512 | tf_op jit(solution)/shard_map/ppermute | solution.py:27
  28.7 0.8 fusion.109
  29.5 1.9 %collective-permute-start = (f32[4,128,128]{2,1,0:T(8,128)}, f32[4,128,128]{2,1,0:T(8,128)}, u32[]{:S(2)}, u32[]{:S(2)}) collective-permute-start(f32[4,128,128]{2,1,0:T(8,128)} %get-tuple-element.57), channel_id=1, source_target_pairs={{0,1},{1,2},{2,3},{3,4},{4,5},{5,6},{6,7},{7,8},{8,9},{9,10},{10,1... | collective-permute-start | bytes 786440 | tf_op jit(solution)/shard_map/ppermute | solution.py:122
  31.4 8.6 %collective-permute-start.1 = (f32[4,128,128]{2,1,0:T(8,128)}, f32[4,128,128]{2,1,0:T(8,128)}, u32[]{:S(2)}, u32[]{:S(2)}) collective-permute-start(f32[4,128,128]{2,1,0:T(8,128)} %get-tuple-element.58), channel_id=1, source_target_pairs={{1,0},{2,1},{3,2},{4,3},{5,4},{6,5},{7,6},{8,7},{9,8},{10,9},{11,1... | collective-permute-start | bytes 786440 | tf_op jit(solution)/shard_map/ppermute | solution.py:123
  40.2 1.9 %collective-permute-start.2 = (f32[4,128,128]{2,1,0:T(8,128)S(1)}, f32[4,128,128]{2,1,0:T(8,128)S(1)}, u32[]{:S(2)}, u32[]{:S(2)}) collective-permute-start(f32[4,128,128]{2,1,0:T(8,128)S(1)} %get-tuple-element.55), channel_id=1, source_target_pairs={{0,1},{1,2},{2,3},{3,4},{4,5},{5,6},{6,7},{7,8},{8,9},{9,10},{10,1... | collective-permute-start | bytes 786440 | tf_op jit(solution)/shard_map/ppermute | solution.py:120
  42.1 8.4 %collective-permute-start.3 = (f32[4,128,128]{2,1,0:T(8,128)S(1)}, f32[4,128,128]{2,1,0:T(8,128)S(1)}, u32[]{:S(2)}, u32[]{:S(2)}) collective-permute-start(f32[4,128,128]{2,1,0:T(8,128)S(1)} %get-tuple-element.56), channel_id=1, source_target_pairs={{1,0},{2,1},{3,2},{4,3},{5,4},{6,5},{7,6},{8,7},{9,8},{10,9},{11,1... | collective-permute-start | bytes 786440 | tf_op jit(solution)/shard_map/ppermute | solution.py:121
  51.2 1.3 slice.741
  53.2 0.9 slice.740
  54.2 1.9 %collective-permute-start.5 = (f32[264,128]{1,0:T(8,128)S(1)}, f32[264,128]{1,0:T(8,128)S(1)}, u32[]{:S(2)}, u32[]{:S(2)}) collective-permute-start(f32[264,128]{1,0:T(8,128)S(1)} %concatenate.64), channel_id=1, source_target_pairs={{32,0},{48,16},{64,32},{80,48},{96,64},{112,80},{128,96},{144,112}... | collective-permute-start | bytes 405512 | tf_op jit(solution)/shard_map/ppermute | solution.py:27
  56.1 11.8 %collective-permute-done.2 = f32[4,128,128]{2,1,0:T(8,128)S(1)} collective-permute-done((f32[4,128,128]{2,1,0:T(8,128)S(1)}, f32[4,128,128]{2,1,0:T(8,128)S(1)}, u32[]{:S(2)}, u32[]{:S(2)}) %collective-permute-start.2) | collective-permute-done | bytes 262176 | tf_op jit(solution)/shard_map/ppermute | solution.py:120
  67.9 0.8 maximum_convert_fusion.material_ref
  68.8 2.2 %shard_map.74 = (f32[8,128,128]{2,1,0:T(8,128)}, f32[8,128,128]{2,1,0:T(8,128)}) custom-call(f32[8]{0:T(128)} %cond_table.3, f32[8]{0:T(128)} %drain_table.3, s32[8,128,128]{2,1,0:T(8,128)} %maximum_convert_fusion.material_ref), custom_call_target="tpu_custom_call" | custom-call | tf_op jit(solution)/shard_map/pallas_call | solution.py:66
  71.0 2.1 %fusion.113 = (f32[4,128,128]{2,1,0:T(8,128)}, f32[4,128,128]{2,1,0:T(8,128)}, f32[4,128,128]{2,1,0:T(8,128)S(1)}, f32[4,128,128]{2,1,0:T(8,128)}) fusion(f32[8,128,128]{2,1,0:T(8,128)} %get-tuple-element.16, f32[8,128,128]{2,1,0:T(8,128)} %get-tuple-element.14), kind=kLoop, calls=%fused_computation.217 | loop fusion | bytes 2097152 | tf_op jit(solution)/shard_map/slice | solution.py:129
  74.4 2.4 %collective-permute-start.6 = (f32[264,128]{1,0:T(8,128)S(1)}, f32[264,128]{1,0:T(8,128)S(1)}, u32[]{:S(2)}, u32[]{:S(2)}) collective-permute-start(f32[264,128]{1,0:T(8,128)S(1)} %concatenate.65), channel_id=1, source_target_pairs={{64,0},{80,16},{96,32},{112,48},{128,64},{144,80},{160,96},{176,11... | collective-permute-start | bytes 405512 | tf_op jit(solution)/shard_map/ppermute | solution.py:27
  76.8 1.1 maximum_select_fusion
  77.9 4.2 %collective-permute-done.6 = f32[264,128]{1,0:T(8,128)S(1)} collective-permute-done((f32[264,128]{1,0:T(8,128)S(1)}, f32[264,128]{1,0:T(8,128)S(1)}, u32[]{:S(2)}, u32[]{:S(2)}) %collective-permute-start.6) | collective-permute-done | bytes 135200 | tf_op jit(solution)/shard_map/ppermute | solution.py:27
  83.5 2.6 %collective-permute-start.7 = (f32[264,128]{1,0:T(8,128)S(1)}, f32[264,128]{1,0:T(8,128)S(1)}, u32[]{:S(2)}, u32[]{:S(2)}) collective-permute-start(f32[264,128]{1,0:T(8,128)S(1)} %concatenate.66), channel_id=1, source_target_pairs={{128,0},{144,16},{160,32},{176,48},{192,64},{208,80},{224,96},{240... | collective-permute-start | bytes 405512 | tf_op jit(solution)/shard_map/ppermute | solution.py:27
  86.1 1.5 maximum_add_fusion
  87.6 8.4 %collective-permute-done.7 = f32[264,128]{1,0:T(8,128)S(1)} collective-permute-done((f32[264,128]{1,0:T(8,128)S(1)}, f32[264,128]{1,0:T(8,128)S(1)}, u32[]{:S(2)}, u32[]{:S(2)}) %collective-permute-start.7) | collective-permute-done | bytes 135200 | tf_op jit(solution)/shard_map/ppermute | solution.py:27
  97.9 1.0 slice.746
  99.0 1.5 collective-permute-start.8
  100.5 1.2 pad_maximum_fusion
  101.7 9.4 %collective-permute-done.8 = f32[264,128]{1,0:T(8,128)S(1)} collective-permute-done((f32[264,128]{1,0:T(8,128)S(1)}, f32[264,128]{1,0:T(8,128)S(1)}, u32[]{:S(2)}, u32[]{:S(2)}) %collective-permute-start.8) | collective-permute-done | bytes 135200 | tf_op jit(solution)/shard_map/ppermute | solution.py:27
  111.4 1.3 slice_multiply_fusion.8
  112.9 1.0 slice_multiply_fusion.12
  114.0 0.8 slice_multiply_fusion.14
  116.7 2.1 %collective-permute-start.9 = (f32[4,64,128]{2,1,0:T(8,128)S(1)}, f32[4,64,128]{2,1,0:T(8,128)S(1)}, u32[]{:S(2)}, u32[]{:S(2)}) collective-permute-start(f32[4,64,128]{2,1,0:T(8,128)S(1)} %add_select_fusion), channel_id=1, source_target_pairs={{16,0},{32,16},{48,32},{64,48},{80,64},{96,80},{112,96},{128,112},... | collective-permute-start | bytes 393224 | tf_op jit(solution)/shard_map/ppermute | solution.py:27
  118.8 5.3 %collective-permute-done.9 = f32[4,64,128]{2,1,0:T(8,128)S(1)} collective-permute-done((f32[4,64,128]{2,1,0:T(8,128)S(1)}, f32[4,64,128]{2,1,0:T(8,128)S(1)}, u32[]{:S(2)}, u32[]{:S(2)}) %collective-permute-start.9) | collective-permute-done | bytes 131104 | tf_op jit(solution)/shard_map/ppermute | solution.py:27
  124.1 1.9 %collective-permute-start.10 = (f32[4,64,128]{2,1,0:T(8,128)S(1)}, f32[4,64,128]{2,1,0:T(8,128)S(1)}, u32[]{:S(2)}, u32[]{:S(2)}) collective-permute-start(f32[4,64,128]{2,1,0:T(8,128)S(1)} %multiply_add_fusion.4), channel_id=1, source_target_pairs={{32,0},{48,16},{64,32},{80,48},{96,64},{112,80},{128,96},{144,112}... | collective-permute-start | bytes 393224 | tf_op jit(solution)/shard_map/ppermute | solution.py:27
  126.1 7.7 %collective-permute-done.10 = f32[4,64,128]{2,1,0:T(8,128)S(1)} collective-permute-done((f32[4,64,128]{2,1,0:T(8,128)S(1)}, f32[4,64,128]{2,1,0:T(8,128)S(1)}, u32[]{:S(2)}, u32[]{:S(2)}) %collective-permute-start.10) | collective-permute-done | bytes 131104 | tf_op jit(solution)/shard_map/ppermute | solution.py:27
  133.8 1.9 %collective-permute-start.11 = (f32[4,64,128]{2,1,0:T(8,128)S(1)}, f32[4,64,128]{2,1,0:T(8,128)S(1)}, u32[]{:S(2)}, u32[]{:S(2)}) collective-permute-start(f32[4,64,128]{2,1,0:T(8,128)S(1)} %multiply_add_fusion.3), channel_id=1, source_target_pairs={{64,0},{80,16},{96,32},{112,48},{128,64},{144,80},{160,96},{176,11... | collective-permute-start | bytes 393224 | tf_op jit(solution)/shard_map/ppermute | solution.py:27
  135.7 4.9 %collective-permute-done.11 = f32[4,64,128]{2,1,0:T(8,128)S(1)} collective-permute-done((f32[4,64,128]{2,1,0:T(8,128)S(1)}, f32[4,64,128]{2,1,0:T(8,128)S(1)}, u32[]{:S(2)}, u32[]{:S(2)}) %collective-permute-start.11) | collective-permute-done | bytes 131104 | tf_op jit(solution)/shard_map/ppermute | solution.py:27
  140.7 1.9 %collective-permute-start.12 = (f32[4,64,128]{2,1,0:T(8,128)S(1)}, f32[4,64,128]{2,1,0:T(8,128)S(1)}, u32[]{:S(2)}, u32[]{:S(2)}) collective-permute-start(f32[4,64,128]{2,1,0:T(8,128)S(1)} %multiply_add_fusion.2), channel_id=1, source_target_pairs={{128,0},{144,16},{160,32},{176,48},{192,64},{208,80},{224,96},{240... | collective-permute-start | bytes 393224 | tf_op jit(solution)/shard_map/ppermute | solution.py:27
  142.6 9.6 %collective-permute-done.12 = f32[4,64,128]{2,1,0:T(8,128)S(1)} collective-permute-done((f32[4,64,128]{2,1,0:T(8,128)S(1)}, f32[4,64,128]{2,1,0:T(8,128)S(1)}, u32[]{:S(2)}, u32[]{:S(2)}) %collective-permute-start.12) | collective-permute-done | bytes 131104 | tf_op jit(solution)/shard_map/ppermute | solution.py:27
  152.2 1.3 collective-permute-start.13
  153.5 9.5 %collective-permute-done.13 = f32[4,64,128]{2,1,0:T(8,128)S(1)} collective-permute-done((f32[4,64,128]{2,1,0:T(8,128)S(1)}, f32[4,64,128]{2,1,0:T(8,128)S(1)}, u32[]{:S(2)}, u32[]{:S(2)}) %collective-permute-start.13) | collective-permute-done | bytes 131104 | tf_op jit(solution)/shard_map/ppermute | solution.py:27
  164.1 1.1 maximum_add_fusion.1
  (94 shorter events, 10.0 us)
Async XLA Ops:
  0.0 7.4 %copy-start.7 = (f32[1,16,128,128]{3,2,1,0:T(8,128)S(1)}, f32[1,16,128,128]{3,2,1,0:T(8,128)}, u32[]{:S(2)}) copy-start(f32[1,16,128,128]{3,2,1,0:T(8,128)} %param.7) | copy-start | bytes 3145732
  5.2 2.2 %copy-start = (f32[16,128,128]{2,1,0:T(8,128)S(1)}, f32[16,128,128]{2,1,0:T(8,128)}, u32[]{:S(2)}) copy-start(f32[16,128,128]{2,1,0:T(8,128)} %get-tuple-element.15) | copy-start | bytes 3145732
  9.3 19.4 %copy-start.1 = (f32[16,128,128]{2,1,0:T(8,128)}, f32[16,128,128]{2,1,0:T(8,128)S(1)}, u32[]{:S(2)}) copy-start(f32[16,128,128]{2,1,0:T(8,128)S(1)} %get-tuple-element.44) | copy-start | bytes 3145732
  11.8 1.2 copy-start.3
  15.5 0.8 copy-start.8
  16.2 0.8 copy-start.4
  17.1 23.0 %copy-start.6 = (s32[16,128,128]{2,1,0:T(8,128)S(1)}, s32[16,128,128]{2,1,0:T(8,128)}, u32[]{:S(2)}) copy-start(s32[16,128,128]{2,1,0:T(8,128)} %material_ref.1) | copy-start | bytes 3145732
  20.9 30.4 %collective-permute-start.4 = (f32[264,128]{1,0:T(8,128)}, f32[264,128]{1,0:T(8,128)}, u32[]{:S(2)}, u32[]{:S(2)}) collective-permute-start(f32[264,128]{1,0:T(8,128)} %concatenate.63), channel_id=1, source_target_pairs={{16,0},{32,16},{48,32},{64,48},{80,64},{96,80},{112,96},{128,112},... | collective-permute-start | bytes 405512 | tf_op jit(solution)/shard_map/ppermute | solution.py:27
  29.5 71.0 %collective-permute-start = (f32[4,128,128]{2,1,0:T(8,128)}, f32[4,128,128]{2,1,0:T(8,128)}, u32[]{:S(2)}, u32[]{:S(2)}) collective-permute-start(f32[4,128,128]{2,1,0:T(8,128)} %get-tuple-element.57), channel_id=1, source_target_pairs={{0,1},{1,2},{2,3},{3,4},{4,5},{5,6},{6,7},{7,8},{8,9},{9,10},{10,1... | collective-permute-start | bytes 786440 | tf_op jit(solution)/shard_map/ppermute | solution.py:122
  31.4 19.1 %copy-start.9 = (f32[8,1,64,1,128]{4,2,0,3,1:T(8,128)S(1)}, f32[8,1,64,1,128]{4,2,0,3,1:T(8,128)}, u32[]{:S(2)}) copy-start(f32[8,1,64,1,128]{4,2,0,3,1:T(8,128)} %copy-done.8) | copy-start | bytes 786436
  31.4 69.1 %collective-permute-start.1 = (f32[4,128,128]{2,1,0:T(8,128)}, f32[4,128,128]{2,1,0:T(8,128)}, u32[]{:S(2)}, u32[]{:S(2)}) collective-permute-start(f32[4,128,128]{2,1,0:T(8,128)} %get-tuple-element.58), channel_id=1, source_target_pairs={{1,0},{2,1},{3,2},{4,3},{5,4},{6,5},{7,6},{8,7},{9,8},{10,9},{11,1... | collective-permute-start | bytes 786440 | tf_op jit(solution)/shard_map/ppermute | solution.py:123
  40.2 27.8 %collective-permute-start.2 = (f32[4,128,128]{2,1,0:T(8,128)S(1)}, f32[4,128,128]{2,1,0:T(8,128)S(1)}, u32[]{:S(2)}, u32[]{:S(2)}) collective-permute-start(f32[4,128,128]{2,1,0:T(8,128)S(1)} %get-tuple-element.55), channel_id=1, source_target_pairs={{0,1},{1,2},{2,3},{3,4},{4,5},{5,6},{6,7},{7,8},{8,9},{9,10},{10,1... | collective-permute-start | bytes 786440 | tf_op jit(solution)/shard_map/ppermute | solution.py:120
  42.1 25.8 %collective-permute-start.3 = (f32[4,128,128]{2,1,0:T(8,128)S(1)}, f32[4,128,128]{2,1,0:T(8,128)S(1)}, u32[]{:S(2)}, u32[]{:S(2)}) collective-permute-start(f32[4,128,128]{2,1,0:T(8,128)S(1)} %get-tuple-element.56), channel_id=1, source_target_pairs={{1,0},{2,1},{3,2},{4,3},{5,4},{6,5},{7,6},{8,7},{9,8},{10,9},{11,1... | collective-permute-start | bytes 786440 | tf_op jit(solution)/shard_map/ppermute | solution.py:121
  54.2 18.9 %collective-permute-start.5 = (f32[264,128]{1,0:T(8,128)S(1)}, f32[264,128]{1,0:T(8,128)S(1)}, u32[]{:S(2)}, u32[]{:S(2)}) collective-permute-start(f32[264,128]{1,0:T(8,128)S(1)} %concatenate.64), channel_id=1, source_target_pairs={{32,0},{48,16},{64,32},{80,48},{96,64},{112,80},{128,96},{144,112}... | collective-permute-start | bytes 405512 | tf_op jit(solution)/shard_map/ppermute | solution.py:27
  74.4 7.7 %collective-permute-start.6 = (f32[264,128]{1,0:T(8,128)S(1)}, f32[264,128]{1,0:T(8,128)S(1)}, u32[]{:S(2)}, u32[]{:S(2)}) collective-permute-start(f32[264,128]{1,0:T(8,128)S(1)} %concatenate.65), channel_id=1, source_target_pairs={{64,0},{80,16},{96,32},{112,48},{128,64},{144,80},{160,96},{176,11... | collective-permute-start | bytes 405512 | tf_op jit(solution)/shard_map/ppermute | solution.py:27
  83.5 12.5 %collective-permute-start.7 = (f32[264,128]{1,0:T(8,128)S(1)}, f32[264,128]{1,0:T(8,128)S(1)}, u32[]{:S(2)}, u32[]{:S(2)}) collective-permute-start(f32[264,128]{1,0:T(8,128)S(1)} %concatenate.66), channel_id=1, source_target_pairs={{128,0},{144,16},{160,32},{176,48},{192,64},{208,80},{224,96},{240... | collective-permute-start | bytes 405512 | tf_op jit(solution)/shard_map/ppermute | solution.py:27
  96.0 0.7 copy-start.14
  97.9 2.6 %copy-start.2 = (f32[16,128,128]{2,1,0:T(8,128)S(1)}, f32[16,128,128]{2,1,0:T(8,128)}, u32[]{:S(2)}) copy-start(f32[16,128,128]{2,1,0:T(8,128)} %copy-done.1) | copy-start | bytes 3145732
  99.0 12.1 %collective-permute-start.8 = (f32[264,128]{1,0:T(8,128)S(1)}, f32[264,128]{1,0:T(8,128)S(1)}, u32[]{:S(2)}, u32[]{:S(2)}) collective-permute-start(f32[264,128]{1,0:T(8,128)S(1)} %concatenate.67), channel_id=1, source_target_pairs={{256,0},{272,16},{288,32},{304,48},{320,64},{336,80},{352,96},{368... | collective-permute-start | bytes 405512 | tf_op jit(solution)/shard_map/ppermute | solution.py:27
  114.0 0.9 copy-start.11
  114.8 0.8 copy-start.12
  116.7 46.3 %copy-start.10 = (f32[8,1,64,1,128]{4,2,0,3,1:T(8,128)S(1)}, f32[8,1,64,1,128]{4,2,0,3,1:T(8,128)}, u32[]{:S(2)}) copy-start(f32[8,1,64,1,128]{4,2,0,3,1:T(8,128)} %copy-done.8) | copy-start | bytes 786436
  116.7 46.3 %copy-start.13 = (f32[4,64,128]{2,1,0:T(8,128)S(1)}, f32[4,64,128]{2,1,0:T(8,128)}, u32[]{:S(2)}) copy-start(f32[4,64,128]{2,1,0:T(8,128)} %get-tuple-element.36) | copy-start | bytes 393220
  116.7 7.4 %collective-permute-start.9 = (f32[4,64,128]{2,1,0:T(8,128)S(1)}, f32[4,64,128]{2,1,0:T(8,128)S(1)}, u32[]{:S(2)}, u32[]{:S(2)}) collective-permute-start(f32[4,64,128]{2,1,0:T(8,128)S(1)} %add_select_fusion), channel_id=1, source_target_pairs={{16,0},{32,16},{48,32},{64,48},{80,64},{96,80},{112,96},{128,112},... | collective-permute-start | bytes 393224 | tf_op jit(solution)/shard_map/ppermute | solution.py:27
  124.1 9.6 %collective-permute-start.10 = (f32[4,64,128]{2,1,0:T(8,128)S(1)}, f32[4,64,128]{2,1,0:T(8,128)S(1)}, u32[]{:S(2)}, u32[]{:S(2)}) collective-permute-start(f32[4,64,128]{2,1,0:T(8,128)S(1)} %multiply_add_fusion.4), channel_id=1, source_target_pairs={{32,0},{48,16},{64,32},{80,48},{96,64},{112,80},{128,96},{144,112}... | collective-permute-start | bytes 393224 | tf_op jit(solution)/shard_map/ppermute | solution.py:27
  133.8 6.9 %collective-permute-start.11 = (f32[4,64,128]{2,1,0:T(8,128)S(1)}, f32[4,64,128]{2,1,0:T(8,128)S(1)}, u32[]{:S(2)}, u32[]{:S(2)}) collective-permute-start(f32[4,64,128]{2,1,0:T(8,128)S(1)} %multiply_add_fusion.3), channel_id=1, source_target_pairs={{64,0},{80,16},{96,32},{112,48},{128,64},{144,80},{160,96},{176,11... | collective-permute-start | bytes 393224 | tf_op jit(solution)/shard_map/ppermute | solution.py:27
  140.7 11.5 %collective-permute-start.12 = (f32[4,64,128]{2,1,0:T(8,128)S(1)}, f32[4,64,128]{2,1,0:T(8,128)S(1)}, u32[]{:S(2)}, u32[]{:S(2)}) collective-permute-start(f32[4,64,128]{2,1,0:T(8,128)S(1)} %multiply_add_fusion.2), channel_id=1, source_target_pairs={{128,0},{144,16},{160,32},{176,48},{192,64},{208,80},{224,96},{240... | collective-permute-start | bytes 393224 | tf_op jit(solution)/shard_map/ppermute | solution.py:27
  152.2 10.8 %collective-permute-start.13 = (f32[4,64,128]{2,1,0:T(8,128)S(1)}, f32[4,64,128]{2,1,0:T(8,128)S(1)}, u32[]{:S(2)}, u32[]{:S(2)}) collective-permute-start(f32[4,64,128]{2,1,0:T(8,128)S(1)} %multiply_add_fusion.1), channel_id=1, source_target_pairs={{256,0},{272,16},{288,32},{304,48},{320,64},{336,80},{352,96},{368... | collective-permute-start | bytes 393224 | tf_op jit(solution)/shard_map/ppermute | solution.py:27
  163.0 1.0 copy-start.5

commit v8 on v6

--- a/solution.py
+++ b/solution.py
@@ -136,18 +136,21 @@
     top = coarse_decay_rate * coarse_old + reduced
     total = jnp.where(is_last, top, reduced)
     shape = total.shape
-    rows = total.size // shape[-1]
-    power = per_cell
+    width = shape[-1]
+    rows = total.size // width
+    packed = jnp.concatenate(
+        [total.reshape(rows, width), jnp.broadcast_to(gain, (8, width))], axis=0
+    )
+    power = jnp.concatenate([per_cell.reshape(rows, width), jnp.ones((8, width), jnp.float32)], axis=0)
+    is_field = lax.broadcasted_iota(jnp.int32, packed.shape, 0) < rows
     distance = 1
     while distance < tm_size:
-        packed = jnp.concatenate(
-            [total.reshape(rows, shape[-1]), jnp.broadcast_to(gain, (8, shape[-1]))], axis=0
-        )
         arrived = shifted(packed, "tm", -distance)
-        total = total + (power * gain) * arrived[:rows].reshape(shape)
-        gain = gain * arrived[rows, 0]
+        own_gain = packed[rows, 0]
+        packed = jnp.where(is_field, packed + (power * own_gain) * arrived, packed * arrived)
         power = power * power
         distance *= 2
+    total = packed[:rows].reshape(shape)
     decayed = jnp.where(is_last, coarse_decay_rate * coarse_old, total - reduced)
     adjoint_new = refine(decayed) + correction
     return adjoint_new[None]

time: 130 us -> 126 us (0.969)
  the two profiles are of different devices: /device:TPU:478 before, /device:TPU:466 now
where the time goes in v8:
time: 126 us; the launch traced here: 125 us
  waiting for transfers between devices  59.6 us (47%)
  starting transfers between devices  28.8 us (23%)
  other arithmetic  17.6 us (14%)
  local copies, waits for them, and re-layouts  11.8 us (9%)
  Pallas kernels  6.06 us (5%)
    ppermute x5, waiting for transfers between devices, shifted(): lax.ppermute(value, axis, [(source, source + steps) for source in range(i...  59.6 us
    ppermute x5, starting transfers between devices, shifted(): lax.ppermute(value, axis, [(source, source + steps) for source in range(i...  9.92 us
    ppermute x1, starting transfers between devices, on_device(): material_next = lax.ppermute(material_f[:halo], 'space', down)  7.55 us
    ppermute x1, starting transfers between devices, on_device(): seeded_next = lax.ppermute(seeded[:halo], 'space', down)  7.55 us
    pallas_call x2, Pallas kernels, lookup_both(): pl.pallas_call(_lookup_kernel, grid=(planes // block[0],), in_specs=[smem...  6.06 us
    mul x4, other arithmetic, on_device(): weighted = cond_ext[lo:hi] * current  5.28 us
    slice x2, local copies, waits for them, and re-layouts, coarsen(): split[:, 1, :, 0]  4.52 us
    select_n x5, other arithmetic, on_device(): jnp.where(is_field, packed + power * own_gain * arrived, packed * arrived)  3.32 us
  transfers between devices with their start and end apart: 9, of which 5 were waited for; matrix products, arithmetic and copies ran while one was open for 11% of the time, Pallas kernels for 5%

profile of v8, /device:TPU:466, one launch (start us, length us, event | category | flops | bytes accessed | tf_op | source)
XLA Modules:
  0.0 125.0 jit_solution(5629352570317471585)
XLA Ops:
  0.0 1.3 %convert_element_type.14 = f32[16,128,128]{2,1,0:T(8,128)S(1)} convert(s32[16,128,128]{2,1,0:T(8,128)} %material_ref.1) | non-fusion elementwise | flops 262144 | bytes 2097152 | tf_op jit(solution)/shard_map/convert_element_type | solution.py:100
  1.3 0.8 fusion.41
  2.2 1.9 %collective-permute-start.2 = (f32[4,128,128]{2,1,0:T(8,128)}, f32[4,128,128]{2,1,0:T(8,128)}, u32[]{:S(2)}, u32[]{:S(2)}) collective-permute-start(f32[4,128,128]{2,1,0:T(8,128)} %get-tuple-element.24), channel_id=1, source_target_pairs={{0,1},{1,2},{2,3},{3,4},{4,5},{5,6},{6,7},{7,8},{8,9},{9,10},{10,1... | collective-permute-start | bytes 786440 | tf_op jit(solution)/shard_map/ppermute | solution.py:101
  4.1 7.6 %collective-permute-start.3 = (f32[4,128,128]{2,1,0:T(8,128)}, f32[4,128,128]{2,1,0:T(8,128)}, u32[]{:S(2)}, u32[]{:S(2)}) collective-permute-start(f32[4,128,128]{2,1,0:T(8,128)} %get-tuple-element.25), channel_id=1, source_target_pairs={{1,0},{2,1},{3,2},{4,3},{5,4},{6,5},{7,6},{8,7},{9,8},{10,9},{11,1... | collective-permute-start | bytes 786440 | tf_op jit(solution)/shard_map/ppermute | solution.py:102
  11.7 1.3 %scatter_custom_fusion = f32[262144]{0:T(1024)S(1)} fusion(s32[64]{0:T(128)S(1)} %compare_select_fusion, f32[64]{0:T(128)} %bitcast.63, f32[]{:T(128)} %constant.22.clone.1), kind=kCustom, calls=%fused_computation.63 | custom fusion | flops 64 | bytes 1049088 | tf_op jit(solution)/shard_map/scatter-add | solution.py:92
  13.0 0.1 bitcast_add_fusion
  13.1 0.8 fusion.42
  14.0 1.9 %collective-permute-start = (f32[4,128,128]{2,1,0:T(8,128)}, f32[4,128,128]{2,1,0:T(8,128)}, u32[]{:S(2)}, u32[]{:S(2)}) collective-permute-start(f32[4,128,128]{2,1,0:T(8,128)} %get-tuple-element.26), channel_id=1, source_target_pairs={{0,1},{1,2},{2,3},{3,4},{4,5},{5,6},{6,7},{7,8},{8,9},{9,10},{10,1... | collective-permute-start | bytes 786440 | tf_op jit(solution)/shard_map/ppermute | solution.py:103
  15.9 7.6 %collective-permute-start.1 = (f32[4,128,128]{2,1,0:T(8,128)}, f32[4,128,128]{2,1,0:T(8,128)}, u32[]{:S(2)}, u32[]{:S(2)}) collective-permute-start(f32[4,128,128]{2,1,0:T(8,128)} %get-tuple-element.27), channel_id=1, source_target_pairs={{1,0},{2,1},{3,2},{4,3},{5,4},{6,5},{7,6},{8,7},{9,8},{10,9},{11,1... | collective-permute-start | bytes 786440 | tf_op jit(solution)/shard_map/ppermute | solution.py:104
  24.1 3.9 %shard_map.73 = (f32[16,128,128]{2,1,0:T(8,128)}, f32[16,128,128]{2,1,0:T(8,128)}) custom-call(f32[8]{0:T(128)} %cond_table.3, f32[8]{0:T(128)} %drain_table.3, s32[16,128,128]{2,1,0:T(8,128)} %material_ref.1), custom_call_target="tpu_custom_call" | custom-call | tf_op jit(solution)/shard_map/pallas_call | solution.py:66
  28.0 2.6 %fusion.43 = (f32[8,1,64,1,128]{4,3,2,1,0:T(1,128)S(1)}, f32[8,1,64,1,128]{4,3,2,1,0:T(1,128)S(1)}, f32[8,1,64,1,128]{4,3,2,1,0:T(1,128)S(1)}, f32[8,1,64,1,128]{4,3,2,1,0:T(1,128)S(1)}) fusion(f32[8,2,64,2,128]{4,3,2,1,0:T(2,128)} %bitcast.47), kind=kLoop, calls=%fused_computation.91 | loop fusion | bytes 2097152 | tf_op jit(solution)/shard_map/slice | solution.py:32
  30.6 1.9 %fusion.44 = (f32[8,1,64,1,128]{4,3,2,1,0:T(1,128)}, f32[8,1,64,1,128]{4,3,2,1,0:T(1,128)}, f32[8,1,64,1,128]{4,3,2,1,0:T(1,128)}, f32[8,1,64,1,128]{4,3,2,1,0:T(1,128)}) fusion(f32[8,2,64,2,128]{4,3,2,1,0:T(2,128)S(1)} %bitcast.43), kind=kLoop, calls=%fused_computation.92 | loop fusion | bytes 2097152 | tf_op jit(solution)/shard_map/slice | solution.py:32
  32.5 1.4 %exponential_multiply_fusion = (f32[8,1,64,1,128]{4,2,0,3,1:T(8,128)S(1)}, f32[8,1,64,1,128]{4,2,0,3,1:T(8,128)S(1)}) fusion(f32[8,1,64,1,128]{4,2,0,3,1:T(8,128)} %bitcast.60, f32[8,1,64,1,128]{4,2,0,3,1:T(8,128)} %bitcast.62, f32[8,1,64,1,128]{4,2,0,3,1:T(8,128)} %bitcast.61, f32[8,1,64,1,128]{4,2,0,3,1:T(8,128)} %bitcast.59, f32[]{:T(128)} %bitcast.35, ...), kind=kLoop, calls=%fused_computation.79 | loop fusion | flops 720896 | bytes 2621444 | tf_op jit(solution)/shard_map/mul | solution.py:154
  33.9 2.0 %maximum_convert_fusion.material_ref = s32[8,128,128]{2,1,0:T(8,128)} fusion(f32[4,128,128]{2,1,0:T(8,128)} %collective-permute-done.3, f32[4,128,128]{2,1,0:T(8,128)} %collective-permute-done.2), kind=kLoop, calls=%fused_computation.62 | loop fusion | flops 262144 | bytes 1048576 | tf_op jit(solution)/shard_map/convert_element_type | solution.py:106
  35.9 2.2 %shard_map.74 = (f32[8,128,128]{2,1,0:T(8,128)}, f32[8,128,128]{2,1,0:T(8,128)}) custom-call(f32[8]{0:T(128)} %cond_table.3, f32[8]{0:T(128)} %drain_table.3, s32[8,128,128]{2,1,0:T(8,128)} %maximum_convert_fusion.material_ref), custom_call_target="tpu_custom_call" | custom-call | tf_op jit(solution)/shard_map/pallas_call | solution.py:66
  38.1 1.1 fusion.46
  39.2 1.4 %fusion.37 = (f32[24,128,128]{2,1,0:T(8,128)S(1)}, f32[24,128,128]{2,1,0:T(8,128)S(1)}, f32[24,128,128]{2,1,0:T(8,128)S(1)}) fusion(f32[4,128,128]{2,1,0:T(8,128)} %collective-permute-done.1, f32[16,128,128]{2,1,0:T(8,128)S(1)} %bitcast_add_fusion, f32[4,128,128]{2,1,0:T(8,128)} %collective-permute-done, f32[4,128,128]{2,1,0:T(8,128)S(1)} %get-tuple-element.39, ...), kind=kLoop, calls=%fused_computation.88 | loop fusion | flops 2359296 | bytes 7864344 | tf_op jit(solution)/shard_map/mul | solution.py:118
  40.6 0.1 slice.272
  40.8 0.9 copy-done.3
  41.7 0.3 copy-done.1
  42.0 0.2 maximum_add_fusion
  42.2 1.4 %slice_multiply_fusion = (f32[22,128,128]{2,1,0:T(8,128)S(1)}, f32[22,128,128]{2,1,0:T(8,128)S(1)}) fusion(f32[24,128,128]{2,1,0:T(8,128)S(1)} %get-tuple-element.20, f32[24,128,128]{2,1,0:T(8,128)S(1)} %maximum_add_fusion, f32[22,128,128]{2,1,0:T(8,128)S(1)} %slice.272, f32[24,128,128]{2,1,0:T(8,128)S(1)} %get-tuple-element.19, ...), kind=kLoop, calls=%fused_computation.27 | loop fusion | flops 3964928 | bytes 11534336 | tf_op jit(solution)/shard_map/mul | solution.py:118
  43.7 1.3 %slice_multiply_fusion.2 = (f32[20,128,128]{2,1,0:T(8,128)S(1)}, f32[20,128,128]{2,1,0:T(8,128)S(1)}) fusion(f32[24,128,128]{2,1,0:T(8,128)S(1)} %get-tuple-element.20, f32[24,128,128]{2,1,0:T(8,128)S(1)} %maximum_add_fusion, f32[20,128,128]{2,1,0:T(8,128)S(1)} %slice.278, f32[22,128,128]{2,1,0:T(8,128)S(1)} %get-tuple-element.17, ...), kind=kLoop, calls=%fused_computation.37 | loop fusion | flops 3604480 | bytes 10485760 | tf_op jit(solution)/shard_map/mul | solution.py:118
  45.1 1.2 slice_multiply_fusion.4
  46.5 0.4 broadcast_in_dim.41
  46.8 0.9 fusion.27
  47.7 0.6 fusion.36
  48.4 2.5 %collective-permute-start.4 = (f32[520,128]{1,0:T(8,128)S(1)}, f32[520,128]{1,0:T(8,128)S(1)}, u32[]{:S(2)}, u32[]{:S(2)}) collective-permute-start(f32[520,128]{1,0:T(8,128)S(1)} %concatenate.22), channel_id=1, source_target_pairs={{16,0},{32,16},{48,32},{64,48},{80,64},{96,80},{112,96},{128,112},... | collective-permute-start | bytes 798728 | tf_op jit(solution)/shard_map/ppermute | solution.py:27
  50.9 10.4 %collective-permute-done.4 = f32[520,128]{1,0:T(8,128)S(1)} collective-permute-done((f32[520,128]{1,0:T(8,128)S(1)}, f32[520,128]{1,0:T(8,128)S(1)}, u32[]{:S(2)}, u32[]{:S(2)}) %collective-permute-start.4) | collective-permute-done | bytes 266272 | tf_op jit(solution)/shard_map/ppermute | solution.py:27
  61.3 0.1 multiply_select_fusion.3
  61.4 1.9 %collective-permute-start.5 = (f32[520,128]{1,0:T(8,128)S(1)}, f32[520,128]{1,0:T(8,128)S(1)}, u32[]{:S(2)}, u32[]{:S(2)}) collective-permute-start(f32[520,128]{1,0:T(8,128)S(1)} %multiply_select_fusion.3), channel_id=1, source_target_pairs={{32,0},{48,16},{64,32},{80,48},{96,64},{112,80},{128,96},{144,112}... | collective-permute-start | bytes 798728 | tf_op jit(solution)/shard_map/ppermute | solution.py:27
  63.4 0.5 slice.296
  63.9 10.3 %collective-permute-done.5 = f32[520,128]{1,0:T(8,128)S(1)} collective-permute-done((f32[520,128]{1,0:T(8,128)S(1)}, f32[520,128]{1,0:T(8,128)S(1)}, u32[]{:S(2)}, u32[]{:S(2)}) %collective-permute-start.5) | collective-permute-done | bytes 266272 | tf_op jit(solution)/shard_map/ppermute | solution.py:27
  74.2 0.8 multiply_select_fusion.2
  75.0 2.3 %collective-permute-start.6 = (f32[520,128]{1,0:T(8,128)S(1)}, f32[520,128]{1,0:T(8,128)S(1)}, u32[]{:S(2)}, u32[]{:S(2)}) collective-permute-start(f32[520,128]{1,0:T(8,128)S(1)} %multiply_select_fusion.2), channel_id=1, source_target_pairs={{64,0},{80,16},{96,32},{112,48},{128,64},{144,80},{160,96},{176,11... | collective-permute-start | bytes 798728 | tf_op jit(solution)/shard_map/ppermute | solution.py:27
  77.3 0.5 slice.297
  77.8 12.1 %collective-permute-done.6 = f32[520,128]{1,0:T(8,128)S(1)} collective-permute-done((f32[520,128]{1,0:T(8,128)S(1)}, f32[520,128]{1,0:T(8,128)S(1)}, u32[]{:S(2)}, u32[]{:S(2)}) %collective-permute-start.6) | collective-permute-done | bytes 266272 | tf_op jit(solution)/shard_map/ppermute | solution.py:27
  89.9 0.8 multiply_select_fusion.1
  90.7 1.9 %collective-permute-start.7 = (f32[520,128]{1,0:T(8,128)S(1)}, f32[520,128]{1,0:T(8,128)S(1)}, u32[]{:S(2)}, u32[]{:S(2)}) collective-permute-start(f32[520,128]{1,0:T(8,128)S(1)} %multiply_select_fusion.1), channel_id=1, source_target_pairs={{128,0},{144,16},{160,32},{176,48},{192,64},{208,80},{224,96},{240... | collective-permute-start | bytes 798728 | tf_op jit(solution)/shard_map/ppermute | solution.py:27
  92.6 0.5 slice.298
  93.1 16.5 %collective-permute-done.7 = f32[520,128]{1,0:T(8,128)S(1)} collective-permute-done((f32[520,128]{1,0:T(8,128)S(1)}, f32[520,128]{1,0:T(8,128)S(1)}, u32[]{:S(2)}, u32[]{:S(2)}) %collective-permute-start.7) | collective-permute-done | bytes 266272 | tf_op jit(solution)/shard_map/ppermute | solution.py:27
  109.7 0.8 multiply_select_fusion
  110.5 1.3 %collective-permute-start.8 = (f32[520,128]{1,0:T(8,128)S(1)}, f32[520,128]{1,0:T(8,128)S(1)}, u32[]{:S(2)}, u32[]{:S(2)}) collective-permute-start(f32[520,128]{1,0:T(8,128)S(1)} %get-tuple-element.40), channel_id=1, source_target_pairs={{256,0},{272,16},{288,32},{304,48},{320,64},{336,80},{352,96},{368... | collective-permute-start | bytes 798728 | tf_op jit(solution)/shard_map/ppermute | solution.py:27
  111.8 0.5 slice.299
  112.3 10.4 %collective-permute-done.8 = f32[520,128]{1,0:T(8,128)S(1)} collective-permute-done((f32[520,128]{1,0:T(8,128)S(1)}, f32[520,128]{1,0:T(8,128)S(1)}, u32[]{:S(2)}, u32[]{:S(2)}) %collective-permute-start.8) | collective-permute-done | bytes 266272 | tf_op jit(solution)/shard_map/ppermute | solution.py:27
  122.7 0.8 fusion.34
  123.6 0.4 broadcast_in_dim.43
  124.0 1.1 add_bitcast_fusion
  (27 shorter events, 0.7 us)
Async XLA Ops:
  0.0 11.7 %copy-start.4 = (s32[64]{0:T(128)S(1)}, s32[64]{0:T(128)}, u32[]{:S(2)}) copy-start(s32[64]{0:T(128)} %param.9) | copy-start | bytes 772
  1.3 11.7 %copy-start = (f32[1,16,128,128]{3,2,1,0:T(8,128)S(1)}, f32[1,16,128,128]{3,2,1,0:T(8,128)}, u32[]{:S(2)}) copy-start(f32[1,16,128,128]{3,2,1,0:T(8,128)} %param.7) | copy-start | bytes 3145732
  2.2 31.7 %collective-permute-start.2 = (f32[4,128,128]{2,1,0:T(8,128)}, f32[4,128,128]{2,1,0:T(8,128)}, u32[]{:S(2)}, u32[]{:S(2)}) collective-permute-start(f32[4,128,128]{2,1,0:T(8,128)} %get-tuple-element.24), channel_id=1, source_target_pairs={{0,1},{1,2},{2,3},{3,4},{4,5},{5,6},{6,7},{7,8},{8,9},{9,10},{10,1... | collective-permute-start | bytes 786440 | tf_op jit(solution)/shard_map/ppermute | solution.py:101
  4.1 29.8 %collective-permute-start.3 = (f32[4,128,128]{2,1,0:T(8,128)}, f32[4,128,128]{2,1,0:T(8,128)}, u32[]{:S(2)}, u32[]{:S(2)}) collective-permute-start(f32[4,128,128]{2,1,0:T(8,128)} %get-tuple-element.25), channel_id=1, source_target_pairs={{1,0},{2,1},{3,2},{4,3},{5,4},{6,5},{7,6},{8,7},{9,8},{10,9},{11,1... | collective-permute-start | bytes 786440 | tf_op jit(solution)/shard_map/ppermute | solution.py:102
  14.0 25.2 %collective-permute-start = (f32[4,128,128]{2,1,0:T(8,128)}, f32[4,128,128]{2,1,0:T(8,128)}, u32[]{:S(2)}, u32[]{:S(2)}) collective-permute-start(f32[4,128,128]{2,1,0:T(8,128)} %get-tuple-element.26), channel_id=1, source_target_pairs={{0,1},{1,2},{2,3},{3,4},{4,5},{5,6},{6,7},{7,8},{8,9},{9,10},{10,1... | collective-permute-start | bytes 786440 | tf_op jit(solution)/shard_map/ppermute | solution.py:103
  15.9 23.3 %collective-permute-start.1 = (f32[4,128,128]{2,1,0:T(8,128)}, f32[4,128,128]{2,1,0:T(8,128)}, u32[]{:S(2)}, u32[]{:S(2)}) collective-permute-start(f32[4,128,128]{2,1,0:T(8,128)} %get-tuple-element.27), channel_id=1, source_target_pairs={{1,0},{2,1},{3,2},{4,3},{5,4},{6,5},{7,6},{8,7},{9,8},{10,9},{11,1... | collective-permute-start | bytes 786440 | tf_op jit(solution)/shard_map/ppermute | solution.py:104
  33.9 5.3 %copy-start.2 = (f32[16,128,128]{2,1,0:T(8,128)S(1)}, f32[16,128,128]{2,1,0:T(8,128)}, u32[]{:S(2)}) copy-start(f32[16,128,128]{2,1,0:T(8,128)} %get-tuple-element.11) | copy-start | bytes 3145732
  40.6 1.0 copy-start.3
  40.6 1.4 %copy-start.1 = (f32[16,128,128]{2,1,0:T(8,128)S(1)}, f32[16,128,128]{2,1,0:T(8,128)}, u32[]{:S(2)}) copy-start(f32[16,128,128]{2,1,0:T(8,128)} %get-tuple-element.9) | copy-start | bytes 3145732
  48.4 12.9 %collective-permute-start.4 = (f32[520,128]{1,0:T(8,128)S(1)}, f32[520,128]{1,0:T(8,128)S(1)}, u32[]{:S(2)}, u32[]{:S(2)}) collective-permute-start(f32[520,128]{1,0:T(8,128)S(1)} %concatenate.22), channel_id=1, source_target_pairs={{16,0},{32,16},{48,32},{64,48},{80,64},{96,80},{112,96},{128,112},... | collective-permute-start | bytes 798728 | tf_op jit(solution)/shard_map/ppermute | solution.py:27
  61.4 12.7 %collective-permute-start.5 = (f32[520,128]{1,0:T(8,128)S(1)}, f32[520,128]{1,0:T(8,128)S(1)}, u32[]{:S(2)}, u32[]{:S(2)}) collective-permute-start(f32[520,128]{1,0:T(8,128)S(1)} %multiply_select_fusion.3), channel_id=1, source_target_pairs={{32,0},{48,16},{64,32},{80,48},{96,64},{112,80},{128,96},{144,112}... | collective-permute-start | bytes 798728 | tf_op jit(solution)/shard_map/ppermute | solution.py:27
  75.0 14.9 %collective-permute-start.6 = (f32[520,128]{1,0:T(8,128)S(1)}, f32[520,128]{1,0:T(8,128)S(1)}, u32[]{:S(2)}, u32[]{:S(2)}) collective-permute-start(f32[520,128]{1,0:T(8,128)S(1)} %multiply_select_fusion.2), channel_id=1, source_target_pairs={{64,0},{80,16},{96,32},{112,48},{128,64},{144,80},{160,96},{176,11... | collective-permute-start | bytes 798728 | tf_op jit(solution)/shard_map/ppermute | solution.py:27
  90.7 19.0 %collective-permute-start.7 = (f32[520,128]{1,0:T(8,128)S(1)}, f32[520,128]{1,0:T(8,128)S(1)}, u32[]{:S(2)}, u32[]{:S(2)}) collective-permute-start(f32[520,128]{1,0:T(8,128)S(1)} %multiply_select_fusion.1), channel_id=1, source_target_pairs={{128,0},{144,16},{160,32},{176,48},{192,64},{208,80},{224,96},{240... | collective-permute-start | bytes 798728 | tf_op jit(solution)/shard_map/ppermute | solution.py:27
  110.5 12.2 %collective-permute-start.8 = (f32[520,128]{1,0:T(8,128)S(1)}, f32[520,128]{1,0:T(8,128)S(1)}, u32[]{:S(2)}, u32[]{:S(2)}) collective-permute-start(f32[520,128]{1,0:T(8,128)S(1)} %get-tuple-element.40), channel_id=1, source_target_pairs={{256,0},{272,16},{288,32},{304,48},{320,64},{336,80},{352,96},{368... | collective-permute-start | bytes 798728 | tf_op jit(solution)/shard_map/ppermute | solution.py:27

commit v9 on v8

--- a/solution.py
+++ b/solution.py
@@ -6,19 +6,6 @@
 from jax.sharding import PartitionSpec as P
 
 FINE_STEPS = 4
-
-
-def padded_2(value, sides, width):
-    for axis, dim in sides:
-        size, length = (lax.axis_size(axis), value.shape[dim])
-        up = [(i, (i + 1) % size) for i in range(size - 1)]
-        down = [(j, i) for i, j in up]
-        last = lax.slice_in_dim(value, length - width, length, axis=dim)
-        initial = lax.slice_in_dim(value, 0, width, axis=dim)
-        before = lax.ppermute(last, axis, up)
-        after = lax.ppermute(initial, axis, down)
-        value = jnp.concatenate([before, value, after], axis=dim)
-    return value
 
 
 def shifted(value, axis, steps):
@@ -34,13 +21,6 @@
 
 def refine(coarse):
     return jnp.repeat(jnp.repeat(coarse, 2, axis=0), 2, axis=1)
-
-
-def neighbours(padded):
-    x_sides = padded[2:, 1:-1, 1:-1] + padded[:-2, 1:-1, 1:-1]
-    y_sides = padded[1:-1, 2:, 1:-1] + padded[1:-1, :-2, 1:-1]
-    z_sides = padded[1:-1, 1:-1, 2:] + padded[1:-1, 1:-1, :-2]
-    return x_sides + y_sides + z_sides
 
 
 def _select_tree(material, table_ref):
@@ -99,10 +79,19 @@
     down = [(i + 1, i) for i in range(space_size - 1)]
     material_f = material.astype(jnp.float32)
     material_prev = lax.ppermute(material_f[-halo:], "space", up)
-    material_next = lax.ppermute(material_f[:halo], "space", down)
+    cond_own, drain_own = lookup_both(material, conductance, rock_heat_drain)
+    material_low, cond_own, drain_own = lax.optimization_barrier(
+        (material_f[:halo], cond_own, drain_own)
+    )
+    material_next = lax.ppermute(material_low, "space", down)
     seeded_prev = lax.ppermute(seeded[-halo:], "space", up)
-    seeded_next = lax.ppermute(seeded[:halo], "space", down)
-    cond_own, drain_own = lookup_both(material, conductance, rock_heat_drain)
+    coarse_baseline = coarsen(drain_own)
+    coarse_decay_rate = jnp.exp(-FINE_STEPS * (coarse_baseline + ventilation_heat_loss[0]))
+    coarse_old = coarsen(adjoint)
+    seeded_low, coarse_baseline, coarse_decay_rate, coarse_old = lax.optimization_barrier(
+        (seeded[:halo], coarse_baseline, coarse_decay_rate, coarse_old)
+    )
+    seeded_next = lax.ppermute(seeded_low, "space", down)
     halo_material = jnp.concatenate([material_prev, material_next], axis=0).astype(jnp.int32)
     cond_halo, drain_halo = lookup_both(halo_material, conductance, rock_heat_drain)
     current = jnp.concatenate([seeded_prev, seeded, seeded_next], axis=0)
@@ -123,10 +112,6 @@
         z_sides = padded[:, 1:-1, 2:] + padded[:, 1:-1, :-2]
         kept = current[1:-1]
         current = kept + ((x_sides + y_sides + z_sides) - 6.0 * inner) - losses_ext[lo + 1 : hi - 1] * kept
-    cell_heat_drain = drain_own
-    coarse_baseline = coarsen(cell_heat_drain)
-    coarse_decay_rate = jnp.exp(-FINE_STEPS * (coarse_baseline + ventilation_heat_loss[0]))
-    coarse_old = coarsen(adjoint)
     correction = current - refine(coarse_decay_rate * coarse_old)
     reduced = coarsen(correction)
     tm_size = lax.axis_size("tm")
@@ -167,6 +152,7 @@
         P(),
     )
     out_specs = P("tm", "space", None, None)
+
     return jax.shard_map(
         on_device, mesh=mesh, in_specs=in_specs, out_specs=out_specs, check_vma=False
     )

time: 126 us -> 134 us (1.063)
  the two profiles are of different devices: /device:TPU:466 before, /device:TPU:212 now
where the time goes in v9:
time: 134 us; the launch traced here: 133 us
  waiting for transfers between devices  67.3 us (50%)
  starting transfers between devices  29.5 us (22%)
  other arithmetic  15.3 us (11%)
  local copies, waits for them, and re-layouts  13.7 us (10%)
  Pallas kernels  6.18 us (5%)
    ppermute x5, waiting for transfers between devices, shifted(): lax.ppermute(value, axis, [(source, source + steps) for source in range(i...  59 us
    ppermute x5, starting transfers between devices, shifted(): lax.ppermute(value, axis, [(source, source + steps) for source in range(i...  9.59 us
    ppermute x1, starting transfers between devices, on_device(): seeded_next = lax.ppermute(seeded_low, 'space', down)  8.44 us
    ppermute x1, waiting for transfers between devices, on_device(): seeded_prev = lax.ppermute(seeded[-halo:], 'space', up)  8.28 us
    ppermute x1, starting transfers between devices, on_device(): material_next = lax.ppermute(material_low, 'space', down)  7.62 us
    pallas_call x2, Pallas kernels, lookup_both(): pl.pallas_call(_lookup_kernel, grid=(planes // block[0],), in_specs=[smem...  6.18 us
    slice x2, local copies, waits for them, and re-layouts, coarsen(): split[:, 1, :, 0]  5.28 us
    mul x4, other arithmetic, on_device(): weighted = cond_ext[lo:hi] * current  4.2 us
  transfers between devices with their start and end apart: 9, of which 6 were waited for; matrix products, arithmetic and copies ran while one was open for 10% of the time, Pallas kernels for 2%

profile of v9, /device:TPU:212, one launch (start us, length us, event | category | flops | bytes accessed | tf_op | source)
XLA Modules:
  0.0 133.2 jit_solution(16122149772390261971)
XLA Ops:
  0.0 1.3 convert_element_type.14
  1.3 0.8 fusion.41
  2.2 3.9 %shard_map.73 = (f32[16,128,128]{2,1,0:T(8,128)}, f32[16,128,128]{2,1,0:T(8,128)}) custom-call(f32[8]{0:T(128)} %cond_table.3, f32[8]{0:T(128)} %drain_table.3, s32[16,128,128]{2,1,0:T(8,128)} %material_ref.1), custom_call_target="tpu_custom_call" | custom-call | tf_op jit(solution)/shard_map/pallas_call | solution.py:46
  6.1 7.6 %collective-permute-start.3 = (f32[4,128,128]{2,1,0:T(8,128)}, f32[4,128,128]{2,1,0:T(8,128)}, u32[]{:S(2)}, u32[]{:S(2)}) collective-permute-start(f32[4,128,128]{2,1,0:T(8,128)} %get-tuple-element.22), channel_id=1, source_target_pairs={{1,0},{2,1},{3,2},{4,3},{5,4},{6,5},{7,6},{8,7},{9,8},{10,9},{11,1... | collective-permute-start | bytes 786440 | tf_op jit(solution)/shard_map/ppermute | solution.py:86
  13.7 1.9 %collective-permute-start.2 = (f32[4,128,128]{2,1,0:T(8,128)}, f32[4,128,128]{2,1,0:T(8,128)}, u32[]{:S(2)}, u32[]{:S(2)}) collective-permute-start(f32[4,128,128]{2,1,0:T(8,128)} %get-tuple-element.38), channel_id=1, source_target_pairs={{0,1},{1,2},{2,3},{3,4},{4,5},{5,6},{6,7},{7,8},{8,9},{9,10},{10,1... | collective-permute-start | bytes 786440 | tf_op jit(solution)/shard_map/ppermute | solution.py:81
  15.7 3.5 %fusion.44 = (f32[8,1,64,1,128]{4,3,2,1,0:T(1,128)}, f32[8,1,64,1,128]{4,3,2,1,0:T(1,128)}, f32[8,1,64,1,128]{4,3,2,1,0:T(1,128)}, f32[8,1,64,1,128]{4,3,2,1,0:T(1,128)}) fusion(f32[8,2,64,2,128]{4,3,2,1,0:T(2,128)} %bitcast.48), kind=kLoop, calls=%fused_computation.93 | loop fusion | bytes 2097152 | tf_op jit(solution)/shard_map/slice | solution.py:19
  19.9 1.8 %fusion.43 = (f32[8,1,64,1,128]{4,3,2,1,0:T(1,128)S(1)}, f32[8,1,64,1,128]{4,3,2,1,0:T(1,128)}, f32[8,1,64,1,128]{4,3,2,1,0:T(1,128)}, f32[8,1,64,1,128]{4,3,2,1,0:T(1,128)}) fusion(f32[8,2,64,2,128]{4,3,2,1,0:T(2,128)S(1)} %bitcast.44), kind=kLoop, calls=%fused_computation.92 | loop fusion | bytes 2097152 | tf_op jit(solution)/shard_map/slice | solution.py:19
  21.6 1.3 scatter_custom_fusion
  23.2 0.7 copy-done.3
  24.5 0.8 fusion.42
  25.3 8.4 %collective-permute-start.1 = (f32[4,128,128]{2,1,0:T(8,128)}, f32[4,128,128]{2,1,0:T(8,128)S(1)}, u32[]{:S(2)}, u32[]{:S(2)}) collective-permute-start(f32[4,128,128]{2,1,0:T(8,128)} %get-tuple-element.21), channel_id=1, source_target_pairs={{1,0},{2,1},{3,2},{4,3},{5,4},{6,5},{7,6},{8,7},{9,8},{10,9},{11,1... | collective-permute-start | bytes 786440 | tf_op jit(solution)/shard_map/ppermute | solution.py:94
  33.7 1.9 %collective-permute-start = (f32[4,128,128]{2,1,0:T(8,128)S(1)}, f32[4,128,128]{2,1,0:T(8,128)S(1)}, u32[]{:S(2)}, u32[]{:S(2)}) collective-permute-start(f32[4,128,128]{2,1,0:T(8,128)S(1)} %get-tuple-element.40), channel_id=1, source_target_pairs={{0,1},{1,2},{2,3},{3,4},{4,5},{5,6},{6,7},{7,8},{8,9},{9,10},{10,1... | collective-permute-start | bytes 786440 | tf_op jit(solution)/shard_map/ppermute | solution.py:87
  35.8 2.0 %maximum_convert_fusion.material_ref = s32[8,128,128]{2,1,0:T(8,128)} fusion(f32[4,128,128]{2,1,0:T(8,128)} %collective-permute-done.3, f32[4,128,128]{2,1,0:T(8,128)} %collective-permute-done.2), kind=kLoop, calls=%fused_computation.62 | loop fusion | flops 262144 | bytes 1048576 | tf_op jit(solution)/shard_map/convert_element_type | solution.py:95
  37.7 2.2 %shard_map.74 = (f32[8,128,128]{2,1,0:T(8,128)}, f32[8,128,128]{2,1,0:T(8,128)}) custom-call(f32[8]{0:T(128)} %cond_table.3, f32[8]{0:T(128)} %drain_table.3, s32[8,128,128]{2,1,0:T(8,128)} %maximum_convert_fusion.material_ref), custom_call_target="tpu_custom_call" | custom-call | tf_op jit(solution)/shard_map/pallas_call | solution.py:46
  40.0 1.1 fusion.46
  41.1 8.3 %collective-permute-done = f32[4,128,128]{2,1,0:T(8,128)S(1)} collective-permute-done((f32[4,128,128]{2,1,0:T(8,128)S(1)}, f32[4,128,128]{2,1,0:T(8,128)S(1)}, u32[]{:S(2)}, u32[]{:S(2)}) %collective-permute-start) | collective-permute-done | bytes 262176 | tf_op jit(solution)/shard_map/ppermute | solution.py:87
  49.3 0.3 fusion.37
  49.7 0.1 slice.272
  49.9 0.9 copy-done.10
  50.8 0.3 copy-done.1
  51.1 0.1 maximum_add_fusion
  51.2 1.4 %slice_multiply_fusion = (f32[22,128,128]{2,1,0:T(8,128)S(1)}, f32[22,128,128]{2,1,0:T(8,128)S(1)}) fusion(f32[24,128,128]{2,1,0:T(8,128)S(1)} %get-tuple-element.34, f32[24,128,128]{2,1,0:T(8,128)S(1)} %maximum_add_fusion, f32[22,128,128]{2,1,0:T(8,128)S(1)} %slice.272, f32[24,128,128]{2,1,0:T(8,128)S(1)} %get-tuple-element.33, ...), kind=kLoop, calls=%fused_computation.27 | loop fusion | flops 3964928 | bytes 11534336 | tf_op jit(solution)/shard_map/mul | solution.py:107
  52.8 1.3 slice_multiply_fusion.2
  54.2 1.2 slice_multiply_fusion.4
  55.5 0.4 broadcast_in_dim.41
  55.8 0.9 fusion.27
  56.8 0.6 fusion.36
  57.5 2.1 %collective-permute-start.4 = (f32[520,128]{1,0:T(8,128)S(1)}, f32[520,128]{1,0:T(8,128)S(1)}, u32[]{:S(2)}, u32[]{:S(2)}) collective-permute-start(f32[520,128]{1,0:T(8,128)S(1)} %concatenate.22), channel_id=1, source_target_pairs={{16,0},{32,16},{48,32},{64,48},{80,64},{96,80},{112,96},{128,112},... | collective-permute-start | bytes 798728 | tf_op jit(solution)/shard_map/ppermute | solution.py:14
  59.6 9.6 %collective-permute-done.4 = f32[520,128]{1,0:T(8,128)S(1)} collective-permute-done((f32[520,128]{1,0:T(8,128)S(1)}, f32[520,128]{1,0:T(8,128)S(1)}, u32[]{:S(2)}, u32[]{:S(2)}) %collective-permute-start.4) | collective-permute-done | bytes 266272 | tf_op jit(solution)/shard_map/ppermute | solution.py:14
  69.2 0.1 multiply_select_fusion.3
  69.4 1.9 %collective-permute-start.5 = (f32[520,128]{1,0:T(8,128)S(1)}, f32[520,128]{1,0:T(8,128)S(1)}, u32[]{:S(2)}, u32[]{:S(2)}) collective-permute-start(f32[520,128]{1,0:T(8,128)S(1)} %multiply_select_fusion.3), channel_id=1, source_target_pairs={{32,0},{48,16},{64,32},{80,48},{96,64},{112,80},{128,96},{144,112}... | collective-permute-start | bytes 798728 | tf_op jit(solution)/shard_map/ppermute | solution.py:14
  71.3 0.5 slice.296
  71.8 10.3 %collective-permute-done.5 = f32[520,128]{1,0:T(8,128)S(1)} collective-permute-done((f32[520,128]{1,0:T(8,128)S(1)}, f32[520,128]{1,0:T(8,128)S(1)}, u32[]{:S(2)}, u32[]{:S(2)}) %collective-permute-start.5) | collective-permute-done | bytes 266272 | tf_op jit(solution)/shard_map/ppermute | solution.py:14
  82.1 0.8 multiply_select_fusion.2
  82.9 2.4 %collective-permute-start.6 = (f32[520,128]{1,0:T(8,128)S(1)}, f32[520,128]{1,0:T(8,128)S(1)}, u32[]{:S(2)}, u32[]{:S(2)}) collective-permute-start(f32[520,128]{1,0:T(8,128)S(1)} %multiply_select_fusion.2), channel_id=1, source_target_pairs={{64,0},{80,16},{96,32},{112,48},{128,64},{144,80},{160,96},{176,11... | collective-permute-start | bytes 798728 | tf_op jit(solution)/shard_map/ppermute | solution.py:14
  85.3 0.5 slice.297
  85.8 12.3 %collective-permute-done.6 = f32[520,128]{1,0:T(8,128)S(1)} collective-permute-done((f32[520,128]{1,0:T(8,128)S(1)}, f32[520,128]{1,0:T(8,128)S(1)}, u32[]{:S(2)}, u32[]{:S(2)}) %collective-permute-start.6) | collective-permute-done | bytes 266272 | tf_op jit(solution)/shard_map/ppermute | solution.py:14
  98.1 0.8 multiply_select_fusion.1
  98.9 1.9 %collective-permute-start.7 = (f32[520,128]{1,0:T(8,128)S(1)}, f32[520,128]{1,0:T(8,128)S(1)}, u32[]{:S(2)}, u32[]{:S(2)}) collective-permute-start(f32[520,128]{1,0:T(8,128)S(1)} %multiply_select_fusion.1), channel_id=1, source_target_pairs={{128,0},{144,16},{160,32},{176,48},{192,64},{208,80},{224,96},{240... | collective-permute-start | bytes 798728 | tf_op jit(solution)/shard_map/ppermute | solution.py:14
  100.8 0.5 slice.298
  101.3 16.5 %collective-permute-done.7 = f32[520,128]{1,0:T(8,128)S(1)} collective-permute-done((f32[520,128]{1,0:T(8,128)S(1)}, f32[520,128]{1,0:T(8,128)S(1)}, u32[]{:S(2)}, u32[]{:S(2)}) %collective-permute-start.7) | collective-permute-done | bytes 266272 | tf_op jit(solution)/shard_map/ppermute | solution.py:14
  117.8 0.8 multiply_select_fusion
  118.6 1.3 collective-permute-start.8
  119.9 0.5 slice.299
  120.4 10.4 %collective-permute-done.8 = f32[520,128]{1,0:T(8,128)S(1)} collective-permute-done((f32[520,128]{1,0:T(8,128)S(1)}, f32[520,128]{1,0:T(8,128)S(1)}, u32[]{:S(2)}, u32[]{:S(2)}) %collective-permute-start.8) | collective-permute-done | bytes 266272 | tf_op jit(solution)/shard_map/ppermute | solution.py:14
  130.8 0.8 fusion.34
  131.7 0.4 broadcast_in_dim.43
  132.1 1.1 add_bitcast_fusion
  (43 shorter events, 1.4 us)
Async XLA Ops:
  2.2 17.7 %copy-start = (f32[1,16,128,128]{3,2,1,0:T(8,128)S(1)}, f32[1,16,128,128]{3,2,1,0:T(8,128)}, u32[]{:S(2)}) copy-start(f32[1,16,128,128]{3,2,1,0:T(8,128)} %param.7) | copy-start | bytes 3145732
  6.1 29.7 %collective-permute-start.3 = (f32[4,128,128]{2,1,0:T(8,128)}, f32[4,128,128]{2,1,0:T(8,128)}, u32[]{:S(2)}, u32[]{:S(2)}) collective-permute-start(f32[4,128,128]{2,1,0:T(8,128)} %get-tuple-element.22), channel_id=1, source_target_pairs={{1,0},{2,1},{3,2},{4,3},{5,4},{6,5},{7,6},{8,7},{9,8},{10,9},{11,1... | collective-permute-start | bytes 786440 | tf_op jit(solution)/shard_map/ppermute | solution.py:86
  13.7 22.0 %collective-permute-start.2 = (f32[4,128,128]{2,1,0:T(8,128)}, f32[4,128,128]{2,1,0:T(8,128)}, u32[]{:S(2)}, u32[]{:S(2)}) collective-permute-start(f32[4,128,128]{2,1,0:T(8,128)} %get-tuple-element.38), channel_id=1, source_target_pairs={{0,1},{1,2},{2,3},{3,4},{4,5},{5,6},{6,7},{7,8},{8,9},{9,10},{10,1... | collective-permute-start | bytes 786440 | tf_op jit(solution)/shard_map/ppermute | solution.py:81
  19.2 2.5 %copy-start.11 = (s32[64]{0:T(128)S(1)}, s32[64]{0:T(128)}, u32[]{:S(2)}) copy-start(s32[64]{0:T(128)} %param.9) | copy-start | bytes 772
  22.9 1.0 copy-start.3
  23.0 1.0 copy-start.4
  23.0 1.1 copy-start.5
  23.1 1.1 copy-start.6
  23.1 1.1 copy-start.7
  23.1 1.2 copy-start.8
  23.1 1.3 copy-start.9
  25.3 15.8 %collective-permute-start.1 = (f32[4,128,128]{2,1,0:T(8,128)}, f32[4,128,128]{2,1,0:T(8,128)S(1)}, u32[]{:S(2)}, u32[]{:S(2)}) collective-permute-start(f32[4,128,128]{2,1,0:T(8,128)} %get-tuple-element.21), channel_id=1, source_target_pairs={{1,0},{2,1},{3,2},{4,3},{5,4},{6,5},{7,6},{8,7},{9,8},{10,9},{11,1... | collective-permute-start | bytes 786440 | tf_op jit(solution)/shard_map/ppermute | solution.py:94
  33.7 15.6 %collective-permute-start = (f32[4,128,128]{2,1,0:T(8,128)S(1)}, f32[4,128,128]{2,1,0:T(8,128)S(1)}, u32[]{:S(2)}, u32[]{:S(2)}) collective-permute-start(f32[4,128,128]{2,1,0:T(8,128)S(1)} %get-tuple-element.40), channel_id=1, source_target_pairs={{0,1},{1,2},{2,3},{3,4},{4,5},{5,6},{6,7},{7,8},{8,9},{9,10},{10,1... | collective-permute-start | bytes 786440 | tf_op jit(solution)/shard_map/ppermute | solution.py:87
  35.7 13.6 %copy-start.2 = (f32[16,128,128]{2,1,0:T(8,128)S(1)}, f32[16,128,128]{2,1,0:T(8,128)}, u32[]{:S(2)}) copy-start(f32[16,128,128]{2,1,0:T(8,128)} %get-tuple-element.24) | copy-start | bytes 3145732
  49.7 1.0 copy-start.10
  49.7 1.4 %copy-start.1 = (f32[16,128,128]{2,1,0:T(8,128)S(1)}, f32[16,128,128]{2,1,0:T(8,128)}, u32[]{:S(2)}) copy-start(f32[16,128,128]{2,1,0:T(8,128)} %get-tuple-element.18) | copy-start | bytes 3145732
  57.5 11.8 %collective-permute-start.4 = (f32[520,128]{1,0:T(8,128)S(1)}, f32[520,128]{1,0:T(8,128)S(1)}, u32[]{:S(2)}, u32[]{:S(2)}) collective-permute-start(f32[520,128]{1,0:T(8,128)S(1)} %concatenate.22), channel_id=1, source_target_pairs={{16,0},{32,16},{48,32},{64,48},{80,64},{96,80},{112,96},{128,112},... | collective-permute-start | bytes 798728 | tf_op jit(solution)/shard_map/ppermute | solution.py:14
  69.4 12.7 %collective-permute-start.5 = (f32[520,128]{1,0:T(8,128)S(1)}, f32[520,128]{1,0:T(8,128)S(1)}, u32[]{:S(2)}, u32[]{:S(2)}) collective-permute-start(f32[520,128]{1,0:T(8,128)S(1)} %multiply_select_fusion.3), channel_id=1, source_target_pairs={{32,0},{48,16},{64,32},{80,48},{96,64},{112,80},{128,96},{144,112}... | collective-permute-start | bytes 798728 | tf_op jit(solution)/shard_map/ppermute | solution.py:14
  82.9 15.1 %collective-permute-start.6 = (f32[520,128]{1,0:T(8,128)S(1)}, f32[520,128]{1,0:T(8,128)S(1)}, u32[]{:S(2)}, u32[]{:S(2)}) collective-permute-start(f32[520,128]{1,0:T(8,128)S(1)} %multiply_select_fusion.2), channel_id=1, source_target_pairs={{64,0},{80,16},{96,32},{112,48},{128,64},{144,80},{160,96},{176,11... | collective-permute-start | bytes 798728 | tf_op jit(solution)/shard_map/ppermute | solution.py:14
  98.9 18.9 %collective-permute-start.7 = (f32[520,128]{1,0:T(8,128)S(1)}, f32[520,128]{1,0:T(8,128)S(1)}, u32[]{:S(2)}, u32[]{:S(2)}) collective-permute-start(f32[520,128]{1,0:T(8,128)S(1)} %multiply_select_fusion.1), channel_id=1, source_target_pairs={{128,0},{144,16},{160,32},{176,48},{192,64},{208,80},{224,96},{240... | collective-permute-start | bytes 798728 | tf_op jit(solution)/shard_map/ppermute | solution.py:14
  118.6 12.2 %collective-permute-start.8 = (f32[520,128]{1,0:T(8,128)S(1)}, f32[520,128]{1,0:T(8,128)S(1)}, u32[]{:S(2)}, u32[]{:S(2)}) collective-permute-start(f32[520,128]{1,0:T(8,128)S(1)} %get-tuple-element.54), channel_id=1, source_target_pairs={{256,0},{272,16},{288,32},{304,48},{320,64},{336,80},{352,96},{368... | collective-permute-start | bytes 798728 | tf_op jit(solution)/shard_map/ppermute | solution.py:14

commit v10 on v8

--- a/solution.py
+++ b/solution.py
@@ -59,7 +59,7 @@
 
 def lookup_both(material, conductance, rock_heat_drain):
     planes = material.shape[0]
-    block = (4,) + material.shape[1:]
+    block = material.shape
     spec = pl.BlockSpec(block, lambda i: (i, 0, 0))
     smem = pl.BlockSpec(memory_space=pltpu.SMEM)
     out = jax.ShapeDtypeStruct(material.shape, jnp.float32)

time: 126 us -> 124 us (0.984)
  the two profiles are of different devices: /device:TPU:466 before, /device:TPU:474 now
where the time goes in v10:
time: 124 us; the launch traced here: 123 us
  waiting for transfers between devices  58.8 us (47%)
  starting transfers between devices  28.4 us (23%)
  other arithmetic  17.6 us (14%)
  local copies, waits for them, and re-layouts  11.8 us (10%)
  Pallas kernels  5.6 us (5%)
    ppermute x5, waiting for transfers between devices, shifted(): lax.ppermute(value, axis, [(source, source + steps) for source in range(i...  58.8 us
    ppermute x5, starting transfers between devices, shifted(): lax.ppermute(value, axis, [(source, source + steps) for source in range(i...  9.51 us
    ppermute x1, starting transfers between devices, on_device(): material_next = lax.ppermute(material_f[:halo], 'space', down)  7.55 us
    ppermute x1, starting transfers between devices, on_device(): seeded_next = lax.ppermute(seeded[:halo], 'space', down)  7.55 us
    pallas_call x2, Pallas kernels, lookup_both(): pl.pallas_call(_lookup_kernel, grid=(planes // block[0],), in_specs=[smem...  5.6 us
    mul x4, other arithmetic, on_device(): weighted = cond_ext[lo:hi] * current  5.28 us
    slice x2, local copies, waits for them, and re-layouts, coarsen(): split[:, 1, :, 0]  4.52 us
    select_n x5, other arithmetic, on_device(): jnp.where(is_field, packed + power * own_gain * arrived, packed * arrived)  3.32 us
  transfers between devices with their start and end apart: 9, of which 5 were waited for; matrix products, arithmetic and copies ran while one was open for 11% of the time, Pallas kernels for 5%

profile of v10, /device:TPU:474, one launch (start us, length us, event | category | flops | bytes accessed | tf_op | source)
XLA Modules:
  0.0 123.3 jit_solution(13546396446187059650)
XLA Ops:
  0.0 1.3 %convert_element_type.14 = f32[16,128,128]{2,1,0:T(8,128)S(1)} convert(s32[16,128,128]{2,1,0:T(8,128)} %material_ref.1) | non-fusion elementwise | flops 262144 | bytes 2097152 | tf_op jit(solution)/shard_map/convert_element_type | solution.py:100
  1.3 0.8 fusion.41
  2.2 1.9 %collective-permute-start.2 = (f32[4,128,128]{2,1,0:T(8,128)}, f32[4,128,128]{2,1,0:T(8,128)}, u32[]{:S(2)}, u32[]{:S(2)}) collective-permute-start(f32[4,128,128]{2,1,0:T(8,128)} %get-tuple-element.24), channel_id=1, source_target_pairs={{0,1},{1,2},{2,3},{3,4},{4,5},{5,6},{6,7},{7,8},{8,9},{9,10},{10,1... | collective-permute-start | bytes 786440 | tf_op jit(solution)/shard_map/ppermute | solution.py:101
  4.1 7.6 %collective-permute-start.3 = (f32[4,128,128]{2,1,0:T(8,128)}, f32[4,128,128]{2,1,0:T(8,128)}, u32[]{:S(2)}, u32[]{:S(2)}) collective-permute-start(f32[4,128,128]{2,1,0:T(8,128)} %get-tuple-element.25), channel_id=1, source_target_pairs={{1,0},{2,1},{3,2},{4,3},{5,4},{6,5},{7,6},{8,7},{9,8},{10,9},{11,1... | collective-permute-start | bytes 786440 | tf_op jit(solution)/shard_map/ppermute | solution.py:102
  11.7 1.3 %scatter_custom_fusion = f32[262144]{0:T(1024)S(1)} fusion(s32[64]{0:T(128)S(1)} %compare_select_fusion, f32[64]{0:T(128)} %bitcast.63, f32[]{:T(128)} %constant.22.clone.1), kind=kCustom, calls=%fused_computation.63 | custom fusion | flops 64 | bytes 1049088 | tf_op jit(solution)/shard_map/scatter-add | solution.py:92
  13.0 0.1 bitcast_add_fusion
  13.1 0.8 fusion.42
  14.0 1.9 %collective-permute-start = (f32[4,128,128]{2,1,0:T(8,128)}, f32[4,128,128]{2,1,0:T(8,128)}, u32[]{:S(2)}, u32[]{:S(2)}) collective-permute-start(f32[4,128,128]{2,1,0:T(8,128)} %get-tuple-element.26), channel_id=1, source_target_pairs={{0,1},{1,2},{2,3},{3,4},{4,5},{5,6},{6,7},{7,8},{8,9},{9,10},{10,1... | collective-permute-start | bytes 786440 | tf_op jit(solution)/shard_map/ppermute | solution.py:103
  15.9 7.6 %collective-permute-start.1 = (f32[4,128,128]{2,1,0:T(8,128)}, f32[4,128,128]{2,1,0:T(8,128)}, u32[]{:S(2)}, u32[]{:S(2)}) collective-permute-start(f32[4,128,128]{2,1,0:T(8,128)} %get-tuple-element.27), channel_id=1, source_target_pairs={{1,0},{2,1},{3,2},{4,3},{5,4},{6,5},{7,6},{8,7},{9,8},{10,9},{11,1... | collective-permute-start | bytes 786440 | tf_op jit(solution)/shard_map/ppermute | solution.py:104
  24.1 3.2 %shard_map.73 = (f32[16,128,128]{2,1,0:T(8,128)}, f32[16,128,128]{2,1,0:T(8,128)}) custom-call(f32[8]{0:T(128)} %cond_table.3, f32[8]{0:T(128)} %drain_table.3, s32[16,128,128]{2,1,0:T(8,128)} %material_ref.1), custom_call_target="tpu_custom_call" | custom-call | tf_op jit(solution)/shard_map/pallas_call | solution.py:66
  27.3 2.6 %fusion.43 = (f32[8,1,64,1,128]{4,3,2,1,0:T(1,128)S(1)}, f32[8,1,64,1,128]{4,3,2,1,0:T(1,128)S(1)}, f32[8,1,64,1,128]{4,3,2,1,0:T(1,128)S(1)}, f32[8,1,64,1,128]{4,3,2,1,0:T(1,128)S(1)}) fusion(f32[8,2,64,2,128]{4,3,2,1,0:T(2,128)} %bitcast.47), kind=kLoop, calls=%fused_computation.91 | loop fusion | bytes 2097152 | tf_op jit(solution)/shard_map/slice | solution.py:32
  29.9 1.9 %fusion.44 = (f32[8,1,64,1,128]{4,3,2,1,0:T(1,128)}, f32[8,1,64,1,128]{4,3,2,1,0:T(1,128)}, f32[8,1,64,1,128]{4,3,2,1,0:T(1,128)}, f32[8,1,64,1,128]{4,3,2,1,0:T(1,128)}) fusion(f32[8,2,64,2,128]{4,3,2,1,0:T(2,128)S(1)} %bitcast.43), kind=kLoop, calls=%fused_computation.92 | loop fusion | bytes 2097152 | tf_op jit(solution)/shard_map/slice | solution.py:32
  31.9 1.4 %exponential_multiply_fusion = (f32[8,1,64,1,128]{4,2,0,3,1:T(8,128)S(1)}, f32[8,1,64,1,128]{4,2,0,3,1:T(8,128)S(1)}) fusion(f32[8,1,64,1,128]{4,2,0,3,1:T(8,128)} %bitcast.60, f32[8,1,64,1,128]{4,2,0,3,1:T(8,128)} %bitcast.62, f32[8,1,64,1,128]{4,2,0,3,1:T(8,128)} %bitcast.61, f32[8,1,64,1,128]{4,2,0,3,1:T(8,128)} %bitcast.59, f32[]{:T(128)} %bitcast.35, ...), kind=kLoop, calls=%fused_computation.79 | loop fusion | flops 720896 | bytes 2621444 | tf_op jit(solution)/shard_map/mul | solution.py:154
  33.3 2.0 %maximum_convert_fusion.material_ref = s32[8,128,128]{2,1,0:T(8,128)} fusion(f32[4,128,128]{2,1,0:T(8,128)} %collective-permute-done.3, f32[4,128,128]{2,1,0:T(8,128)} %collective-permute-done.2), kind=kLoop, calls=%fused_computation.62 | loop fusion | flops 262144 | bytes 1048576 | tf_op jit(solution)/shard_map/convert_element_type | solution.py:106
  35.3 2.4 %shard_map.74 = (f32[8,128,128]{2,1,0:T(8,128)}, f32[8,128,128]{2,1,0:T(8,128)}) custom-call(f32[8]{0:T(128)} %cond_table.3, f32[8]{0:T(128)} %drain_table.3, s32[8,128,128]{2,1,0:T(8,128)} %maximum_convert_fusion.material_ref), custom_call_target="tpu_custom_call" | custom-call | tf_op jit(solution)/shard_map/pallas_call | solution.py:66
  37.7 1.1 fusion.46
  38.8 1.4 %fusion.37 = (f32[24,128,128]{2,1,0:T(8,128)S(1)}, f32[24,128,128]{2,1,0:T(8,128)S(1)}, f32[24,128,128]{2,1,0:T(8,128)S(1)}) fusion(f32[4,128,128]{2,1,0:T(8,128)} %collective-permute-done.1, f32[16,128,128]{2,1,0:T(8,128)S(1)} %bitcast_add_fusion, f32[4,128,128]{2,1,0:T(8,128)} %collective-permute-done, f32[4,128,128]{2,1,0:T(8,128)S(1)} %get-tuple-element.39, ...), kind=kLoop, calls=%fused_computation.88 | loop fusion | flops 2359296 | bytes 7864344 | tf_op jit(solution)/shard_map/mul | solution.py:118
  40.1 0.1 slice.272
  40.3 0.9 copy-done.3
  41.2 0.3 copy-done.1
  41.5 0.2 maximum_add_fusion
  41.7 1.4 %slice_multiply_fusion = (f32[22,128,128]{2,1,0:T(8,128)S(1)}, f32[22,128,128]{2,1,0:T(8,128)S(1)}) fusion(f32[24,128,128]{2,1,0:T(8,128)S(1)} %get-tuple-element.20, f32[24,128,128]{2,1,0:T(8,128)S(1)} %maximum_add_fusion, f32[22,128,128]{2,1,0:T(8,128)S(1)} %slice.272, f32[24,128,128]{2,1,0:T(8,128)S(1)} %get-tuple-element.19, ...), kind=kLoop, calls=%fused_computation.27 | loop fusion | flops 3964928 | bytes 11534336 | tf_op jit(solution)/shard_map/mul | solution.py:118
  43.2 1.3 %slice_multiply_fusion.2 = (f32[20,128,128]{2,1,0:T(8,128)S(1)}, f32[20,128,128]{2,1,0:T(8,128)S(1)}) fusion(f32[24,128,128]{2,1,0:T(8,128)S(1)} %get-tuple-element.20, f32[24,128,128]{2,1,0:T(8,128)S(1)} %maximum_add_fusion, f32[20,128,128]{2,1,0:T(8,128)S(1)} %slice.278, f32[22,128,128]{2,1,0:T(8,128)S(1)} %get-tuple-element.17, ...), kind=kLoop, calls=%fused_computation.37 | loop fusion | flops 3604480 | bytes 10485760 | tf_op jit(solution)/shard_map/mul | solution.py:118
  44.6 1.2 slice_multiply_fusion.4
  46.0 0.4 broadcast_in_dim.41
  46.4 0.9 fusion.27
  47.3 0.6 fusion.36
  47.9 2.5 %collective-permute-start.4 = (f32[520,128]{1,0:T(8,128)S(1)}, f32[520,128]{1,0:T(8,128)S(1)}, u32[]{:S(2)}, u32[]{:S(2)}) collective-permute-start(f32[520,128]{1,0:T(8,128)S(1)} %concatenate.22), channel_id=1, source_target_pairs={{16,0},{32,16},{48,32},{64,48},{80,64},{96,80},{112,96},{128,112},... | collective-permute-start | bytes 798728 | tf_op jit(solution)/shard_map/ppermute | solution.py:27
  50.5 10.8 %collective-permute-done.4 = f32[520,128]{1,0:T(8,128)S(1)} collective-permute-done((f32[520,128]{1,0:T(8,128)S(1)}, f32[520,128]{1,0:T(8,128)S(1)}, u32[]{:S(2)}, u32[]{:S(2)}) %collective-permute-start.4) | collective-permute-done | bytes 266272 | tf_op jit(solution)/shard_map/ppermute | solution.py:27
  61.2 0.1 multiply_select_fusion.3
  61.4 1.9 %collective-permute-start.5 = (f32[520,128]{1,0:T(8,128)S(1)}, f32[520,128]{1,0:T(8,128)S(1)}, u32[]{:S(2)}, u32[]{:S(2)}) collective-permute-start(f32[520,128]{1,0:T(8,128)S(1)} %multiply_select_fusion.3), channel_id=1, source_target_pairs={{32,0},{48,16},{64,32},{80,48},{96,64},{112,80},{128,96},{144,112}... | collective-permute-start | bytes 798728 | tf_op jit(solution)/shard_map/ppermute | solution.py:27
  63.3 0.5 slice.296
  63.8 11.2 %collective-permute-done.5 = f32[520,128]{1,0:T(8,128)S(1)} collective-permute-done((f32[520,128]{1,0:T(8,128)S(1)}, f32[520,128]{1,0:T(8,128)S(1)}, u32[]{:S(2)}, u32[]{:S(2)}) %collective-permute-start.5) | collective-permute-done | bytes 266272 | tf_op jit(solution)/shard_map/ppermute | solution.py:27
  75.1 0.8 multiply_select_fusion.2
  75.9 1.9 %collective-permute-start.6 = (f32[520,128]{1,0:T(8,128)S(1)}, f32[520,128]{1,0:T(8,128)S(1)}, u32[]{:S(2)}, u32[]{:S(2)}) collective-permute-start(f32[520,128]{1,0:T(8,128)S(1)} %multiply_select_fusion.2), channel_id=1, source_target_pairs={{64,0},{80,16},{96,32},{112,48},{128,64},{144,80},{160,96},{176,11... | collective-permute-start | bytes 798728 | tf_op jit(solution)/shard_map/ppermute | solution.py:27
  77.8 0.5 slice.297
  78.3 10.4 %collective-permute-done.6 = f32[520,128]{1,0:T(8,128)S(1)} collective-permute-done((f32[520,128]{1,0:T(8,128)S(1)}, f32[520,128]{1,0:T(8,128)S(1)}, u32[]{:S(2)}, u32[]{:S(2)}) %collective-permute-start.6) | collective-permute-done | bytes 266272 | tf_op jit(solution)/shard_map/ppermute | solution.py:27
  88.7 0.8 multiply_select_fusion.1
  89.5 1.9 %collective-permute-start.7 = (f32[520,128]{1,0:T(8,128)S(1)}, f32[520,128]{1,0:T(8,128)S(1)}, u32[]{:S(2)}, u32[]{:S(2)}) collective-permute-start(f32[520,128]{1,0:T(8,128)S(1)} %multiply_select_fusion.1), channel_id=1, source_target_pairs={{128,0},{144,16},{160,32},{176,48},{192,64},{208,80},{224,96},{240... | collective-permute-start | bytes 798728 | tf_op jit(solution)/shard_map/ppermute | solution.py:27
  91.4 0.5 slice.298
  91.9 16.0 %collective-permute-done.7 = f32[520,128]{1,0:T(8,128)S(1)} collective-permute-done((f32[520,128]{1,0:T(8,128)S(1)}, f32[520,128]{1,0:T(8,128)S(1)}, u32[]{:S(2)}, u32[]{:S(2)}) %collective-permute-start.7) | collective-permute-done | bytes 266272 | tf_op jit(solution)/shard_map/ppermute | solution.py:27
  108.0 0.8 multiply_select_fusion
  108.8 1.3 %collective-permute-start.8 = (f32[520,128]{1,0:T(8,128)S(1)}, f32[520,128]{1,0:T(8,128)S(1)}, u32[]{:S(2)}, u32[]{:S(2)}) collective-permute-start(f32[520,128]{1,0:T(8,128)S(1)} %get-tuple-element.40), channel_id=1, source_target_pairs={{256,0},{272,16},{288,32},{304,48},{320,64},{336,80},{352,96},{368... | collective-permute-start | bytes 798728 | tf_op jit(solution)/shard_map/ppermute | solution.py:27
  110.1 0.5 slice.299
  110.6 10.4 %collective-permute-done.8 = f32[520,128]{1,0:T(8,128)S(1)} collective-permute-done((f32[520,128]{1,0:T(8,128)S(1)}, f32[520,128]{1,0:T(8,128)S(1)}, u32[]{:S(2)}, u32[]{:S(2)}) %collective-permute-start.8) | collective-permute-done | bytes 266272 | tf_op jit(solution)/shard_map/ppermute | solution.py:27
  121.0 0.8 fusion.34
  121.9 0.4 broadcast_in_dim.43
  122.3 1.1 add_bitcast_fusion
  (27 shorter events, 0.7 us)
Async XLA Ops:
  0.0 11.7 %copy-start.4 = (s32[64]{0:T(128)S(1)}, s32[64]{0:T(128)}, u32[]{:S(2)}) copy-start(s32[64]{0:T(128)} %param.9) | copy-start | bytes 772
  1.3 11.7 %copy-start = (f32[1,16,128,128]{3,2,1,0:T(8,128)S(1)}, f32[1,16,128,128]{3,2,1,0:T(8,128)}, u32[]{:S(2)}) copy-start(f32[1,16,128,128]{3,2,1,0:T(8,128)} %param.7) | copy-start | bytes 3145732
  2.2 31.1 %collective-permute-start.2 = (f32[4,128,128]{2,1,0:T(8,128)}, f32[4,128,128]{2,1,0:T(8,128)}, u32[]{:S(2)}, u32[]{:S(2)}) collective-permute-start(f32[4,128,128]{2,1,0:T(8,128)} %get-tuple-element.24), channel_id=1, source_target_pairs={{0,1},{1,2},{2,3},{3,4},{4,5},{5,6},{6,7},{7,8},{8,9},{9,10},{10,1... | collective-permute-start | bytes 786440 | tf_op jit(solution)/shard_map/ppermute | solution.py:101
  4.1 29.2 %collective-permute-start.3 = (f32[4,128,128]{2,1,0:T(8,128)}, f32[4,128,128]{2,1,0:T(8,128)}, u32[]{:S(2)}, u32[]{:S(2)}) collective-permute-start(f32[4,128,128]{2,1,0:T(8,128)} %get-tuple-element.25), channel_id=1, source_target_pairs={{1,0},{2,1},{3,2},{4,3},{5,4},{6,5},{7,6},{8,7},{9,8},{10,9},{11,1... | collective-permute-start | bytes 786440 | tf_op jit(solution)/shard_map/ppermute | solution.py:102
  14.0 24.7 %collective-permute-start = (f32[4,128,128]{2,1,0:T(8,128)}, f32[4,128,128]{2,1,0:T(8,128)}, u32[]{:S(2)}, u32[]{:S(2)}) collective-permute-start(f32[4,128,128]{2,1,0:T(8,128)} %get-tuple-element.26), channel_id=1, source_target_pairs={{0,1},{1,2},{2,3},{3,4},{4,5},{5,6},{6,7},{7,8},{8,9},{9,10},{10,1... | collective-permute-start | bytes 786440 | tf_op jit(solution)/shard_map/ppermute | solution.py:103
  15.9 22.8 %collective-permute-start.1 = (f32[4,128,128]{2,1,0:T(8,128)}, f32[4,128,128]{2,1,0:T(8,128)}, u32[]{:S(2)}, u32[]{:S(2)}) collective-permute-start(f32[4,128,128]{2,1,0:T(8,128)} %get-tuple-element.27), channel_id=1, source_target_pairs={{1,0},{2,1},{3,2},{4,3},{5,4},{6,5},{7,6},{8,7},{9,8},{10,9},{11,1... | collective-permute-start | bytes 786440 | tf_op jit(solution)/shard_map/ppermute | solution.py:104
  33.3 5.5 %copy-start.2 = (f32[16,128,128]{2,1,0:T(8,128)S(1)}, f32[16,128,128]{2,1,0:T(8,128)}, u32[]{:S(2)}) copy-start(f32[16,128,128]{2,1,0:T(8,128)} %get-tuple-element.11) | copy-start | bytes 3145732
  40.1 1.0 copy-start.3
  40.1 1.4 %copy-start.1 = (f32[16,128,128]{2,1,0:T(8,128)S(1)}, f32[16,128,128]{2,1,0:T(8,128)}, u32[]{:S(2)}) copy-start(f32[16,128,128]{2,1,0:T(8,128)} %get-tuple-element.9) | copy-start | bytes 3145732
  47.9 13.3 %collective-permute-start.4 = (f32[520,128]{1,0:T(8,128)S(1)}, f32[520,128]{1,0:T(8,128)S(1)}, u32[]{:S(2)}, u32[]{:S(2)}) collective-permute-start(f32[520,128]{1,0:T(8,128)S(1)} %concatenate.22), channel_id=1, source_target_pairs={{16,0},{32,16},{48,32},{64,48},{80,64},{96,80},{112,96},{128,112},... | collective-permute-start | bytes 798728 | tf_op jit(solution)/shard_map/ppermute | solution.py:27
  61.4 13.7 %collective-permute-start.5 = (f32[520,128]{1,0:T(8,128)S(1)}, f32[520,128]{1,0:T(8,128)S(1)}, u32[]{:S(2)}, u32[]{:S(2)}) collective-permute-start(f32[520,128]{1,0:T(8,128)S(1)} %multiply_select_fusion.3), channel_id=1, source_target_pairs={{32,0},{48,16},{64,32},{80,48},{96,64},{112,80},{128,96},{144,112}... | collective-permute-start | bytes 798728 | tf_op jit(solution)/shard_map/ppermute | solution.py:27
  75.9 12.8 %collective-permute-start.6 = (f32[520,128]{1,0:T(8,128)S(1)}, f32[520,128]{1,0:T(8,128)S(1)}, u32[]{:S(2)}, u32[]{:S(2)}) collective-permute-start(f32[520,128]{1,0:T(8,128)S(1)} %multiply_select_fusion.2), channel_id=1, source_target_pairs={{64,0},{80,16},{96,32},{112,48},{128,64},{144,80},{160,96},{176,11... | collective-permute-start | bytes 798728 | tf_op jit(solution)/shard_map/ppermute | solution.py:27
  89.5 18.5 %collective-permute-start.7 = (f32[520,128]{1,0:T(8,128)S(1)}, f32[520,128]{1,0:T(8,128)S(1)}, u32[]{:S(2)}, u32[]{:S(2)}) collective-permute-start(f32[520,128]{1,0:T(8,128)S(1)} %multiply_select_fusion.1), channel_id=1, source_target_pairs={{128,0},{144,16},{160,32},{176,48},{192,64},{208,80},{224,96},{240... | collective-permute-start | bytes 798728 | tf_op jit(solution)/shard_map/ppermute | solution.py:27
  108.8 12.2 %collective-permute-start.8 = (f32[520,128]{1,0:T(8,128)S(1)}, f32[520,128]{1,0:T(8,128)S(1)}, u32[]{:S(2)}, u32[]{:S(2)}) collective-permute-start(f32[520,128]{1,0:T(8,128)S(1)} %get-tuple-element.40), channel_id=1, source_target_pairs={{256,0},{272,16},{288,32},{304,48},{320,64},{336,80},{352,96},{368... | collective-permute-start | bytes 798728 | tf_op jit(solution)/shard_map/ppermute | solution.py:27

commit v11 on v10

--- a/solution.py
+++ b/solution.py
@@ -97,17 +97,16 @@
     space_size = lax.axis_size("space")
     up = [(i, i + 1) for i in range(space_size - 1)]
     down = [(i + 1, i) for i in range(space_size - 1)]
-    material_f = material.astype(jnp.float32)
-    material_prev = lax.ppermute(material_f[-halo:], "space", up)
-    material_next = lax.ppermute(material_f[:halo], "space", down)
+    cond_own, drain_own = lookup_both(material, conductance, rock_heat_drain)
+    tables_up = jnp.concatenate([cond_own[-halo:], drain_own[-halo:]], axis=0)
+    tables_down = jnp.concatenate([cond_own[:halo], drain_own[:halo]], axis=0)
+    tables_prev = lax.ppermute(tables_up, "space", up)
+    tables_next = lax.ppermute(tables_down, "space", down)
     seeded_prev = lax.ppermute(seeded[-halo:], "space", up)
     seeded_next = lax.ppermute(seeded[:halo], "space", down)
-    cond_own, drain_own = lookup_both(material, conductance, rock_heat_drain)
-    halo_material = jnp.concatenate([material_prev, material_next], axis=0).astype(jnp.int32)
-    cond_halo, drain_halo = lookup_both(halo_material, conductance, rock_heat_drain)
     current = jnp.concatenate([seeded_prev, seeded, seeded_next], axis=0)
-    cond_ext = jnp.concatenate([cond_halo[:halo], cond_own, cond_halo[halo:]], axis=0)
-    drain_ext = jnp.concatenate([drain_halo[:halo], drain_own, drain_halo[halo:]], axis=0)
+    cond_ext = jnp.concatenate([tables_prev[:halo], cond_own, tables_next[:halo]], axis=0)
+    drain_ext = jnp.concatenate([tables_prev[halo:], drain_own, tables_next[halo:]], axis=0)
     extended = planes + 2 * halo
     plane = lax.axis_index("space") * planes - halo + lax.iota(jnp.int32, extended)
     inside = (plane >= 0) & (plane < space_size * planes)

time: 124 us -> 137 us (1.10)
  the two profiles are of different devices: /device:TPU:474 before, /device:TPU:21 now
where the time goes in v11:
time: 137 us; the launch traced here: 136 us
  waiting for transfers between devices  72.6 us (53%)
  starting transfers between devices  31.7 us (23%)
  other arithmetic  16.8 us (12%)
  local copies, waits for them, and re-layouts  10.6 us (8%)
  Pallas kernels  3.24 us (2%)
    ppermute x5, waiting for transfers between devices, shifted(): lax.ppermute(value, axis, [(source, source + steps) for source in range(i...  57.3 us
    ppermute x1, waiting for transfers between devices, on_device(): tables_next = lax.ppermute(tables_down, 'space', down)  11.4 us
    ppermute x1, starting transfers between devices, on_device(): tables_prev = lax.ppermute(tables_up, 'space', up)  11.2 us
    ppermute x5, starting transfers between devices, shifted(): lax.ppermute(value, axis, [(source, source + steps) for source in range(i...  9.18 us
    ppermute x1, starting transfers between devices, on_device(): seeded_prev = lax.ppermute(seeded[-halo:], 'space', up)  7.54 us
    mul x4, other arithmetic, on_device(): weighted = cond_ext[lo:hi] * current  5.28 us
    ppermute x1, waiting for transfers between devices, on_device(): seeded_next = lax.ppermute(seeded[:halo], 'space', down)  3.88 us
    select_n x5, other arithmetic, on_device(): jnp.where(is_field, packed + power * own_gain * arrived, packed * arrived)  3.33 us
  transfers between devices with their start and end apart: 9, of which 7 were waited for; matrix products, arithmetic and copies ran while one was open for 9% of the time, Pallas kernels for 0%

profile of v11, /device:TPU:21, one launch (start us, length us, event | category | flops | bytes accessed | tf_op | source)
XLA Modules:
  0.0 136.1 jit_solution(4754169463743245977)
XLA Ops:
  0.0 3.2 %shard_map.73 = (f32[16,128,128]{2,1,0:T(8,128)}, f32[16,128,128]{2,1,0:T(8,128)}) custom-call(f32[8]{0:T(128)} %cond_table.1, f32[8]{0:T(128)} %drain_table.1, s32[16,128,128]{2,1,0:T(8,128)} %material_ref.1), custom_call_target="tpu_custom_call" | custom-call | tf_op jit(solution)/shard_map/pallas_call | solution.py:66
  3.2 1.3 fusion.41
  4.5 0.8 pad_maximum_fusion.1
  5.4 11.2 %collective-permute-start.2 = (f32[8,128,128]{2,1,0:T(8,128)}, f32[8,128,128]{2,1,0:T(8,128)}, u32[]{:S(2)}, u32[]{:S(2)}) collective-permute-start(f32[8,128,128]{2,1,0:T(8,128)} %pad_maximum_fusion.1), channel_id=1, source_target_pairs={{0,1},{1,2},{2,3},{3,4},{4,5},{5,6},{6,7},{7,8},{8,9},{9,10},{10,1... | collective-permute-start | bytes 1572872 | tf_op jit(solution)/shard_map/ppermute | solution.py:103
  16.6 0.8 pad_maximum_fusion.2
  17.4 1.9 %collective-permute-start.3 = (f32[8,128,128]{2,1,0:T(8,128)}, f32[8,128,128]{2,1,0:T(8,128)}, u32[]{:S(2)}, u32[]{:S(2)}) collective-permute-start(f32[8,128,128]{2,1,0:T(8,128)} %pad_maximum_fusion.2), channel_id=1, source_target_pairs={{1,0},{2,1},{3,2},{4,3},{5,4},{6,5},{7,6},{8,7},{9,8},{10,9},{11,1... | collective-permute-start | bytes 1572872 | tf_op jit(solution)/shard_map/ppermute | solution.py:104
  19.4 2.0 %scatter_custom_fusion = f32[262144]{0:T(1024)} fusion(s32[64]{0:T(128)S(1)} %compare_select_fusion, f32[64]{0:T(128)} %bitcast.63, f32[]{:T(128)} %constant.22.clone.1), kind=kCustom, calls=%fused_computation.64 | custom fusion | flops 64 | bytes 1049088 | tf_op jit(solution)/shard_map/scatter-add | solution.py:92
  21.4 1.4 %bitcast_add_fusion = f32[16,128,128]{2,1,0:T(8,128)S(1)} fusion(f32[16,128,128]{2,1,0:T(8,128)} %bitcast.46, f32[1,16,128,128]{3,2,1,0:T(8,128)S(1)} %copy-done.1), kind=kLoop, calls=%fused_computation.60 | loop fusion | flops 262144 | bytes 3145728 | tf_op jit(solution)/shard_map/add | solution.py:95
  22.8 0.9 fusion.43
  23.7 7.5 %collective-permute-start = (f32[4,128,128]{2,1,0:T(8,128)}, f32[4,128,128]{2,1,0:T(8,128)}, u32[]{:S(2)}, u32[]{:S(2)}) collective-permute-start(f32[4,128,128]{2,1,0:T(8,128)} %get-tuple-element.24), channel_id=1, source_target_pairs={{0,1},{1,2},{2,3},{3,4},{4,5},{5,6},{6,7},{7,8},{8,9},{9,10},{10,1... | collective-permute-start | bytes 786440 | tf_op jit(solution)/shard_map/ppermute | solution.py:105
  31.2 1.9 %collective-permute-start.1 = (f32[4,128,128]{2,1,0:T(8,128)}, f32[4,128,128]{2,1,0:T(8,128)}, u32[]{:S(2)}, u32[]{:S(2)}) collective-permute-start(f32[4,128,128]{2,1,0:T(8,128)} %get-tuple-element.25), channel_id=1, source_target_pairs={{1,0},{2,1},{3,2},{4,3},{5,4},{6,5},{7,6},{8,7},{9,8},{10,9},{11,1... | collective-permute-start | bytes 786440 | tf_op jit(solution)/shard_map/ppermute | solution.py:106
  33.8 1.8 %fusion.44 = (f32[8,1,64,1,128]{4,3,2,1,0:T(1,128)S(1)}, f32[8,1,64,1,128]{4,3,2,1,0:T(1,128)}, f32[8,1,64,1,128]{4,3,2,1,0:T(1,128)}, f32[8,1,64,1,128]{4,3,2,1,0:T(1,128)}) fusion(f32[8,2,64,2,128]{4,3,2,1,0:T(2,128)S(1)} %bitcast.43), kind=kLoop, calls=%fused_computation.93 | loop fusion | bytes 2097152 | tf_op jit(solution)/shard_map/slice | solution.py:32
  35.7 1.1 fusion.45
  36.9 0.2 exponential_multiply_fusion
  37.1 1.2 fusion.46
  38.2 11.4 %collective-permute-done.3 = f32[8,128,128]{2,1,0:T(8,128)} collective-permute-done((f32[8,128,128]{2,1,0:T(8,128)}, f32[8,128,128]{2,1,0:T(8,128)}, u32[]{:S(2)}, u32[]{:S(2)}) %collective-permute-start.3) | collective-permute-done | bytes 524320 | tf_op jit(solution)/shard_map/ppermute | solution.py:104
  49.7 1.1 fusion.47
  50.8 3.9 %collective-permute-done.1 = f32[4,128,128]{2,1,0:T(8,128)} collective-permute-done((f32[4,128,128]{2,1,0:T(8,128)}, f32[4,128,128]{2,1,0:T(8,128)}, u32[]{:S(2)}, u32[]{:S(2)}) %collective-permute-start.1) | collective-permute-done | bytes 262176 | tf_op jit(solution)/shard_map/ppermute | solution.py:106
  54.6 1.4 %fusion.37 = (f32[24,128,128]{2,1,0:T(8,128)S(1)}, f32[24,128,128]{2,1,0:T(8,128)S(1)}, f32[24,128,128]{2,1,0:T(8,128)S(1)}) fusion(f32[4,128,128]{2,1,0:T(8,128)} %collective-permute-done.1, f32[16,128,128]{2,1,0:T(8,128)S(1)} %bitcast_add_fusion, f32[4,128,128]{2,1,0:T(8,128)} %collective-permute-done, f32[4,128,128]{2,1,0:T(8,128)S(1)} %get-tuple-element.37, ...), kind=kLoop, calls=%fused_computation.89 | loop fusion | flops 2359296 | bytes 7864344 | tf_op jit(solution)/shard_map/mul | solution.py:117
  56.0 0.1 slice.280
  56.2 0.1 maximum_add_fusion
  56.3 1.4 %slice_multiply_fusion = (f32[22,128,128]{2,1,0:T(8,128)S(1)}, f32[22,128,128]{2,1,0:T(8,128)S(1)}) fusion(f32[24,128,128]{2,1,0:T(8,128)S(1)} %get-tuple-element.16, f32[24,128,128]{2,1,0:T(8,128)S(1)} %maximum_add_fusion, f32[22,128,128]{2,1,0:T(8,128)S(1)} %slice.280, f32[24,128,128]{2,1,0:T(8,128)S(1)} %get-tuple-element.15, ...), kind=kLoop, calls=%fused_computation.27 | loop fusion | flops 3964928 | bytes 11534336 | tf_op jit(solution)/shard_map/mul | solution.py:117
  57.8 1.3 slice_multiply_fusion.2
  59.2 1.2 slice_multiply_fusion.4
  60.6 0.4 broadcast_in_dim.41
  61.0 0.9 fusion.27
  61.9 0.6 fusion.36
  62.5 1.9 %collective-permute-start.4 = (f32[520,128]{1,0:T(8,128)S(1)}, f32[520,128]{1,0:T(8,128)S(1)}, u32[]{:S(2)}, u32[]{:S(2)}) collective-permute-start(f32[520,128]{1,0:T(8,128)S(1)} %concatenate.26), channel_id=1, source_target_pairs={{16,0},{32,16},{48,32},{64,48},{80,64},{96,80},{112,96},{128,112},... | collective-permute-start | bytes 798728 | tf_op jit(solution)/shard_map/ppermute | solution.py:27
  64.5 5.5 %collective-permute-done.4 = f32[520,128]{1,0:T(8,128)S(1)} collective-permute-done((f32[520,128]{1,0:T(8,128)S(1)}, f32[520,128]{1,0:T(8,128)S(1)}, u32[]{:S(2)}, u32[]{:S(2)}) %collective-permute-start.4) | collective-permute-done | bytes 266272 | tf_op jit(solution)/shard_map/ppermute | solution.py:27
  70.0 0.1 multiply_select_fusion.3
  70.2 1.9 %collective-permute-start.5 = (f32[520,128]{1,0:T(8,128)S(1)}, f32[520,128]{1,0:T(8,128)S(1)}, u32[]{:S(2)}, u32[]{:S(2)}) collective-permute-start(f32[520,128]{1,0:T(8,128)S(1)} %multiply_select_fusion.3), channel_id=1, source_target_pairs={{32,0},{48,16},{64,32},{80,48},{96,64},{112,80},{128,96},{144,112}... | collective-permute-start | bytes 798728 | tf_op jit(solution)/shard_map/ppermute | solution.py:27
  72.1 0.5 slice.306
  72.6 12.8 %collective-permute-done.5 = f32[520,128]{1,0:T(8,128)S(1)} collective-permute-done((f32[520,128]{1,0:T(8,128)S(1)}, f32[520,128]{1,0:T(8,128)S(1)}, u32[]{:S(2)}, u32[]{:S(2)}) %collective-permute-start.5) | collective-permute-done | bytes 266272 | tf_op jit(solution)/shard_map/ppermute | solution.py:27
  85.4 0.8 multiply_select_fusion.2
  86.2 2.1 %collective-permute-start.6 = (f32[520,128]{1,0:T(8,128)S(1)}, f32[520,128]{1,0:T(8,128)S(1)}, u32[]{:S(2)}, u32[]{:S(2)}) collective-permute-start(f32[520,128]{1,0:T(8,128)S(1)} %multiply_select_fusion.2), channel_id=1, source_target_pairs={{64,0},{80,16},{96,32},{112,48},{128,64},{144,80},{160,96},{176,11... | collective-permute-start | bytes 798728 | tf_op jit(solution)/shard_map/ppermute | solution.py:27
  88.3 0.5 slice.307
  88.8 7.5 %collective-permute-done.6 = f32[520,128]{1,0:T(8,128)S(1)} collective-permute-done((f32[520,128]{1,0:T(8,128)S(1)}, f32[520,128]{1,0:T(8,128)S(1)}, u32[]{:S(2)}, u32[]{:S(2)}) %collective-permute-start.6) | collective-permute-done | bytes 266272 | tf_op jit(solution)/shard_map/ppermute | solution.py:27
  96.3 0.8 multiply_select_fusion.1
  97.1 2.0 %collective-permute-start.7 = (f32[520,128]{1,0:T(8,128)S(1)}, f32[520,128]{1,0:T(8,128)S(1)}, u32[]{:S(2)}, u32[]{:S(2)}) collective-permute-start(f32[520,128]{1,0:T(8,128)S(1)} %multiply_select_fusion.1), channel_id=1, source_target_pairs={{128,0},{144,16},{160,32},{176,48},{192,64},{208,80},{224,96},{240... | collective-permute-start | bytes 798728 | tf_op jit(solution)/shard_map/ppermute | solution.py:27
  99.1 0.5 slice.308
  99.6 14.8 %collective-permute-done.7 = f32[520,128]{1,0:T(8,128)S(1)} collective-permute-done((f32[520,128]{1,0:T(8,128)S(1)}, f32[520,128]{1,0:T(8,128)S(1)}, u32[]{:S(2)}, u32[]{:S(2)}) %collective-permute-start.7) | collective-permute-done | bytes 266272 | tf_op jit(solution)/shard_map/ppermute | solution.py:27
  114.4 0.8 multiply_select_fusion
  115.2 1.3 collective-permute-start.8
  116.5 0.5 slice.309
  117.0 16.7 %collective-permute-done.8 = f32[520,128]{1,0:T(8,128)S(1)} collective-permute-done((f32[520,128]{1,0:T(8,128)S(1)}, f32[520,128]{1,0:T(8,128)S(1)}, u32[]{:S(2)}, u32[]{:S(2)}) %collective-permute-start.8) | collective-permute-done | bytes 266272 | tf_op jit(solution)/shard_map/ppermute | solution.py:27
  133.7 0.8 fusion.34
  134.6 0.4 broadcast_in_dim.43
  135.0 1.1 add_bitcast_fusion
  (30 shorter events, 0.6 us)
Async XLA Ops:
  4.5 14.8 %copy-start.6 = (s32[64]{0:T(128)S(1)}, s32[64]{0:T(128)}, u32[]{:S(2)}) copy-start(s32[64]{0:T(128)} %param.9) | copy-start | bytes 772
  4.5 16.9 %copy-start.1 = (f32[1,16,128,128]{3,2,1,0:T(8,128)S(1)}, f32[1,16,128,128]{3,2,1,0:T(8,128)}, u32[]{:S(2)}) copy-start(f32[1,16,128,128]{3,2,1,0:T(8,128)} %param.7) | copy-start | bytes 3145732
  5.4 31.7 %collective-permute-start.2 = (f32[8,128,128]{2,1,0:T(8,128)}, f32[8,128,128]{2,1,0:T(8,128)}, u32[]{:S(2)}, u32[]{:S(2)}) collective-permute-start(f32[8,128,128]{2,1,0:T(8,128)} %pad_maximum_fusion.1), channel_id=1, source_target_pairs={{0,1},{1,2},{2,3},{3,4},{4,5},{5,6},{6,7},{7,8},{8,9},{9,10},{10,1... | collective-permute-start | bytes 1572872 | tf_op jit(solution)/shard_map/ppermute | solution.py:103
  17.4 32.3 %collective-permute-start.3 = (f32[8,128,128]{2,1,0:T(8,128)}, f32[8,128,128]{2,1,0:T(8,128)}, u32[]{:S(2)}, u32[]{:S(2)}) collective-permute-start(f32[8,128,128]{2,1,0:T(8,128)} %pad_maximum_fusion.2), channel_id=1, source_target_pairs={{1,0},{2,1},{3,2},{4,3},{5,4},{6,5},{7,6},{8,7},{9,8},{10,9},{11,1... | collective-permute-start | bytes 1572872 | tf_op jit(solution)/shard_map/ppermute | solution.py:104
  21.4 12.4 %copy-start = (f32[16,128,128]{2,1,0:T(8,128)S(1)}, f32[16,128,128]{2,1,0:T(8,128)}, u32[]{:S(2)}) copy-start(f32[16,128,128]{2,1,0:T(8,128)} %get-tuple-element.7) | copy-start | bytes 3145732
  23.7 27.1 %collective-permute-start = (f32[4,128,128]{2,1,0:T(8,128)}, f32[4,128,128]{2,1,0:T(8,128)}, u32[]{:S(2)}, u32[]{:S(2)}) collective-permute-start(f32[4,128,128]{2,1,0:T(8,128)} %get-tuple-element.24), channel_id=1, source_target_pairs={{0,1},{1,2},{2,3},{3,4},{4,5},{5,6},{6,7},{7,8},{8,9},{9,10},{10,1... | collective-permute-start | bytes 786440 | tf_op jit(solution)/shard_map/ppermute | solution.py:105
  31.2 23.4 %collective-permute-start.1 = (f32[4,128,128]{2,1,0:T(8,128)}, f32[4,128,128]{2,1,0:T(8,128)}, u32[]{:S(2)}, u32[]{:S(2)}) collective-permute-start(f32[4,128,128]{2,1,0:T(8,128)} %get-tuple-element.25), channel_id=1, source_target_pairs={{1,0},{2,1},{3,2},{4,3},{5,4},{6,5},{7,6},{8,7},{9,8},{10,9},{11,1... | collective-permute-start | bytes 786440 | tf_op jit(solution)/shard_map/ppermute | solution.py:106
  35.7 1.1 copy-start.3
  35.7 1.1 copy-start.4
  35.7 1.1 copy-start.5
  37.1 17.6 %copy-start.2 = (f32[16,128,128]{2,1,0:T(8,128)S(1)}, f32[16,128,128]{2,1,0:T(8,128)}, u32[]{:S(2)}) copy-start(f32[16,128,128]{2,1,0:T(8,128)} %get-tuple-element.8) | copy-start | bytes 3145732
  62.5 7.5 %collective-permute-start.4 = (f32[520,128]{1,0:T(8,128)S(1)}, f32[520,128]{1,0:T(8,128)S(1)}, u32[]{:S(2)}, u32[]{:S(2)}) collective-permute-start(f32[520,128]{1,0:T(8,128)S(1)} %concatenate.26), channel_id=1, source_target_pairs={{16,0},{32,16},{48,32},{64,48},{80,64},{96,80},{112,96},{128,112},... | collective-permute-start | bytes 798728 | tf_op jit(solution)/shard_map/ppermute | solution.py:27
  70.2 15.2 %collective-permute-start.5 = (f32[520,128]{1,0:T(8,128)S(1)}, f32[520,128]{1,0:T(8,128)S(1)}, u32[]{:S(2)}, u32[]{:S(2)}) collective-permute-start(f32[520,128]{1,0:T(8,128)S(1)} %multiply_select_fusion.3), channel_id=1, source_target_pairs={{32,0},{48,16},{64,32},{80,48},{96,64},{112,80},{128,96},{144,112}... | collective-permute-start | bytes 798728 | tf_op jit(solution)/shard_map/ppermute | solution.py:27
  86.2 10.1 %collective-permute-start.6 = (f32[520,128]{1,0:T(8,128)S(1)}, f32[520,128]{1,0:T(8,128)S(1)}, u32[]{:S(2)}, u32[]{:S(2)}) collective-permute-start(f32[520,128]{1,0:T(8,128)S(1)} %multiply_select_fusion.2), channel_id=1, source_target_pairs={{64,0},{80,16},{96,32},{112,48},{128,64},{144,80},{160,96},{176,11... | collective-permute-start | bytes 798728 | tf_op jit(solution)/shard_map/ppermute | solution.py:27
  97.1 17.3 %collective-permute-start.7 = (f32[520,128]{1,0:T(8,128)S(1)}, f32[520,128]{1,0:T(8,128)S(1)}, u32[]{:S(2)}, u32[]{:S(2)}) collective-permute-start(f32[520,128]{1,0:T(8,128)S(1)} %multiply_select_fusion.1), channel_id=1, source_target_pairs={{128,0},{144,16},{160,32},{176,48},{192,64},{208,80},{224,96},{240... | collective-permute-start | bytes 798728 | tf_op jit(solution)/shard_map/ppermute | solution.py:27
  115.2 18.5 %collective-permute-start.8 = (f32[520,128]{1,0:T(8,128)S(1)}, f32[520,128]{1,0:T(8,128)S(1)}, u32[]{:S(2)}, u32[]{:S(2)}) collective-permute-start(f32[520,128]{1,0:T(8,128)S(1)} %get-tuple-element.38), channel_id=1, source_target_pairs={{256,0},{272,16},{288,32},{304,48},{320,64},{336,80},{352,96},{368... | collective-permute-start | bytes 798728 | tf_op jit(solution)/shard_map/ppermute | solution.py:27
